TPU v7x, 128 devices: a whole 4x4x4 slice. The times are simulated.
128 devices in a mesh: dp: 2 (over core), expert: 64 (over z, y, x).
Axes of the slice: x: 4, y: 4, z: 4, core: 2. Of those that a mesh axis runs over, the one named last changes fastest.
Arguments:
- tokens: bfloat16 [32768, 3584], P(('dp', 'expert')), may hold values from -6 to 6
- cotangent: bfloat16 [32768, 3584], P(('dp', 'expert')), may hold values from -6 to 6
- expert_ids: int32 [32768, 1], P(('dp', 'expert')), may hold values from 0 to 63; in each aligned block of 256 rows (0 to 255, 256 to 511, ...) at most 8 rows name the same one
- gate_probs: float32 [32768, 1], P(('dp', 'expert')), may hold values from 0.2 to 1
- w_gate: bfloat16 [64, 3584, 1024], P('expert', None, 'dp'), may hold values from -0.09375 to 0.09375
- w_up: bfloat16 [64, 3584, 1024], P('expert', None, 'dp'), may hold values from -0.09375 to 0.09375
- w_down: bfloat16 [64, 1024, 3584], P('expert', 'dp'), may hold values from -0.1875 to 0.1875
Outputs:
- grad_tokens: bfloat16 [32768, 3584], P(('dp', 'expert'))
- grad_gate: bfloat16 [64, 3584, 1024], P('expert', None, 'dp')
- grad_up: bfloat16 [64, 3584, 1024], P('expert', None, 'dp')
- grad_down: bfloat16 [64, 1024, 3584], P('expert', 'dp')
Inputs may be any that keep to these rules, and one draw needn't show every extreme that they name: `expert_ids`: within the entries of one device's 256 tokens, no expert is named more than 8 times, and in some device one expert is named exactly 8 times. Each row names exactly one expert.
All inputs are finite; a program needn't handle non-finite values.
Results may differ from a plain program's by a relative error of at most 0.0065.
Values may be sent and summed in bfloat16 or wider, within the bound.
No kernel may reach another device: no remote copies, remote signals or barrier semaphores. Data moves between devices by JAX's collectives and lax.ppermute only.
A program may use at most 192 MiB of HBM per device.

v0:
```python
import jax
import jax.numpy as jnp
from jax import lax
from jax.sharding import PartitionSpec as P


def front_rows(rows_x, rows_cot, gate_w, up_w, down_w):
    gate_pre = jnp.dot(rows_x, gate_w, preferred_element_type=jnp.float32)
    up_pre = jnp.dot(rows_x, up_w, preferred_element_type=jnp.float32)
    sigmoid_gate = jax.nn.sigmoid(gate_pre)
    swish_gate = gate_pre * sigmoid_gate
    hidden = (swish_gate * up_pre).astype(jnp.bfloat16)
    d_hidden = lax.dot_general(
        rows_cot, down_w, (((1,), (1,)), ((), ())), preferred_element_type=jnp.float32
    )
    d_gate = (d_hidden * up_pre * sigmoid_gate * (1.0 + gate_pre * (1.0 - sigmoid_gate))).astype(
        jnp.bfloat16
    )
    d_up = (d_hidden * swish_gate).astype(jnp.bfloat16)
    dx_part = lax.dot_general(
        d_gate, gate_w, (((1,), (1,)), ((), ())), preferred_element_type=jnp.float32
    )
    dx_part = dx_part + lax.dot_general(
        d_up, up_w, (((1,), (1,)), ((), ())), preferred_element_type=jnp.float32
    )
    return (hidden, d_gate, d_up, dx_part.astype(jnp.bfloat16))


def weight_sums(rows_x, rows_cot, hidden, d_gate, d_up):
    grad_gate = lax.dot_general(
        rows_x, d_gate, (((0,), (0,)), ((), ())), preferred_element_type=jnp.float32
    )
    grad_up = lax.dot_general(
        rows_x, d_up, (((0,), (0,)), ((), ())), preferred_element_type=jnp.float32
    )
    grad_down = lax.dot_general(
        hidden, rows_cot, (((0,), (0,)), ((), ())), preferred_element_type=jnp.float32
    )
    return (grad_gate, grad_up, grad_down)


def live_of(counts_three, capacity):
    return (jnp.arange(capacity, dtype=jnp.int32) < counts_three).reshape(-1)


def tile_flags(counts_three, capacity):
    live_rows = live_of(counts_three, capacity).astype(jnp.int32)
    return jnp.max(live_rows.reshape(-1, 128), axis=1) > 0


def run_front(rows_four, cots_four, counts_three, weights, capacity):
    model_width = rows_four.shape[-1]
    rows_flat = rows_four.reshape(-1, model_width)
    cots_flat = cots_four.reshape(-1, model_width)
    slot_count = rows_flat.shape[0]
    hidden_width = weights[0].shape[1]
    spare_rows = -slot_count % 128
    tiles_all = (slot_count + spare_rows) // 128
    flags = tile_flags(counts_three, capacity)

    def empty_tile():
        return (
            jnp.zeros((128, hidden_width), jnp.bfloat16),
            jnp.zeros((128, hidden_width), jnp.bfloat16),
            jnp.zeros((128, hidden_width), jnp.bfloat16),
            jnp.zeros((128, model_width), jnp.bfloat16),
        )

    def add_tile(index_tile, outputs):
        start = index_tile * 128
        tile_x = lax.dynamic_slice_in_dim(rows_flat, start, 128)
        tile_cot = lax.dynamic_slice_in_dim(cots_flat, start, 128)
        tile_out = lax.cond(
            flags[index_tile],
            lambda: front_rows(tile_x, tile_cot, weights[0], weights[1], weights[2]),
            empty_tile,
        )
        return tuple(
            (
                lax.dynamic_update_slice_in_dim(whole, piece, start, 0)
                for whole, piece in zip(outputs, tile_out)
            )
        )

    total_rows = slot_count + spare_rows
    initial = (
        jnp.zeros((total_rows, hidden_width), jnp.bfloat16),
        jnp.zeros((total_rows, hidden_width), jnp.bfloat16),
        jnp.zeros((total_rows, hidden_width), jnp.bfloat16),
        jnp.zeros((total_rows, model_width), jnp.bfloat16),
    )
    outputs = lax.fori_loop(0, tiles_all, add_tile, initial)
    results = tuple((whole for whole in outputs))
    return results


def run_sums(rows_x, rows_cot, hidden, d_gate, d_up, counts_three, capacity):
    slot_count = rows_x.shape[0]
    model_width = rows_x.shape[1]
    hidden_width = hidden.shape[1]
    spare_rows = -slot_count % 128
    tiles_all = (slot_count + spare_rows) // 128
    sources = [source for source in (rows_x, rows_cot, hidden, d_gate, d_up)]
    flags = tile_flags(counts_three, capacity)

    def add_tile(index_tile, totals):
        start = index_tile * 128
        operands = [lax.dynamic_slice_in_dim(source, start, 128) for source in sources]

        def with_tile():
            added = weight_sums(operands[0], operands[1], operands[2], operands[3], operands[4])
            return tuple((running + extra for running, extra in zip(totals, added)))

        return lax.cond(flags[index_tile], with_tile, lambda: totals)

    initial = (
        jnp.zeros((model_width, hidden_width), jnp.float32),
        jnp.zeros((model_width, hidden_width), jnp.float32),
        jnp.zeros((hidden_width, model_width), jnp.float32),
    )
    sums = lax.fori_loop(0, tiles_all, add_tile, initial)
    return sums


def local(tokens, cotangent, expert_ids, gate_probs, w_gate, w_up, w_down):
    owners = lax.axis_size("expert")
    groups = lax.axis_size("dp")
    tok_rows = tokens.shape[0]
    model_width = tokens.shape[1]
    fanout = expert_ids.shape[1]
    capacity = max(2, 2 * tok_rows * fanout // owners)
    copies = tok_rows * fanout
    flat_ids = expert_ids.reshape(copies)
    onehot = (flat_ids[:, None] == jnp.arange(owners, dtype=jnp.int32)[None, :]).astype(jnp.int32)
    before = jnp.cumsum(onehot, axis=0) - onehot
    slot_rank = jnp.sum(before * onehot, axis=1)
    counts = jnp.sum(onehot, axis=0).reshape(owners, 1)
    position = flat_ids * capacity + slot_rank
    copy_rows = tokens[:, None, :].reshape(copies, model_width)
    copy_tok_cot = cotangent[:, None, :].reshape(copies, model_width)
    copy_cots = (gate_probs * copy_tok_cot.astype(jnp.float32)).astype(jnp.bfloat16)
    placing = (jnp.arange(owners * capacity, dtype=jnp.int32)[:, None] == position[None, :]).astype(
        jnp.bfloat16
    )
    sent_rows = (
        jnp.dot(placing, copy_rows, preferred_element_type=jnp.float32)
        .astype(jnp.bfloat16)
        .reshape(owners, capacity, model_width)
    )
    sent_cots = (
        jnp.dot(placing, copy_cots, preferred_element_type=jnp.float32)
        .astype(jnp.bfloat16)
        .reshape(owners, capacity, model_width)
    )
    came_rows, came_cots, came_counts = (
        lax.all_to_all(sent_rows, "expert", split_axis=0, concat_axis=0, tiled=True),
        lax.all_to_all(sent_cots, "expert", split_axis=0, concat_axis=0, tiled=True),
        lax.all_to_all(counts, "expert", split_axis=0, concat_axis=0, tiled=True),
    )
    got_rows, got_cots, got_counts = (
        lax.all_gather(came_rows, "dp", axis=0, tiled=True),
        lax.all_gather(came_cots, "dp", axis=0, tiled=True),
        lax.all_gather(came_counts, "dp", axis=0, tiled=True),
    )
    got_rows = got_rows.reshape(groups, owners, capacity, model_width)
    got_cots = got_cots.reshape(groups, owners, capacity, model_width)
    got_counts = got_counts.reshape(groups, owners, 1)
    slots_all = owners * groups * capacity
    weights_own = (w_gate[0], w_up[0], w_down[0])
    hidden, d_gate, d_up, dx_part = run_front(got_rows, got_cots, got_counts, weights_own, capacity)
    rows_x = got_rows.reshape(slots_all, model_width)
    rows_cot = got_cots.reshape(slots_all, model_width)
    grad_gate, grad_up, grad_down = run_sums(
        rows_x, rows_cot, hidden, d_gate, d_up, got_counts, capacity
    )
    dx_float = dx_part.astype(jnp.float32)
    summed = lax.psum_scatter(
        dx_float.reshape(groups * owners, capacity, model_width).astype(jnp.bfloat16),
        "dp",
        scatter_dimension=0,
        tiled=True,
    )
    returned = lax.all_to_all(summed, "expert", split_axis=0, concat_axis=0, tiled=True)
    copy_grad = lax.dot_general(
        placing,
        returned.reshape(owners * capacity, model_width),
        (((0,), (0,)), ((), ())),
        preferred_element_type=jnp.float32,
    )
    grad_tokens = jnp.sum(copy_grad.reshape(tok_rows, fanout, model_width), axis=1).astype(
        jnp.bfloat16
    )
    return (
        grad_tokens,
        grad_gate.astype(jnp.bfloat16)[None],
        grad_up.astype(jnp.bfloat16)[None],
        grad_down.astype(jnp.bfloat16)[None],
    )


def solution(mesh):
    return jax.shard_map(
        local,
        mesh=mesh,
        in_specs=(
            P(("dp", "expert"), None),
            P(("dp", "expert"), None),
            P(("dp", "expert"), None),
            P(("dp", "expert"), None),
            P("expert", None, "dp"),
            P("expert", None, "dp"),
            P("expert", "dp", None),
        ),
        out_specs=(
            P(("dp", "expert"), None),
            P("expert", None, "dp"),
            P("expert", None, "dp"),
            P("expert", "dp", None),
        ),
        check_vma=False,
    )
```

profile of v0, /device:TPU:1, one launch (start us, length us, event | category | flops | bytes accessed | tf_op | source)
XLA Modules:
  0.0 535.9 jit_solution(294715349386406284)
XLA Ops:
  13.2 57.5 %all_to_all.27 = bf16[64,8,3584]{2,1,0:T(8,128)(2,1)} all-to-all(bf16[64,8,3584]{2,1,0:T(8,128)(2,1)S(1)} %fusion.21), channel_id=1, replica_groups=mesh['dp'=2,'expert'=64] {'expert'}, dimensions={0} | all-to-all | bytes 7340032 | tf_op jit(solution)/shard_map/all_to_all | solution.py:157
  71.9 52.2 %all_to_all.28 = bf16[64,8,3584]{2,1,0:T(8,128)(2,1)} all-to-all(bf16[64,8,3584]{2,1,0:T(8,128)(2,1)S(1)} %fusion.20), channel_id=1, replica_groups=mesh['dp'=2,'expert'=64] {'expert'}, dimensions={0} | all-to-all | bytes 7340032 | tf_op jit(solution)/shard_map/all_to_all | solution.py:156
  124.8 6.6 %all-to-all-start = ((s32[64,1,1]{2,1,0:T(1,128)}), s32[64,1,1]{2,1,0:T(1,128)S(1)}, u32[]{:S(2)}, u32[]{:S(2)}) async-start(s32[64,1,1]{2,1,0:T(1,128)} %copy.17), calls=%async_computation | async-start | bytes 65536 | tf_op jit(solution)/shard_map/all_to_all | solution.py:158
  132.7 7.0 %all-to-all-done = s32[64,1,1]{2,1,0:T(1,128)S(1)} async-done(((s32[64,1,1]{2,1,0:T(1,128)}), s32[64,1,1]{2,1,0:T(1,128)S(1)}, u32[]{:S(2)}, u32[]{:S(2)}) %all-to-all-start) | async-done | bytes 288 | tf_op jit(solution)/shard_map/all_to_all | solution.py:158
  141.2 3.6 all-reduce
  148.2 3.4 broadcast_in_dim.20
  151.6 142.5 %while.36 = (s32[]{:T(128)}, bf16[1024,512]{1,0:T(8,128)(2,1)}, bf16[1024,512]{1,0:T(8,128)(2,1)}, bf16[1024,512]{1,0:T(8,128)(2,1)}, bf16[1024,3584]{1,0:T(8,12...) while((s32[]{:T(128)}, bf16[1024,512]{1,0:T(8,128)(2,1)}, ...), condition=%wide.region_9.10_spmd, body=%wide.region_6.9_spmd.sunk | while | flops 2350710784 | bytes 74059120 | solution.py:92
  152.9 13.2 %conditional.4 = (bf16[128,512]{1,0:T(8,128)(2,1)S(1)}, bf16[128,512]{1,0:T(8,128)(2,1)}, bf16[128,512]{1,0:T(8,128)(2,1)}, bf16[128,3584]{1,0:T(8,128)(2,1)S(1)}) conditional(s32[]{:T(128)} %bitcast.47, () %tuple.97, (bf16[1024,3584]{1,0:T(8,128)(2,1)}, s32[]{:T(128)}, bf16[3584,512]{1,0:T(8,128)(2,1)}, bf16[3584,512]{1,0:T(8,128)(2,1)}, ...), branch_computations={%region_7.7_spmd, %region_8.8_spmd} | conditional | flops 2350710784 | bytes 71435888 | solution.py:73
  152.9 3.1 fusion.3
  158.3 3.2 multiply_convert_fusion
  170.7 13.2 %conditional.4 = (bf16[128,512]{1,0:T(8,128)(2,1)S(1)}, bf16[128,512]{1,0:T(8,128)(2,1)}, bf16[128,512]{1,0:T(8,128)(2,1)}, bf16[128,3584]{1,0:T(8,128)(2,1)S(1)}) conditional(s32[]{:T(128)} %bitcast.47, () %tuple.97, (bf16[1024,3584]{1,0:T(8,128)(2,1)}, s32[]{:T(128)}, bf16[3584,512]{1,0:T(8,128)(2,1)}, bf16[3584,512]{1,0:T(8,128)(2,1)}, ...), branch_computations={%region_7.7_spmd, %region_8.8_spmd} | conditional | flops 2350710784 | bytes 71435888 | solution.py:73
  170.7 3.1 fusion.3
  176.1 3.2 multiply_convert_fusion
  188.5 13.2 %conditional.4 = (bf16[128,512]{1,0:T(8,128)(2,1)S(1)}, bf16[128,512]{1,0:T(8,128)(2,1)}, bf16[128,512]{1,0:T(8,128)(2,1)}, bf16[128,3584]{1,0:T(8,128)(2,1)S(1)}) conditional(s32[]{:T(128)} %bitcast.47, () %tuple.97, (bf16[1024,3584]{1,0:T(8,128)(2,1)}, s32[]{:T(128)}, bf16[3584,512]{1,0:T(8,128)(2,1)}, bf16[3584,512]{1,0:T(8,128)(2,1)}, ...), branch_computations={%region_7.7_spmd, %region_8.8_spmd} | conditional | flops 2350710784 | bytes 71435888 | solution.py:73
  188.6 3.1 fusion.3
  193.9 3.2 multiply_convert_fusion
  206.4 13.2 %conditional.4 = (bf16[128,512]{1,0:T(8,128)(2,1)S(1)}, bf16[128,512]{1,0:T(8,128)(2,1)}, bf16[128,512]{1,0:T(8,128)(2,1)}, bf16[128,3584]{1,0:T(8,128)(2,1)S(1)}) conditional(s32[]{:T(128)} %bitcast.47, () %tuple.97, (bf16[1024,3584]{1,0:T(8,128)(2,1)}, s32[]{:T(128)}, bf16[3584,512]{1,0:T(8,128)(2,1)}, bf16[3584,512]{1,0:T(8,128)(2,1)}, ...), branch_computations={%region_7.7_spmd, %region_8.8_spmd} | conditional | flops 2350710784 | bytes 71435888 | solution.py:73
  206.4 3.1 fusion.3
  211.7 3.2 multiply_convert_fusion
  224.2 13.2 %conditional.4 = (bf16[128,512]{1,0:T(8,128)(2,1)S(1)}, bf16[128,512]{1,0:T(8,128)(2,1)}, bf16[128,512]{1,0:T(8,128)(2,1)}, bf16[128,3584]{1,0:T(8,128)(2,1)S(1)}) conditional(s32[]{:T(128)} %bitcast.47, () %tuple.97, (bf16[1024,3584]{1,0:T(8,128)(2,1)}, s32[]{:T(128)}, bf16[3584,512]{1,0:T(8,128)(2,1)}, bf16[3584,512]{1,0:T(8,128)(2,1)}, ...), branch_computations={%region_7.7_spmd, %region_8.8_spmd} | conditional | flops 2350710784 | bytes 71435888 | solution.py:73
  224.2 3.1 fusion.3
  229.6 3.2 multiply_convert_fusion
  242.0 13.2 %conditional.4 = (bf16[128,512]{1,0:T(8,128)(2,1)S(1)}, bf16[128,512]{1,0:T(8,128)(2,1)}, bf16[128,512]{1,0:T(8,128)(2,1)}, bf16[128,3584]{1,0:T(8,128)(2,1)S(1)}) conditional(s32[]{:T(128)} %bitcast.47, () %tuple.97, (bf16[1024,3584]{1,0:T(8,128)(2,1)}, s32[]{:T(128)}, bf16[3584,512]{1,0:T(8,128)(2,1)}, bf16[3584,512]{1,0:T(8,128)(2,1)}, ...), branch_computations={%region_7.7_spmd, %region_8.8_spmd} | conditional | flops 2350710784 | bytes 71435888 | solution.py:73
  242.0 3.1 fusion.3
  247.4 3.2 multiply_convert_fusion
  259.8 13.2 %conditional.4 = (bf16[128,512]{1,0:T(8,128)(2,1)S(1)}, bf16[128,512]{1,0:T(8,128)(2,1)}, bf16[128,512]{1,0:T(8,128)(2,1)}, bf16[128,3584]{1,0:T(8,128)(2,1)S(1)}) conditional(s32[]{:T(128)} %bitcast.47, () %tuple.97, (bf16[1024,3584]{1,0:T(8,128)(2,1)}, s32[]{:T(128)}, bf16[3584,512]{1,0:T(8,128)(2,1)}, bf16[3584,512]{1,0:T(8,128)(2,1)}, ...), branch_computations={%region_7.7_spmd, %region_8.8_spmd} | conditional | flops 2350710784 | bytes 71435888 | solution.py:73
  259.8 3.1 fusion.3
  265.2 3.2 multiply_convert_fusion
  277.6 13.2 %conditional.4 = (bf16[128,512]{1,0:T(8,128)(2,1)S(1)}, bf16[128,512]{1,0:T(8,128)(2,1)}, bf16[128,512]{1,0:T(8,128)(2,1)}, bf16[128,3584]{1,0:T(8,128)(2,1)S(1)}) conditional(s32[]{:T(128)} %bitcast.47, () %tuple.97, (bf16[1024,3584]{1,0:T(8,128)(2,1)}, s32[]{:T(128)}, bf16[3584,512]{1,0:T(8,128)(2,1)}, bf16[3584,512]{1,0:T(8,128)(2,1)}, ...), branch_computations={%region_7.7_spmd, %region_8.8_spmd} | conditional | flops 2350710784 | bytes 71435888 | solution.py:73
  277.7 3.1 fusion.3
  283.0 3.2 multiply_convert_fusion
  294.2 18.6 %reduce-scatter.2.cloned.1.call-done = bf16[64,8,3584]{2,1,0:T(8,128)(2,1)} async-done(((bf16[128,8,3584]{2,1,0:T(8,128)(2,1)}), bf16[64,8,3584]{2,1,0:T(8,128)(2,1)}) %reduce-scatter.2.cloned.1.call-update) | async-done | bytes 3670032 | tf_op jit(solution)/shard_map/reduce_scatter | solution.py:177
  312.8 10.4 %all-to-all-start.3 = ((bf16[64,8,3584]{2,1,0:T(8,128)(2,1)}), bf16[64,8,3584]{2,1,0:T(8,128)(2,1)}, u32[]{:S(2)}, u32[]{:S(2)}) async-start(bf16[64,8,3584]{2,1,0:T(8,128)(2,1)} %reduce-scatter.2.cloned.1.call-done), calls=%async_computation.4 | async-start | bytes 7340032 | tf_op jit(solution)/shard_map/all_to_all | solution.py:183
  323.2 3.9 broadcast.44.clone
  327.1 3.9 broadcast_in_dim.21
  331.0 3.9 broadcast.44
  334.9 175.4 %while.37 = (s32[]{:T(128)}, f32[3584,512]{1,0:T(8,128)}, f32[3584,512]{1,0:T(8,128)}, f32[512,3584]{1,0:T(8,128)}, pred[8]{0:T(512)(128)(4,1)S(1)}, /*index=5*/...) while((s32[]{:T(128)}, f32[3584,512]{1,0:T(8,128)}, ...), condition=%wide.region_14.15_spmd, body=%wide.region_11.14_spmd.sunk | while | flops 1414791168 | bytes 105909608 | solution.py:121
  336.1 20.7 %conditional.5 = ((f32[3584,512]{1,0:T(8,128)}, f32[3584,512]{1,0:T(8,128)}, f32[512,3584]{1,0:T(8,128)})) conditional(s32[]{:T(128)} %bitcast.48, (f32[3584,512]{1,0:T(8,128)}, f32[3584,512]{1,0:T(8,128)}, f32[512,3584]{1,0:T(8,128)}) %tuple.100, (s32[]{:T(128)}, bf16[1024,3584]{1,0:T(8,128)(2,1)}, bf16[1024,512]{1,0:T(8,128)(2,1)}, ...), branch_computations={%region_12.12_spmd, %region_13.13_spmd} | conditional | flops 1414791168 | bytes 105909384 | solution.py:114
  336.2 7.6 %convolution_add_fusion.3 = f32[3584,512]{1,0:T(8,128)} fusion(f32[3584,512]{1,0:T(8,128)} %get-tuple-element.534, bf16[1024,3584]{1,0:T(8,128)(2,1)} %get-tuple-element.535, s32[]{:T(128)S(6)} %select_n.35, bf16[1024,512]{1,0:T(8,128)(2,1)} %get-tuple-element.537), kind=kOutput, calls=%fused_computation.22 | convolution fusion | flops 471597056 | bytes 15729664 | tf_op jit(solution)/shard_map/while/body/eval_jaxpr/cond/branch_1_fun/dot_general | solution.py:30
  346.6 10.2 %convolution_add_fusion.2 = f32[3584,512]{1,0:T(8,128)} fusion(f32[3584,512]{1,0:T(8,128)} %get-tuple-element.538, bf16[1024,3584]{1,0:T(8,128)(2,1)} %get-tuple-element.535, s32[]{:T(128)S(6)} %select_n.35, bf16[1024,512]{1,0:T(8,128)(2,1)} %get-tuple-element.539), kind=kOutput, calls=%fused_computation.21 | convolution fusion | flops 471597056 | bytes 15729664 | tf_op jit(solution)/shard_map/while/body/eval_jaxpr/cond/branch_1_fun/dot_general | solution.py:33
  358.1 20.7 %conditional.5 = ((f32[3584,512]{1,0:T(8,128)}, f32[3584,512]{1,0:T(8,128)}, f32[512,3584]{1,0:T(8,128)})) conditional(s32[]{:T(128)} %bitcast.48, (f32[3584,512]{1,0:T(8,128)}, f32[3584,512]{1,0:T(8,128)}, f32[512,3584]{1,0:T(8,128)}) %tuple.100, (s32[]{:T(128)}, bf16[1024,3584]{1,0:T(8,128)(2,1)}, bf16[1024,512]{1,0:T(8,128)(2,1)}, ...), branch_computations={%region_12.12_spmd, %region_13.13_spmd} | conditional | flops 1414791168 | bytes 105909384 | solution.py:114
  358.1 7.6 %convolution_add_fusion.3 = f32[3584,512]{1,0:T(8,128)} fusion(f32[3584,512]{1,0:T(8,128)} %get-tuple-element.534, bf16[1024,3584]{1,0:T(8,128)(2,1)} %get-tuple-element.535, s32[]{:T(128)S(6)} %select_n.35, bf16[1024,512]{1,0:T(8,128)(2,1)} %get-tuple-element.537), kind=kOutput, calls=%fused_computation.22 | convolution fusion | flops 471597056 | bytes 15729664 | tf_op jit(solution)/shard_map/while/body/eval_jaxpr/cond/branch_1_fun/dot_general | solution.py:30
  368.6 10.2 %convolution_add_fusion.2 = f32[3584,512]{1,0:T(8,128)} fusion(f32[3584,512]{1,0:T(8,128)} %get-tuple-element.538, bf16[1024,3584]{1,0:T(8,128)(2,1)} %get-tuple-element.535, s32[]{:T(128)S(6)} %select_n.35, bf16[1024,512]{1,0:T(8,128)(2,1)} %get-tuple-element.539), kind=kOutput, calls=%fused_computation.21 | convolution fusion | flops 471597056 | bytes 15729664 | tf_op jit(solution)/shard_map/while/body/eval_jaxpr/cond/branch_1_fun/dot_general | solution.py:33
  380.0 20.7 %conditional.5 = ((f32[3584,512]{1,0:T(8,128)}, f32[3584,512]{1,0:T(8,128)}, f32[512,3584]{1,0:T(8,128)})) conditional(s32[]{:T(128)} %bitcast.48, (f32[3584,512]{1,0:T(8,128)}, f32[3584,512]{1,0:T(8,128)}, f32[512,3584]{1,0:T(8,128)}) %tuple.100, (s32[]{:T(128)}, bf16[1024,3584]{1,0:T(8,128)(2,1)}, bf16[1024,512]{1,0:T(8,128)(2,1)}, ...), branch_computations={%region_12.12_spmd, %region_13.13_spmd} | conditional | flops 1414791168 | bytes 105909384 | solution.py:114
  380.0 7.6 %convolution_add_fusion.3 = f32[3584,512]{1,0:T(8,128)} fusion(f32[3584,512]{1,0:T(8,128)} %get-tuple-element.534, bf16[1024,3584]{1,0:T(8,128)(2,1)} %get-tuple-element.535, s32[]{:T(128)S(6)} %select_n.35, bf16[1024,512]{1,0:T(8,128)(2,1)} %get-tuple-element.537), kind=kOutput, calls=%fused_computation.22 | convolution fusion | flops 471597056 | bytes 15729664 | tf_op jit(solution)/shard_map/while/body/eval_jaxpr/cond/branch_1_fun/dot_general | solution.py:30
  390.5 10.2 %convolution_add_fusion.2 = f32[3584,512]{1,0:T(8,128)} fusion(f32[3584,512]{1,0:T(8,128)} %get-tuple-element.538, bf16[1024,3584]{1,0:T(8,128)(2,1)} %get-tuple-element.535, s32[]{:T(128)S(6)} %select_n.35, bf16[1024,512]{1,0:T(8,128)(2,1)} %get-tuple-element.539), kind=kOutput, calls=%fused_computation.21 | convolution fusion | flops 471597056 | bytes 15729664 | tf_op jit(solution)/shard_map/while/body/eval_jaxpr/cond/branch_1_fun/dot_general | solution.py:33
  401.9 20.7 %conditional.5 = ((f32[3584,512]{1,0:T(8,128)}, f32[3584,512]{1,0:T(8,128)}, f32[512,3584]{1,0:T(8,128)})) conditional(s32[]{:T(128)} %bitcast.48, (f32[3584,512]{1,0:T(8,128)}, f32[3584,512]{1,0:T(8,128)}, f32[512,3584]{1,0:T(8,128)}) %tuple.100, (s32[]{:T(128)}, bf16[1024,3584]{1,0:T(8,128)(2,1)}, bf16[1024,512]{1,0:T(8,128)(2,1)}, ...), branch_computations={%region_12.12_spmd, %region_13.13_spmd} | conditional | flops 1414791168 | bytes 105909384 | solution.py:114
  402.0 7.6 %convolution_add_fusion.3 = f32[3584,512]{1,0:T(8,128)} fusion(f32[3584,512]{1,0:T(8,128)} %get-tuple-element.534, bf16[1024,3584]{1,0:T(8,128)(2,1)} %get-tuple-element.535, s32[]{:T(128)S(6)} %select_n.35, bf16[1024,512]{1,0:T(8,128)(2,1)} %get-tuple-element.537), kind=kOutput, calls=%fused_computation.22 | convolution fusion | flops 471597056 | bytes 15729664 | tf_op jit(solution)/shard_map/while/body/eval_jaxpr/cond/branch_1_fun/dot_general | solution.py:30
  412.4 10.2 %convolution_add_fusion.2 = f32[3584,512]{1,0:T(8,128)} fusion(f32[3584,512]{1,0:T(8,128)} %get-tuple-element.538, bf16[1024,3584]{1,0:T(8,128)(2,1)} %get-tuple-element.535, s32[]{:T(128)S(6)} %select_n.35, bf16[1024,512]{1,0:T(8,128)(2,1)} %get-tuple-element.539), kind=kOutput, calls=%fused_computation.21 | convolution fusion | flops 471597056 | bytes 15729664 | tf_op jit(solution)/shard_map/while/body/eval_jaxpr/cond/branch_1_fun/dot_general | solution.py:33
  423.9 20.7 %conditional.5 = ((f32[3584,512]{1,0:T(8,128)}, f32[3584,512]{1,0:T(8,128)}, f32[512,3584]{1,0:T(8,128)})) conditional(s32[]{:T(128)} %bitcast.48, (f32[3584,512]{1,0:T(8,128)}, f32[3584,512]{1,0:T(8,128)}, f32[512,3584]{1,0:T(8,128)}) %tuple.100, (s32[]{:T(128)}, bf16[1024,3584]{1,0:T(8,128)(2,1)}, bf16[1024,512]{1,0:T(8,128)(2,1)}, ...), branch_computations={%region_12.12_spmd, %region_13.13_spmd} | conditional | flops 1414791168 | bytes 105909384 | solution.py:114
  423.9 7.6 %convolution_add_fusion.3 = f32[3584,512]{1,0:T(8,128)} fusion(f32[3584,512]{1,0:T(8,128)} %get-tuple-element.534, bf16[1024,3584]{1,0:T(8,128)(2,1)} %get-tuple-element.535, s32[]{:T(128)S(6)} %select_n.35, bf16[1024,512]{1,0:T(8,128)(2,1)} %get-tuple-element.537), kind=kOutput, calls=%fused_computation.22 | convolution fusion | flops 471597056 | bytes 15729664 | tf_op jit(solution)/shard_map/while/body/eval_jaxpr/cond/branch_1_fun/dot_general | solution.py:30
  434.3 10.2 %convolution_add_fusion.2 = f32[3584,512]{1,0:T(8,128)} fusion(f32[3584,512]{1,0:T(8,128)} %get-tuple-element.538, bf16[1024,3584]{1,0:T(8,128)(2,1)} %get-tuple-element.535, s32[]{:T(128)S(6)} %select_n.35, bf16[1024,512]{1,0:T(8,128)(2,1)} %get-tuple-element.539), kind=kOutput, calls=%fused_computation.21 | convolution fusion | flops 471597056 | bytes 15729664 | tf_op jit(solution)/shard_map/while/body/eval_jaxpr/cond/branch_1_fun/dot_general | solution.py:33
  445.8 20.7 %conditional.5 = ((f32[3584,512]{1,0:T(8,128)}, f32[3584,512]{1,0:T(8,128)}, f32[512,3584]{1,0:T(8,128)})) conditional(s32[]{:T(128)} %bitcast.48, (f32[3584,512]{1,0:T(8,128)}, f32[3584,512]{1,0:T(8,128)}, f32[512,3584]{1,0:T(8,128)}) %tuple.100, (s32[]{:T(128)}, bf16[1024,3584]{1,0:T(8,128)(2,1)}, bf16[1024,512]{1,0:T(8,128)(2,1)}, ...), branch_computations={%region_12.12_spmd, %region_13.13_spmd} | conditional | flops 1414791168 | bytes 105909384 | solution.py:114
  445.8 7.6 %convolution_add_fusion.3 = f32[3584,512]{1,0:T(8,128)} fusion(f32[3584,512]{1,0:T(8,128)} %get-tuple-element.534, bf16[1024,3584]{1,0:T(8,128)(2,1)} %get-tuple-element.535, s32[]{:T(128)S(6)} %select_n.35, bf16[1024,512]{1,0:T(8,128)(2,1)} %get-tuple-element.537), kind=kOutput, calls=%fused_computation.22 | convolution fusion | flops 471597056 | bytes 15729664 | tf_op jit(solution)/shard_map/while/body/eval_jaxpr/cond/branch_1_fun/dot_general | solution.py:30
  456.3 10.2 %convolution_add_fusion.2 = f32[3584,512]{1,0:T(8,128)} fusion(f32[3584,512]{1,0:T(8,128)} %get-tuple-element.538, bf16[1024,3584]{1,0:T(8,128)(2,1)} %get-tuple-element.535, s32[]{:T(128)S(6)} %select_n.35, bf16[1024,512]{1,0:T(8,128)(2,1)} %get-tuple-element.539), kind=kOutput, calls=%fused_computation.21 | convolution fusion | flops 471597056 | bytes 15729664 | tf_op jit(solution)/shard_map/while/body/eval_jaxpr/cond/branch_1_fun/dot_general | solution.py:33
  467.7 20.7 %conditional.5 = ((f32[3584,512]{1,0:T(8,128)}, f32[3584,512]{1,0:T(8,128)}, f32[512,3584]{1,0:T(8,128)})) conditional(s32[]{:T(128)} %bitcast.48, (f32[3584,512]{1,0:T(8,128)}, f32[3584,512]{1,0:T(8,128)}, f32[512,3584]{1,0:T(8,128)}) %tuple.100, (s32[]{:T(128)}, bf16[1024,3584]{1,0:T(8,128)(2,1)}, bf16[1024,512]{1,0:T(8,128)(2,1)}, ...), branch_computations={%region_12.12_spmd, %region_13.13_spmd} | conditional | flops 1414791168 | bytes 105909384 | solution.py:114
  467.8 7.6 %convolution_add_fusion.3 = f32[3584,512]{1,0:T(8,128)} fusion(f32[3584,512]{1,0:T(8,128)} %get-tuple-element.534, bf16[1024,3584]{1,0:T(8,128)(2,1)} %get-tuple-element.535, s32[]{:T(128)S(6)} %select_n.35, bf16[1024,512]{1,0:T(8,128)(2,1)} %get-tuple-element.537), kind=kOutput, calls=%fused_computation.22 | convolution fusion | flops 471597056 | bytes 15729664 | tf_op jit(solution)/shard_map/while/body/eval_jaxpr/cond/branch_1_fun/dot_general | solution.py:30
  478.2 10.2 %convolution_add_fusion.2 = f32[3584,512]{1,0:T(8,128)} fusion(f32[3584,512]{1,0:T(8,128)} %get-tuple-element.538, bf16[1024,3584]{1,0:T(8,128)(2,1)} %get-tuple-element.535, s32[]{:T(128)S(6)} %select_n.35, bf16[1024,512]{1,0:T(8,128)(2,1)} %get-tuple-element.539), kind=kOutput, calls=%fused_computation.21 | convolution fusion | flops 471597056 | bytes 15729664 | tf_op jit(solution)/shard_map/while/body/eval_jaxpr/cond/branch_1_fun/dot_general | solution.py:33
  489.7 20.7 %conditional.5 = ((f32[3584,512]{1,0:T(8,128)}, f32[3584,512]{1,0:T(8,128)}, f32[512,3584]{1,0:T(8,128)})) conditional(s32[]{:T(128)} %bitcast.48, (f32[3584,512]{1,0:T(8,128)}, f32[3584,512]{1,0:T(8,128)}, f32[512,3584]{1,0:T(8,128)}) %tuple.100, (s32[]{:T(128)}, bf16[1024,3584]{1,0:T(8,128)(2,1)}, bf16[1024,512]{1,0:T(8,128)(2,1)}, ...), branch_computations={%region_12.12_spmd, %region_13.13_spmd} | conditional | flops 1414791168 | bytes 105909384 | solution.py:114
  489.7 7.6 %convolution_add_fusion.3 = f32[3584,512]{1,0:T(8,128)} fusion(f32[3584,512]{1,0:T(8,128)} %get-tuple-element.534, bf16[1024,3584]{1,0:T(8,128)(2,1)} %get-tuple-element.535, s32[]{:T(128)S(6)} %select_n.35, bf16[1024,512]{1,0:T(8,128)(2,1)} %get-tuple-element.537), kind=kOutput, calls=%fused_computation.22 | convolution fusion | flops 471597056 | bytes 15729664 | tf_op jit(solution)/shard_map/while/body/eval_jaxpr/cond/branch_1_fun/dot_general | solution.py:30
  500.1 10.2 %convolution_add_fusion.2 = f32[3584,512]{1,0:T(8,128)} fusion(f32[3584,512]{1,0:T(8,128)} %get-tuple-element.538, bf16[1024,3584]{1,0:T(8,128)(2,1)} %get-tuple-element.535, s32[]{:T(128)S(6)} %select_n.35, bf16[1024,512]{1,0:T(8,128)(2,1)} %get-tuple-element.539), kind=kOutput, calls=%fused_computation.21 | convolution fusion | flops 471597056 | bytes 15729664 | tf_op jit(solution)/shard_map/while/body/eval_jaxpr/cond/branch_1_fun/dot_general | solution.py:33
  510.3 5.3 convert_bitcast_fusion
  515.6 9.3 %convert_bitcast_fusion.1 = (bf16[1,3584,512]{2,1,0:T(8,128)(2,1)}, bf16[1,3584,512]{2,1,0:T(8,128)(2,1)}) fusion(f32[3584,512]{1,0:T(8,128)} %get-tuple-element.573, f32[3584,512]{1,0:T(8,128)} %get-tuple-element.572), kind=kLoop, calls=%fused_computation.39 | loop fusion | flops 3670016 | bytes 22020096 | tf_op jit(solution)/shard_map/broadcast_in_dim | solution.py:196
  524.9 4.4 convolution_convert_fusion.2
  (189 shorter events, 126.8 us)
Async XLA Ops:
  7.2 63.6 %copy-start = (bf16[256,3584]{1,0:T(8,128)(2,1)S(1)}, bf16[256,3584]{1,0:T(8,128)(2,1)}, u32[]{:S(2)}) copy-start(bf16[256,3584]{1,0:T(8,128)(2,1)} %param.15) | copy-start | bytes 5505028
  7.2 137.9 %all-gather.6.cloned.1.call-start = ((), (), s32[]{:S(2)}) async-start(), calls=%async_computation.6 | async-start | bytes 11010048 | tf_op jit(solution)/shard_map/all_gather | solution.py:162
  70.7 74.4 %all-gather.4.cloned.1.call-start = ((), (), s32[]{:S(2)}) async-start(), calls=%async_computation.5 | async-start | bytes 11010048 | tf_op jit(solution)/shard_map/all_gather | solution.py:161
  124.0 7.4 %copy-start.7 = (u32[128]{0:T(128)S(1)}, u32[128]{0:T(128)}, u32[]{:S(2)}) copy-start(u32[128]{0:T(128)} %constant.129) | copy-start | bytes 1540
  124.8 14.9 %all-to-all-start = ((s32[64,1,1]{2,1,0:T(1,128)}), s32[64,1,1]{2,1,0:T(1,128)S(1)}, u32[]{:S(2)}, u32[]{:S(2)}) async-start(s32[64,1,1]{2,1,0:T(1,128)} %copy.17), calls=%async_computation | async-start | bytes 65536 | tf_op jit(solution)/shard_map/all_to_all | solution.py:158
  131.4 181.4 %reduce-scatter.2.cloned.1.call-start = ((), (), s32[]{:S(2)}) async-start(), calls=%async_computation.7 | async-start | bytes 11010048 | tf_op jit(solution)/shard_map/reduce_scatter | solution.py:177
  152.9 3.4 copy-start.5
  152.9 5.3 copy-start.6
  161.5 2.4 copy-start.4
  170.7 3.4 copy-start.5
  170.7 5.3 copy-start.6
  179.3 2.4 copy-start.4
  188.6 3.4 copy-start.5
  188.6 5.3 copy-start.6
  197.1 2.4 copy-start.4
  206.4 3.4 copy-start.5
  206.4 5.3 copy-start.6
  215.0 2.4 copy-start.4
  224.2 3.4 copy-start.5
  224.2 5.3 copy-start.6
  232.8 2.4 copy-start.4
  242.0 3.4 copy-start.5
  242.0 5.3 copy-start.6
  250.6 2.4 copy-start.4
  259.8 3.4 copy-start.5
  259.8 5.3 copy-start.6
  268.4 2.4 copy-start.4
  277.6 3.4 copy-start.5
  277.6 5.3 copy-start.6
  286.2 2.4 copy-start.4
  312.8 212.1 %all-to-all-start.3 = ((bf16[64,8,3584]{2,1,0:T(8,128)(2,1)}), bf16[64,8,3584]{2,1,0:T(8,128)(2,1)}, u32[]{:S(2)}, u32[]{:S(2)}) async-start(bf16[64,8,3584]{2,1,0:T(8,128)(2,1)} %reduce-scatter.2.cloned.1.call-done), calls=%async_computation.4 | async-start | bytes 7340032 | tf_op jit(solution)/shard_map/all_to_all | solution.py:183
  336.2 7.7 %copy-start.2 = (f32[512,3584]{1,0:T(8,128)S(1)}, f32[512,3584]{1,0:T(8,128)}, u32[]{:S(2)}) copy-start(f32[512,3584]{1,0:T(8,128)} %get-tuple-element.540) | copy-start | bytes 22020100 | tf_op jit(solution)/shard_map/while/body/eval_jaxpr/cond
  346.6 10.2 %copy-start.3 = (f32[512,3584]{1,0:T(8,128)}, f32[512,3584]{1,0:T(8,128)S(1)}, u32[]{:S(2)}) copy-start(f32[512,3584]{1,0:T(8,128)S(1)} %convolution_add_fusion.1) | copy-start | bytes 22020100 | tf_op jit(solution)/shard_map/while/body/eval_jaxpr/cond
  358.1 7.7 %copy-start.2 = (f32[512,3584]{1,0:T(8,128)S(1)}, f32[512,3584]{1,0:T(8,128)}, u32[]{:S(2)}) copy-start(f32[512,3584]{1,0:T(8,128)} %get-tuple-element.540) | copy-start | bytes 22020100 | tf_op jit(solution)/shard_map/while/body/eval_jaxpr/cond
  368.5 10.2 %copy-start.3 = (f32[512,3584]{1,0:T(8,128)}, f32[512,3584]{1,0:T(8,128)S(1)}, u32[]{:S(2)}) copy-start(f32[512,3584]{1,0:T(8,128)S(1)} %convolution_add_fusion.1) | copy-start | bytes 22020100 | tf_op jit(solution)/shard_map/while/body/eval_jaxpr/cond
  380.0 7.7 %copy-start.2 = (f32[512,3584]{1,0:T(8,128)S(1)}, f32[512,3584]{1,0:T(8,128)}, u32[]{:S(2)}) copy-start(f32[512,3584]{1,0:T(8,128)} %get-tuple-element.540) | copy-start | bytes 22020100 | tf_op jit(solution)/shard_map/while/body/eval_jaxpr/cond
  390.5 10.2 %copy-start.3 = (f32[512,3584]{1,0:T(8,128)}, f32[512,3584]{1,0:T(8,128)S(1)}, u32[]{:S(2)}) copy-start(f32[512,3584]{1,0:T(8,128)S(1)} %convolution_add_fusion.1) | copy-start | bytes 22020100 | tf_op jit(solution)/shard_map/while/body/eval_jaxpr/cond
  402.0 7.7 %copy-start.2 = (f32[512,3584]{1,0:T(8,128)S(1)}, f32[512,3584]{1,0:T(8,128)}, u32[]{:S(2)}) copy-start(f32[512,3584]{1,0:T(8,128)} %get-tuple-element.540) | copy-start | bytes 22020100 | tf_op jit(solution)/shard_map/while/body/eval_jaxpr/cond
  412.4 10.2 %copy-start.3 = (f32[512,3584]{1,0:T(8,128)}, f32[512,3584]{1,0:T(8,128)S(1)}, u32[]{:S(2)}) copy-start(f32[512,3584]{1,0:T(8,128)S(1)} %convolution_add_fusion.1) | copy-start | bytes 22020100 | tf_op jit(solution)/shard_map/while/body/eval_jaxpr/cond
  423.9 7.7 %copy-start.2 = (f32[512,3584]{1,0:T(8,128)S(1)}, f32[512,3584]{1,0:T(8,128)}, u32[]{:S(2)}) copy-start(f32[512,3584]{1,0:T(8,128)} %get-tuple-element.540) | copy-start | bytes 22020100 | tf_op jit(solution)/shard_map/while/body/eval_jaxpr/cond
  434.3 10.2 %copy-start.3 = (f32[512,3584]{1,0:T(8,128)}, f32[512,3584]{1,0:T(8,128)S(1)}, u32[]{:S(2)}) copy-start(f32[512,3584]{1,0:T(8,128)S(1)} %convolution_add_fusion.1) | copy-start | bytes 22020100 | tf_op jit(solution)/shard_map/while/body/eval_jaxpr/cond
  445.8 7.7 %copy-start.2 = (f32[512,3584]{1,0:T(8,128)S(1)}, f32[512,3584]{1,0:T(8,128)}, u32[]{:S(2)}) copy-start(f32[512,3584]{1,0:T(8,128)} %get-tuple-element.540) | copy-start | bytes 22020100 | tf_op jit(solution)/shard_map/while/body/eval_jaxpr/cond
  456.3 10.2 %copy-start.3 = (f32[512,3584]{1,0:T(8,128)}, f32[512,3584]{1,0:T(8,128)S(1)}, u32[]{:S(2)}) copy-start(f32[512,3584]{1,0:T(8,128)S(1)} %convolution_add_fusion.1) | copy-start | bytes 22020100 | tf_op jit(solution)/shard_map/while/body/eval_jaxpr/cond
  467.7 7.7 %copy-start.2 = (f32[512,3584]{1,0:T(8,128)S(1)}, f32[512,3584]{1,0:T(8,128)}, u32[]{:S(2)}) copy-start(f32[512,3584]{1,0:T(8,128)} %get-tuple-element.540) | copy-start | bytes 22020100 | tf_op jit(solution)/shard_map/while/body/eval_jaxpr/cond
  478.2 10.2 %copy-start.3 = (f32[512,3584]{1,0:T(8,128)}, f32[512,3584]{1,0:T(8,128)S(1)}, u32[]{:S(2)}) copy-start(f32[512,3584]{1,0:T(8,128)S(1)} %convolution_add_fusion.1) | copy-start | bytes 22020100 | tf_op jit(solution)/shard_map/while/body/eval_jaxpr/cond
  489.7 7.7 %copy-start.2 = (f32[512,3584]{1,0:T(8,128)S(1)}, f32[512,3584]{1,0:T(8,128)}, u32[]{:S(2)}) copy-start(f32[512,3584]{1,0:T(8,128)} %get-tuple-element.540) | copy-start | bytes 22020100 | tf_op jit(solution)/shard_map/while/body/eval_jaxpr/cond
  500.1 10.2 %copy-start.3 = (f32[512,3584]{1,0:T(8,128)}, f32[512,3584]{1,0:T(8,128)S(1)}, u32[]{:S(2)}) copy-start(f32[512,3584]{1,0:T(8,128)S(1)} %convolution_add_fusion.1) | copy-start | bytes 22020100 | tf_op jit(solution)/shard_map/while/body/eval_jaxpr/cond
  515.6 13.7 %copy-start.1 = (bf16[256,3584]{1,0:T(8,128)(2,1)S(1)}, bf16[256,3584]{1,0:T(8,128)(2,1)}, u32[]{:S(2)}) copy-start(bf16[256,3584]{1,0:T(8,128)(2,1)} %param.15) | copy-start | bytes 5505028
Sparse Core Ops, SparseCore 0:
  70.8 19.2 all-gather.5
  124.2 19.2 all-gather.3
  294.3 18.3 reduce-scatter.1
where the time goes:
time: 537 us; the launch traced here: 536 us
  matrix products  276 us (51%)
  blocking collectives  113 us (21%)
  local copies, waits for them, and re-layouts  59.1 us (11%)
  waiting for transfers between devices  25.7 us (5%)
  other arithmetic  19 us (4%)
  starting transfers between devices  17.1 us (3%)
  between operations  14.5 us (3%)
  loops' own time  11.4 us (2%)
    dot_general x8, matrix products, weight_sums(): lax.dot_general(rows_x, d_up, (((0,), (0,)), ((), ())), preferred_element...  81.5 us
    dot_general x8, matrix products, weight_sums(): lax.dot_general(rows_x, d_gate, (((0,), (0,)), ((), ())), preferred_eleme...  61.1 us
    all_to_all x1, blocking collectives, local(): lax.all_to_all(sent_cots, 'expert', split_axis=0, concat_axis=0, tiled=True)  57.5 us
    all_to_all x1, blocking collectives, local(): lax.all_to_all(sent_rows, 'expert', split_axis=0, concat_axis=0, tiled=True)  52.2 us
    dynamic_update_slice x24, local copies, waits for them, and re-layouts, add_tile(): lax.dynamic_update_slice_in_dim(whole, piece, start, 0)  26.8 us
    dot_general x8, matrix products, front_rows(): lax.dot_general(rows_cot, down_w, (((1,), (1,)), ((), ())), preferred_ele...  25.7 us
    dot_general x8, matrix products, front_rows(): up_pre = jnp.dot(rows_x, up_w, preferred_element_type=jnp.float32)  24.9 us
    dot_general x8, matrix products, weight_sums(): lax.dot_general(hidden, rows_cot, (((0,), (0,)), ((), ())), preferred_ele...  22.2 us
  transfers between devices with their start and end apart: 5, of which 2 were waited for; matrix products, arithmetic and copies ran while one was open for 37% of the time, Pallas kernels for 0%

commit v1 on v0

--- a/solution.py
+++ b/solution.py
@@ -167,12 +167,10 @@
     got_counts = got_counts.reshape(groups, owners, 1)
     slots_all = owners * groups * capacity
     weights_own = (w_gate[0], w_up[0], w_down[0])
-    hidden, d_gate, d_up, dx_part = run_front(got_rows, got_cots, got_counts, weights_own, capacity)
     rows_x = got_rows.reshape(slots_all, model_width)
     rows_cot = got_cots.reshape(slots_all, model_width)
-    grad_gate, grad_up, grad_down = run_sums(
-        rows_x, rows_cot, hidden, d_gate, d_up, got_counts, capacity
-    )
+    hidden, d_gate, d_up, dx_part = front_rows(rows_x, rows_cot, *weights_own)
+    grad_gate, grad_up, grad_down = weight_sums(rows_x, rows_cot, hidden, d_gate, d_up)
     dx_float = dx_part.astype(jnp.float32)
     summed = lax.psum_scatter(
         dx_float.reshape(groups * owners, capacity, model_width).astype(jnp.bfloat16),

time: 537 us -> 260 us (0.48)
  matrix products: 276 us -> 71.7 us
  local copies, waits for them, and re-layouts: 59.1 us -> 1.67 us
  waiting for transfers between devices: 25.7 us -> 47.9 us
  other arithmetic: 19 us -> 2.93 us
  loops' own time: 11.4 us -> 0 us
  starting transfers between devices: 17.1 us -> 11 us
    dot_general x8 -> x1, matrix products: 81.5 us -> 8.76 us  [weight_sums(): lax.dot_general(rows_x, d_up, (((0,), (0,)), ((), ())), preferred_element...]
    dot_general x8 -> x1, matrix products: 61.1 us -> 8.76 us  [weight_sums(): lax.dot_general(rows_x, d_gate, (((0,), (0,)), ((), ())), preferred_eleme...]
    dynamic_update_slice x24 -> x0, local copies, waits for them, and re-layouts: 26.8 us -> none  [add_tile(): lax.dynamic_update_slice_in_dim(whole, piece, start, 0)]
    all_to_all x1, waiting for transfers between devices: 0.01 us -> 23.4 us  [local(): lax.all_to_all(summed, 'expert', split_axis=0, concat_axis=0, tiled=True)]
    dot_general x8 -> x1, matrix products: 24.9 us -> 5.34 us  [front_rows(): up_pre = jnp.dot(rows_x, up_w, preferred_element_type=jnp.float32)]
    dot_general x8 -> x1, matrix products: 22.2 us -> 5.84 us  [weight_sums(): lax.dot_general(hidden, rows_cot, (((0,), (0,)), ((), ())), preferred_ele...]
    dot_general x8 -> x1, matrix products: 25.7 us -> 10.1 us  [front_rows(): lax.dot_general(rows_cot, down_w, (((1,), (1,)), ((), ())), preferred_ele...]
    broadcast_in_dim x2 -> x0, other arithmetic: 14.6 us -> none  [the longest x1 9.29 us: local(): grad_up.astype(jnp.bfloat16)[None]]
  transfers between devices with their start and end apart: 5 -> 4, of which waited for: 2 -> 3; matrix products, arithmetic and copies ran while one was open for 37% -> 15% of each run, Pallas kernels for 0% -> 0%
where the time goes in v1:
time: 260 us; the launch traced here: 259 us
  blocking collectives  110 us (42%)
  matrix products  71.7 us (28%)
  waiting for transfers between devices  47.9 us (18%)
  between operations  13.9 us (5%)
  starting transfers between devices  11 us (4%)
  other arithmetic  2.93 us (1%)
    all_to_all x1, blocking collectives, local(): lax.all_to_all(sent_rows, 'expert', split_axis=0, concat_axis=0, tiled=True)  57.5 us
    all_to_all x1, blocking collectives, local(): lax.all_to_all(sent_cots, 'expert', split_axis=0, concat_axis=0, tiled=True)  52.2 us
    all_to_all x1, waiting for transfers between devices, local(): lax.all_to_all(summed, 'expert', split_axis=0, concat_axis=0, tiled=True)  23.4 us
    reduce_scatter x1, waiting for transfers between devices, local(): lax.psum_scatter(dx_float.reshape(groups * owners, capacity, model_width)...  20.2 us
    all_to_all x1, starting transfers between devices, local(): lax.all_to_all(summed, 'expert', split_axis=0, concat_axis=0, tiled=True)  10.7 us
    dot_general x1, matrix products, front_rows(): lax.dot_general(rows_cot, down_w, (((1,), (1,)), ((), ())), preferred_ele...  10.1 us
    dot_general x1, matrix products, front_rows(): gate_pre = jnp.dot(rows_x, gate_w, preferred_element_type=jnp.float32)  9.54 us
    dot_general x1, matrix products, front_rows(): lax.dot_general(d_up, up_w, (((1,), (1,)), ((), ())), preferred_element_t...  9.26 us
  transfers between devices with their start and end apart: 4, of which 3 were waited for; matrix products, arithmetic and copies ran while one was open for 15% of the time, Pallas kernels for 0%

profile of v1, /device:TPU:1, one launch (start us, length us, event | category | flops | bytes accessed | tf_op | source)
XLA Modules:
  0.0 258.7 jit_solution(10464166641324584218)
XLA Ops:
  7.2 0.0 copy-start
  7.2 0.0 all-gather.5.cloned.1.call-start
  7.2 0.8 fusion.49
  8.0 0.6 reduce-window.6
  8.6 0.2 slice_reduce_fusion
  8.9 0.8 fusion.48
  9.7 0.7 multiply_add_fusion
  10.3 0.0 copy-done
  10.3 1.1 fusion.32
  11.5 57.5 %all_to_all.15 = bf16[64,8,3584]{2,1,0:T(8,128)(2,1)} all-to-all(bf16[64,8,3584]{2,1,0:T(8,128)(2,1)S(1)} %fusion.32), channel_id=1, replica_groups=mesh['dp'=2,'expert'=64] {'expert'}, dimensions={0} | all-to-all | bytes 7340032 | tf_op jit(solution)/shard_map/all_to_all | solution.py:156
  68.9 0.0 copy-start.2
  68.9 0.0 copy-start.3
  68.9 0.0 all-gather.5.cloned.1.call-update
  69.0 0.0 all-gather.3.cloned.1.call-start
  69.0 1.4 copy-done.2
  70.4 0.0 copy-done.3
  70.4 1.2 fusion.31
  71.7 52.2 %all_to_all.16 = bf16[64,8,3584]{2,1,0:T(8,128)(2,1)} all-to-all(bf16[64,8,3584]{2,1,0:T(8,128)(2,1)S(1)} %fusion.31), channel_id=1, replica_groups=mesh['dp'=2,'expert'=64] {'expert'}, dimensions={0} | all-to-all | bytes 7340032 | tf_op jit(solution)/shard_map/all_to_all | solution.py:157
  123.9 0.0 all-gather.3.cloned.1.call-update
  123.9 0.2 reduce-scatter.2.cloned.1.call-start
  124.1 0.0 all-gather.5.cloned.1.call-done
  124.2 0.0 copy-start.4
  124.2 0.0 copy-start.6
  124.2 9.5 %fusion.4 = f32[1024,512]{1,0:T(8,128)} fusion(bf16[128,8,3584]{2,1,0:T(8,128)(2,1)} %all-gather.5.cloned.1.call-done, bf16[1,3584,512]{2,1,0:T(8,128)(2,1)} %param.11), kind=kOutput, calls=%fused_computation.5 | convolution fusion | flops 3758096384 | bytes 13107200 | tf_op jit(solution)/shard_map/dot_general | solution.py:8
  133.7 0.0 copy-done.4
  133.7 0.0 copy-done.6
  133.7 5.3 %fusion.6 = f32[1024,512]{1,0:T(8,128)} fusion(bf16[128,8,3584]{2,1,0:T(8,128)(2,1)S(1)} %copy-done.4, bf16[1,3584,512]{2,1,0:T(8,128)(2,1)S(1)} %copy-done.6), kind=kOutput, calls=%fused_computation.7 | convolution fusion | flops 3758096384 | bytes 13107200 | tf_op jit(solution)/shard_map/dot_general | solution.py:9
  139.1 4.2 %all-gather.3.cloned.1.call-done = bf16[128,8,3584]{2,1,0:T(8,128)(2,1)} async-done(((bf16[64,8,3584]{2,1,0:T(8,128)(2,1)}), bf16[128,8,3584]{2,1,0:T(8,128)(2,1)}) %all-gather.3.cloned.1.call-update) | async-done | bytes 7340048 | tf_op jit(solution)/shard_map/all_gather | solution.py:162
  143.3 0.0 copy-start.5
  143.3 10.1 %multiply_convert_fusion.2 = (bf16[1024,512]{1,0:T(8,128)(2,1)S(1)}, bf16[1024,512]{1,0:T(8,128)(2,1)S(1)}) fusion(f32[1024,512]{1,0:T(8,128)} %fusion.4, f32[1024,512]{1,0:T(8,128)} %fusion.6, bf16[1,512,3584]{2,1,0:T(8,128)(2,1)} %param.13, bf16[128,8,3584]{2,1,0:T(8,128)(2,1)} %all-gather.3.cloned.1.call-done), kind=kOutput, calls=%fused_computation.34 | convolution fusion | flops 3764912128 | bytes 17301504 | tf_op jit(solution)/shard_map/dot_general | solution.py:13
  153.4 0.0 copy-done.5
  153.4 0.0 copy-start.7
  153.4 7.4 %fusion.34 = f32[1024,3584]{1,0:T(8,128)} fusion(bf16[1024,512]{1,0:T(8,128)(2,1)S(1)} %get-tuple-element.5, bf16[1,3584,512]{2,1,0:T(8,128)(2,1)S(1)} %copy-done.5), kind=kOutput, calls=%fused_computation.26 | convolution fusion | flops 3758096384 | bytes 19398656 | tf_op jit(solution)/shard_map/dot_general | solution.py:20
  160.8 0.0 copy-done.7
  160.8 9.3 %fusion.12 = bf16[128,8,3584]{2,1,0:T(8,128)(2,1)} fusion(f32[1024,3584]{1,0:T(8,128)} %fusion.34, bf16[1024,512]{1,0:T(8,128)(2,1)S(1)} %get-tuple-element.4, bf16[1,3584,512]{2,1,0:T(8,128)(2,1)S(1)} %copy-done.7), kind=kOutput, calls=%fused_computation.13 | convolution fusion | flops 3765436416 | bytes 26738688 | tf_op jit(solution)/shard_map/dot_general | solution.py:23
  170.0 0.0 reduce-scatter.2.cloned.1.call-update
  170.1 20.2 %reduce-scatter.2.cloned.1.call-done = bf16[64,8,3584]{2,1,0:T(8,128)(2,1)} async-done(((bf16[128,8,3584]{2,1,0:T(8,128)(2,1)}), bf16[64,8,3584]{2,1,0:T(8,128)(2,1)}) %reduce-scatter.2.cloned.1.call-update) | async-done | bytes 3670032 | tf_op jit(solution)/shard_map/reduce_scatter | solution.py:175
  190.3 10.7 %all-to-all-start.2 = ((bf16[64,8,3584]{2,1,0:T(8,128)(2,1)}), bf16[64,8,3584]{2,1,0:T(8,128)(2,1)}, u32[]{:S(2)}, u32[]{:S(2)}) async-start(bf16[64,8,3584]{2,1,0:T(8,128)(2,1)} %reduce-scatter.2.cloned.1.call-done), calls=%async_computation.3 | async-start | bytes 7340032 | tf_op jit(solution)/shard_map/all_to_all | solution.py:181
  200.9 0.0 slice-start
  201.0 8.8 %fusion.22 = bf16[1,3584,512]{2,1,0:T(8,128)(2,1)} fusion(bf16[1024,512]{1,0:T(8,128)(2,1)S(1)} %get-tuple-element.4, bf16[128,8,3584]{2,1,0:T(8,128)(2,1)} %all-gather.5.cloned.1.call-done), kind=kOutput, calls=%fused_computation.19 | convolution fusion | flops 3759931392 | bytes 12058624 | tf_op jit(solution)/shard_map/dot_general | solution.py:33
  209.7 0.0 slice-start.1
  209.7 0.0 copy-start.8
  209.7 0.0 copy-start.9
  209.7 8.8 %fusion.25 = bf16[1,3584,512]{2,1,0:T(8,128)(2,1)} fusion(bf16[1024,512]{1,0:T(8,128)(2,1)S(1)} %get-tuple-element.5, bf16[128,8,3584]{2,1,0:T(8,128)(2,1)} %all-gather.5.cloned.1.call-done), kind=kOutput, calls=%fused_computation.20 | convolution fusion | flops 3759931392 | bytes 12058624 | tf_op jit(solution)/shard_map/dot_general | solution.py:30
  218.5 0.0 slice-done
  218.5 0.0 slice-done.1
  218.5 0.0 copy-done.8
  218.5 0.0 copy-done.9
  218.5 0.0 copy-start.1
  218.5 5.8 %fusion.28 = bf16[1,512,3584]{2,1,0:T(8,128)(2,1)} fusion(bf16[128,8,3584]{2,1,0:T(8,128)(2,1)S(1)} %bitcast.90, f32[1024,512]{1,0:T(8,128)S(1)} %copy-done.9, f32[1024,512]{1,0:T(8,128)S(1)} %copy-done.8), kind=kOutput, calls=%fused_computation.21 | convolution fusion | flops 3763077120 | bytes 15204352 | tf_op jit(solution)/shard_map/dot_general | solution.py:36
  224.4 23.4 %all-to-all-done.2 = bf16[64,8,3584]{2,1,0:T(8,128)(2,1)} async-done(((bf16[64,8,3584]{2,1,0:T(8,128)(2,1)}), bf16[64,8,3584]{2,1,0:T(8,128)(2,1)}, u32[]{:S(2)}, u32[]{:S(2)}) %all-to-all-start.2) | async-done | bytes 3670048 | tf_op jit(solution)/shard_map/all_to_all | solution.py:181
  247.8 4.4 %convolution_convert_fusion.2 = bf16[256,3584]{1,0:T(8,128)(2,1)} fusion(bf16[64,8,3584]{2,1,0:T(8,128)(2,1)} %all-to-all-done.2, s32[256]{0:T(256)S(1)} %multiply_add_fusion), kind=kOutput, calls=%fused_computation.24 | convolution fusion | flops 940572672 | bytes 5506048 | tf_op jit(solution)/shard_map/dot_general | solution.py:182
  252.2 0.0 copy-done.1
  (3 shorter events, 0.0 us)
Async XLA Ops:
  7.2 3.2 %copy-start = (bf16[256,3584]{1,0:T(8,128)(2,1)S(1)}, bf16[256,3584]{1,0:T(8,128)(2,1)}, u32[]{:S(2)}) copy-start(bf16[256,3584]{1,0:T(8,128)(2,1)} %param.7) | copy-start | bytes 5505028
  7.2 117.0 %all-gather.5.cloned.1.call-start = ((), (), s32[]{:S(2)}) async-start(), calls=%async_computation.5 | async-start | bytes 11010048 | tf_op jit(solution)/shard_map/all_gather | solution.py:161
  68.9 1.5 copy-start.2
  68.9 1.5 copy-start.3
  69.0 74.3 %all-gather.3.cloned.1.call-start = ((), (), s32[]{:S(2)}) async-start(), calls=%async_computation.4 | async-start | bytes 11010048 | tf_op jit(solution)/shard_map/all_gather | solution.py:162
  123.9 66.4 %reduce-scatter.2.cloned.1.call-start = ((), (), s32[]{:S(2)}) async-start(), calls=%async_computation.6 | async-start | bytes 11010048 | tf_op jit(solution)/shard_map/reduce_scatter | solution.py:175
  124.2 9.6 %copy-start.4 = (bf16[128,8,3584]{2,1,0:T(8,128)(2,1)S(1)}, bf16[128,8,3584]{2,1,0:T(8,128)(2,1)}, u32[]{:S(2)}) copy-start(bf16[128,8,3584]{2,1,0:T(8,128)(2,1)} %all-gather.5.cloned.1.call-done) | copy-start | bytes 22020100
  124.2 9.6 %copy-start.6 = (bf16[1,3584,512]{2,1,0:T(8,128)(2,1)S(1)}, bf16[1,3584,512]{2,1,0:T(8,128)(2,1)}, u32[]{:S(2)}) copy-start(bf16[1,3584,512]{2,1,0:T(8,128)(2,1)} %param.12) | copy-start | bytes 11010052
  143.3 10.1 %copy-start.5 = (bf16[1,3584,512]{2,1,0:T(8,128)(2,1)S(1)}, bf16[1,3584,512]{2,1,0:T(8,128)(2,1)}, u32[]{:S(2)}) copy-start(bf16[1,3584,512]{2,1,0:T(8,128)(2,1)} %param.11) | copy-start | bytes 11010052
  153.4 7.4 %copy-start.7 = (bf16[1,3584,512]{2,1,0:T(8,128)(2,1)S(1)}, bf16[1,3584,512]{2,1,0:T(8,128)(2,1)}, u32[]{:S(2)}) copy-start(bf16[1,3584,512]{2,1,0:T(8,128)(2,1)} %param.12) | copy-start | bytes 11010052
  190.3 57.5 %all-to-all-start.2 = ((bf16[64,8,3584]{2,1,0:T(8,128)(2,1)}), bf16[64,8,3584]{2,1,0:T(8,128)(2,1)}, u32[]{:S(2)}, u32[]{:S(2)}) async-start(bf16[64,8,3584]{2,1,0:T(8,128)(2,1)} %reduce-scatter.2.cloned.1.call-done), calls=%async_computation.3 | async-start | bytes 7340032 | tf_op jit(solution)/shard_map/all_to_all | solution.py:181
  200.9 17.5 %slice-start = ((s8[7340032]{0:T(1024)(128)(4,1)}), s8[4194304]{0:T(1024)(128)(4,1)S(1)}, s32[]{:S(2)}) async-start(s8[7340032]{0:T(1024)(128)(4,1)} %bitcast.89), calls=%async_computation.7 | async-start | bytes 8388608
  209.7 8.8 %slice-start.1 = ((s8[7340032]{0:T(1024)(128)(4,1)}), s8[3145728]{0:T(1024)(128)(4,1)S(1)}, s32[]{:S(2)}) async-start(s8[7340032]{0:T(1024)(128)(4,1)} %bitcast.89), calls=%async_computation.8 | async-start | bytes 6291456
  209.7 8.8 %copy-start.8 = (f32[1024,512]{1,0:T(8,128)S(1)}, f32[1024,512]{1,0:T(8,128)}, u32[]{:S(2)}) copy-start(f32[1024,512]{1,0:T(8,128)} %fusion.4) | copy-start | bytes 6291460
  209.7 8.8 %copy-start.9 = (f32[1024,512]{1,0:T(8,128)S(1)}, f32[1024,512]{1,0:T(8,128)}, u32[]{:S(2)}) copy-start(f32[1024,512]{1,0:T(8,128)} %fusion.6) | copy-start | bytes 6291460
  218.5 33.7 %copy-start.1 = (bf16[256,3584]{1,0:T(8,128)(2,1)S(1)}, bf16[256,3584]{1,0:T(8,128)(2,1)}, u32[]{:S(2)}) copy-start(bf16[256,3584]{1,0:T(8,128)(2,1)} %param.7) | copy-start | bytes 5505028
Sparse Core Ops, SparseCore 0:
  69.1 19.2 all-gather.4
  124.0 19.2 all-gather.2
  170.2 20.0 reduce-scatter.1

commit v2 on v1

--- a/solution.py
+++ b/solution.py
@@ -134,7 +134,6 @@
     onehot = (flat_ids[:, None] == jnp.arange(owners, dtype=jnp.int32)[None, :]).astype(jnp.int32)
     before = jnp.cumsum(onehot, axis=0) - onehot
     slot_rank = jnp.sum(before * onehot, axis=1)
-    counts = jnp.sum(onehot, axis=0).reshape(owners, 1)
     position = flat_ids * capacity + slot_rank
     copy_rows = tokens[:, None, :].reshape(copies, model_width)
     copy_tok_cot = cotangent[:, None, :].reshape(copies, model_width)
@@ -142,43 +141,31 @@
     placing = (jnp.arange(owners * capacity, dtype=jnp.int32)[:, None] == position[None, :]).astype(
         jnp.bfloat16
     )
-    sent_rows = (
-        jnp.dot(placing, copy_rows, preferred_element_type=jnp.float32)
+    stacked = jnp.stack([copy_rows, copy_cots], axis=1)
+    sent = (
+        jnp.einsum("pc,cxd->pxd", placing, stacked, preferred_element_type=jnp.float32)
         .astype(jnp.bfloat16)
-        .reshape(owners, capacity, model_width)
-    )
-    sent_cots = (
-        jnp.dot(placing, copy_cots, preferred_element_type=jnp.float32)
-        .astype(jnp.bfloat16)
-        .reshape(owners, capacity, model_width)
-    )
-    came_rows, came_cots, came_counts = (
-        lax.all_to_all(sent_rows, "expert", split_axis=0, concat_axis=0, tiled=True),
-        lax.all_to_all(sent_cots, "expert", split_axis=0, concat_axis=0, tiled=True),
-        lax.all_to_all(counts, "expert", split_axis=0, concat_axis=0, tiled=True),
-    )
-    got_rows, got_cots, got_counts = (
-        lax.all_gather(came_rows, "dp", axis=0, tiled=True),
-        lax.all_gather(came_cots, "dp", axis=0, tiled=True),
-        lax.all_gather(came_counts, "dp", axis=0, tiled=True),
-    )
-    got_rows = got_rows.reshape(groups, owners, capacity, model_width)
-    got_cots = got_cots.reshape(groups, owners, capacity, model_width)
-    got_counts = got_counts.reshape(groups, owners, 1)
-    slots_all = owners * groups * capacity
+        .reshape(owners, capacity, 2, model_width)
+    )
+    came = lax.all_to_all(sent, "expert", split_axis=0, concat_axis=0, tiled=True)
+    swap = [(0, 1), (1, 0)]
+    other = lax.ppermute(came, "dp", swap)
+    half_slots = owners * capacity
     weights_own = (w_gate[0], w_up[0], w_down[0])
-    rows_x = got_rows.reshape(slots_all, model_width)
-    rows_cot = got_cots.reshape(slots_all, model_width)
-    hidden, d_gate, d_up, dx_part = front_rows(rows_x, rows_cot, *weights_own)
-    grad_gate, grad_up, grad_down = weight_sums(rows_x, rows_cot, hidden, d_gate, d_up)
-    dx_float = dx_part.astype(jnp.float32)
-    summed = lax.psum_scatter(
-        dx_float.reshape(groups * owners, capacity, model_width).astype(jnp.bfloat16),
-        "dp",
-        scatter_dimension=0,
-        tiled=True,
-    )
-    returned = lax.all_to_all(summed, "expert", split_axis=0, concat_axis=0, tiled=True)
+    own_x = came[:, :, 0].reshape(half_slots, model_width)
+    own_cot = came[:, :, 1].reshape(half_slots, model_width)
+    own_h, own_dg, own_du, own_dx = front_rows(own_x, own_cot, *weights_own)
+    oth_x = other[:, :, 0].reshape(half_slots, model_width)
+    oth_cot = other[:, :, 1].reshape(half_slots, model_width)
+    oth_h, oth_dg, oth_du, oth_dx = front_rows(oth_x, oth_cot, *weights_own)
+    back = lax.ppermute(oth_dx, "dp", swap)
+    summed = (own_dx.astype(jnp.float32) + back.astype(jnp.float32)).astype(jnp.bfloat16)
+    returned = lax.all_to_all(
+        summed.reshape(owners, capacity, model_width), "expert", split_axis=0, concat_axis=0, tiled=True
+    )
+    sums_own = weight_sums(own_x, own_cot, own_h, own_dg, own_du)
+    sums_oth = weight_sums(oth_x, oth_cot, oth_h, oth_dg, oth_du)
+    grad_gate, grad_up, grad_down = (a + b for a, b in zip(sums_own, sums_oth))
     copy_grad = lax.dot_general(
         placing,
         returned.reshape(owners * capacity, model_width),

time: 260 us -> 214 us (0.82)
  waiting for transfers between devices: 47.9 us -> 29.3 us
  between operations: 13.9 us -> 1.04 us
  blocking collectives: 110 us -> 97.2 us
  matrix products: 71.7 us -> 62.6 us
  local copies, waits for them, and re-layouts: 1.67 us -> 8.47 us
    reduce_scatter x1 -> x0, waiting for transfers between devices: 20.2 us -> none  [local(): lax.psum_scatter(dx_float.reshape(groups * owners, capacity, model_width)...]
    all_to_all x2 -> x1, blocking collectives: 110 us -> 97.2 us  [local(): lax.all_to_all(sent, 'expert', split_axis=0, concat_axis=0, tiled=True)]
    ppermute x0 -> x2, waiting for transfers between devices: none -> 11.3 us  [the longest x1 11.3 us: local(): other = lax.ppermute(came, 'dp', swap)]
    dot_general x1 -> x2, matrix products: 8.76 us -> 14.7 us  [weight_sums(): lax.dot_general(rows_x, d_up, (((0,), (0,)), ((), ())), preferred_element...]
    all_to_all x1, waiting for transfers between devices: 23.4 us -> 18 us  [local(): lax.all_to_all(summed.reshape(owners, capacity, model_width), 'expert', s...]
    dot_general x1 -> x2, matrix products: 9.54 us -> 4.16 us  [front_rows(): gate_pre = jnp.dot(rows_x, gate_w, preferred_element_type=jnp.float32)]
    dot_general x1 -> x2, matrix products: 10.1 us -> 4.81 us  [front_rows(): lax.dot_general(rows_cot, down_w, (((1,), (1,)), ((), ())), preferred_ele...]
    all_to_all x1, starting transfers between devices: 10.7 us -> 6.09 us  [local(): lax.all_to_all(summed.reshape(owners, capacity, model_width), 'expert', s...]
  transfers between devices with their start and end apart: 4 -> 3, of which waited for: 3 -> 2; matrix products, arithmetic and copies ran while one was open for 15% -> 18% of each run, Pallas kernels for 0% -> 0%
where the time goes in v2:
time: 214 us; the launch traced here: 213 us
  blocking collectives  97.2 us (45%)
  matrix products  62.6 us (29%)
  waiting for transfers between devices  29.3 us (14%)
  starting transfers between devices  9.99 us (5%)
  local copies, waits for them, and re-layouts  8.47 us (4%)
  other arithmetic  4.89 us (2%)
    all_to_all x1, blocking collectives, local(): lax.all_to_all(sent, 'expert', split_axis=0, concat_axis=0, tiled=True)  97.2 us
    all_to_all x1, waiting for transfers between devices, local(): lax.all_to_all(summed.reshape(owners, capacity, model_width), 'expert', s...  18 us
    dot_general x2, matrix products, weight_sums(): lax.dot_general(rows_x, d_up, (((0,), (0,)), ((), ())), preferred_element...  14.7 us
    ppermute x1, waiting for transfers between devices, local(): other = lax.ppermute(came, 'dp', swap)  11.3 us
    dot_general x2, matrix products, weight_sums(): lax.dot_general(rows_x, d_gate, (((0,), (0,)), ((), ())), preferred_eleme...  9.3 us
    dot_general x2, matrix products, weight_sums(): lax.dot_general(hidden, rows_cot, (((0,), (0,)), ((), ())), preferred_ele...  6.5 us
    dot_general x2, matrix products, front_rows(): lax.dot_general(d_up, up_w, (((1,), (1,)), ((), ())), preferred_element_t...  6.18 us
    all_to_all x1, starting transfers between devices, local(): lax.all_to_all(summed.reshape(owners, capacity, model_width), 'expert', s...  6.09 us
  transfers between devices with their start and end apart: 3, of which 2 were waited for; matrix products, arithmetic and copies ran while one was open for 18% of the time, Pallas kernels for 0%

profile of v2, /device:TPU:1, one launch (start us, length us, event | category | flops | bytes accessed | tf_op | source)
XLA Modules:
  0.0 213.4 jit_solution(2892924238030803572)
XLA Ops:
  0.6 0.0 copy-start.3
  0.6 0.8 fusion.42
  1.5 0.6 reduce-window.6
  2.1 0.2 slice_reduce_fusion
  2.3 0.8 fusion.41
  3.1 0.7 multiply_add_fusion
  3.8 1.9 fusion.30
  5.7 0.0 copy-done.3
  5.7 4.2 %fusion = bf16[64,8,2,3584]{3,1,0,2:T(8,128)(2,1)} fusion(bf16[256,1,3584]{2,0,1:T(8,128)(2,1)S(1)} %fusion.30, bf16[256,1,3584]{2,0,1:T(8,128)(2,1)S(1)} %bitcast.104, s32[256]{0:T(256)S(1)} %multiply_add_fusion), kind=kOutput, calls=%fused_computation.7 | convolution fusion | flops 1890189312 | bytes 11011072 | tf_op jit(solution)/shard_map/pc,cxd->pxd/dot_general | solution.py:146
  9.9 4.1 %copy.13 = bf16[64,8,2,3584]{3,1,2,0:T(8,128)(2,1)S(1)} copy(bf16[64,8,2,3584]{3,1,0,2:T(8,128)(2,1)} %fusion) | data formatting | bytes 14680064 | tf_op jit(solution)/shard_map/reshape | solution.py:148
  14.0 0.0 copy-start.2
  14.0 97.2 %all_to_all.10 = bf16[64,8,2,3584]{3,1,2,0:T(8,128)(2,1)S(1)} all-to-all(bf16[64,8,2,3584]{3,1,2,0:T(8,128)(2,1)S(1)} %copy.13), channel_id=1, replica_groups=mesh['dp'=2,'expert'=64] {'expert'}, dimensions={0} | all-to-all | bytes 14680064 | tf_op jit(solution)/shard_map/all_to_all | solution.py:150
  111.2 3.0 %copy-done = bf16[64,8,2,3584]{3,1,2,0:T(8,128)(2,1)} copy-done((bf16[64,8,2,3584]{3,1,2,0:T(8,128)(2,1)}, bf16[64,8,2,3584]{3,1,2,0:T(8,128)(2,1)S(1)}, u32[]{:S(2)}) %copy-start) | copy-done | bytes 7340056
  114.2 3.3 %collective-permute-start = (bf16[64,8,2,3584]{3,1,2,0:T(8,128)(2,1)S(1)}, bf16[64,8,2,3584]{3,1,2,0:T(8,128)(2,1)S(1)}, u32[]{:S(2)}, u32[]{:S(2)}) collective-permute-start(bf16[64,8,2,3584]{3,1,2,0:T(8,128)(2,1)S(1)} %all_to_all.10), channel_id=1, source_target_pairs={{0,64},{64,0},{1,65},{65,1},{2,66},{66,2},{3,67},{67,3},{4,68},{68... | collective-permute-start | bytes 22020104 | tf_op jit(solution)/shard_map/ppermute | solution.py:152
  117.5 11.3 %collective-permute-done = bf16[64,8,2,3584]{3,1,2,0:T(8,128)(2,1)S(1)} collective-permute-done((bf16[64,8,2,3584]{3,1,2,0:T(8,128)(2,1)S(1)}, bf16[64,8,2,3584]{3,1,2,0:T(8,128)(2,1)S(1)}, u32[]{:S(2)}, u32[]{:S(2)}) %collective-permute-start) | collective-permute-done | bytes 7340064 | tf_op jit(solution)/shard_map/ppermute | solution.py:152
  128.8 0.0 copy-done.2
  128.8 2.1 fusion.11
  130.9 0.0 copy-done.1
  130.9 0.0 copy-start.18
  130.9 0.0 copy-start.16
  130.9 2.1 fusion.18
  132.9 0.0 copy-done.15
  133.0 0.0 copy-done.18
  133.0 0.7 copy-done.16
  133.6 2.4 %multiply_convert_fusion.3 = (bf16[512,512]{1,0:T(8,128)(2,1)S(1)}, bf16[512,512]{1,0:T(8,128)(2,1)S(1)}) fusion(f32[512,512]{1,0:T(8,128)S(1)} %fusion.11, f32[512,512]{1,0:T(8,128)S(1)} %fusion.18, bf16[1,512,3584]{2,1,0:T(8,128)(2,1)S(1)} %copy-done.16, bf16[64,8,2,3584]{3,1,2,0:T(8,128)(2,1)S(1)} %collective-permute-done), kind=kOutput, calls=%fused_computation.46 | convolution fusion | flops 1882456064 | bytes 10485760 | tf_op jit(solution)/shard_map/dot_general | solution.py:13
  136.0 0.0 copy-done.20
  136.1 0.0 copy-start.10
  136.1 0.0 copy-start.4
  136.1 0.0 slice-start
  136.1 2.1 fusion.9
  138.2 0.0 slice-start.1
  138.2 2.2 %add_convert_fusion.4 = bf16[512,3584]{1,0:T(8,128)(2,1)S(1)} fusion(f32[512,3584]{1,0:T(8,128)S(1)} %fusion.9, bf16[512,512]{1,0:T(8,128)(2,1)S(1)} %get-tuple-element.6, bf16[1,3584,512]{2,1,0:T(8,128)(2,1)S(1)} %copy-done.1), kind=kOutput, calls=%fused_computation.5 | convolution fusion | flops 1882718208 | bytes 15204352 | tf_op jit(solution)/shard_map/dot_general | solution.py:23
  140.5 0.6 collective-permute-start.1
  141.1 2.1 fusion.15
  143.2 0.0 copy-start.6
  143.2 0.0 copy-start.17
  143.2 2.1 fusion.21
  145.3 0.3 copy-done.17
  145.6 2.4 %multiply_convert_fusion.5 = (bf16[512,512]{1,0:T(8,128)(2,1)S(1)}, bf16[512,512]{1,0:T(8,128)(2,1)S(1)}) fusion(f32[512,512]{1,0:T(8,128)S(1)} %fusion.15, f32[512,512]{1,0:T(8,128)S(1)} %fusion.21, bf16[1,512,3584]{2,1,0:T(8,128)(2,1)S(1)} %copy-done.17, bf16[64,8,2,3584]{3,1,2,0:T(8,128)(2,1)S(1)} %bitcast.101), kind=kOutput, calls=%fused_computation.50 | convolution fusion | flops 1882456064 | bytes 10485760 | tf_op jit(solution)/shard_map/dot_general | solution.py:13
  148.0 0.0 copy-done.8
  148.0 0.0 copy-start.12
  148.1 2.1 %fusion.13 = f32[512,3584]{1,0:T(8,128)S(1)} fusion(bf16[512,512]{1,0:T(8,128)(2,1)S(1)} %get-tuple-element.5, bf16[1,3584,512]{2,1,0:T(8,128)(2,1)S(1)} %copy-done.2), kind=kOutput, calls=%fused_computation.25 | convolution fusion | flops 1879048192 | bytes 11534336 | tf_op jit(solution)/shard_map/dot_general | solution.py:20
  150.2 0.0 copy-done.12
  150.2 0.0 collective-permute-done.1
  150.2 4.0 %fusion.4 = bf16[64,8,3584]{2,1,0:T(8,128)(2,1)} fusion(bf16[512,3584]{1,0:T(8,128)(2,1)S(1)} %collective-permute-done.1, f32[512,3584]{1,0:T(8,128)S(1)} %fusion.13, bf16[512,512]{1,0:T(8,128)(2,1)S(1)} %get-tuple-element.4, bf16[1,3584,512]{2,1,0:T(8,128)(2,1)S(1)} %copy-done.1), kind=kOutput, calls=%fused_computation.12 | convolution fusion | flops 1890058240 | bytes 18874368 | tf_op jit(solution)/shard_map/dot_general | solution.py:23
  154.2 6.1 %all-to-all-start.1 = ((bf16[64,8,3584]{2,1,0:T(8,128)(2,1)}), bf16[64,8,3584]{2,1,0:T(8,128)(2,1)}, u32[]{:S(2)}, u32[]{:S(2)}) async-start(bf16[64,8,3584]{2,1,0:T(8,128)(2,1)} %fusion.4), calls=%async_computation.1 | async-start | bytes 7340032 | tf_op jit(solution)/shard_map/all_to_all | solution.py:163
  160.3 0.0 slice-start.3
  160.3 0.0 copy-start.13
  160.3 0.0 slice-start.4
  160.3 7.4 %fusion.28 = f32[3584,512]{1,0:T(8,128)} fusion(bf16[512,512]{1,0:T(8,128)(2,1)} %copy-done.14, bf16[64,8,2,3584]{3,1,2,0:T(8,128)(2,1)} %copy-done), kind=kOutput, calls=%fused_computation.41 | convolution fusion | flops 1879048192 | bytes 11534336 | tf_op jit(solution)/shard_map/dot_general | solution.py:33
  167.7 0.0 copy-done.13
  167.7 0.0 copy-start.7
  167.7 0.0 copy-start.9
  167.7 0.0 slice-start.5
  167.8 5.1 %fusion.29 = f32[3584,512]{1,0:T(8,128)} fusion(bf16[512,512]{1,0:T(8,128)(2,1)S(1)} %copy-done.13, bf16[64,8,2,3584]{3,1,2,0:T(8,128)(2,1)S(1)} %bitcast.103), kind=kOutput, calls=%fused_computation.42 | convolution fusion | flops 1879048192 | bytes 11534336 | tf_op jit(solution)/shard_map/dot_general | solution.py:30
  172.9 2.2 %fusion.27 = f32[512,3584]{1,0:T(8,128)S(1)} fusion(bf16[64,8,2,3584]{3,1,2,0:T(8,128)(2,1)S(1)} %bitcast.103, f32[512,512]{1,0:T(8,128)S(1)} %copy-done.9, f32[512,512]{1,0:T(8,128)S(1)} %copy-done.7), kind=kOutput, calls=%fused_computation.40 | convolution fusion | flops 1880621056 | bytes 13107200 | tf_op jit(solution)/shard_map/dot_general | solution.py:36
  175.2 0.0 copy-start.11
  175.2 0.0 slice-start.7
  175.2 7.3 %fusion.2 = bf16[1,3584,512]{2,1,0:T(8,128)(2,1)} fusion(f32[3584,512]{1,0:T(8,128)} %fusion.28, bf16[512,512]{1,0:T(8,128)(2,1)S(1)} %copy-done.5, bf16[64,8,2,3584]{3,1,2,0:T(8,128)(2,1)S(1)} %bitcast.110), kind=kOutput, calls=%fused_computation.9 | convolution fusion | flops 1882718208 | bytes 15204352 | tf_op jit(solution)/shard_map/dot_general | solution.py:33
  182.5 4.2 %fusion.1 = bf16[1,3584,512]{2,1,0:T(8,128)(2,1)} fusion(f32[3584,512]{1,0:T(8,128)S(1)} %bitcast.112, bf16[512,512]{1,0:T(8,128)(2,1)S(1)} %copy-done.11, bf16[64,8,2,3584]{3,1,2,0:T(8,128)(2,1)S(1)} %bitcast.110), kind=kOutput, calls=%fused_computation.8 | convolution fusion | flops 1882718208 | bytes 15204352 | tf_op jit(solution)/shard_map/dot_general | solution.py:30
  186.7 0.0 copy-done.21
  186.7 4.3 %fusion.3 = bf16[1,512,3584]{2,1,0:T(8,128)(2,1)} fusion(f32[512,3584]{1,0:T(8,128)S(1)} %fusion.27, bf16[64,8,2,3584]{3,1,2,0:T(8,128)(2,1)S(1)} %bitcast.110, f32[512,512]{1,0:T(8,128)S(1)} %copy-done.21, f32[512,512]{1,0:T(8,128)S(1)} %copy-done.19), kind=kOutput, calls=%fused_computation.10 | convolution fusion | flops 1884291072 | bytes 16777216 | tf_op jit(solution)/shard_map/dot_general | solution.py:36
  191.0 18.0 %all-to-all-done.1 = bf16[64,8,3584]{2,1,0:T(8,128)(2,1)} async-done(((bf16[64,8,3584]{2,1,0:T(8,128)(2,1)}), bf16[64,8,3584]{2,1,0:T(8,128)(2,1)}, u32[]{:S(2)}, u32[]{:S(2)}) %all-to-all-start.1) | async-done | bytes 3670048 | tf_op jit(solution)/shard_map/all_to_all | solution.py:163
  209.0 4.4 %convolution_convert_fusion.1 = bf16[256,3584]{1,0:T(8,128)(2,1)} fusion(bf16[64,8,3584]{2,1,0:T(8,128)(2,1)} %all-to-all-done.1, s32[256]{0:T(256)S(1)} %multiply_add_fusion), kind=kOutput, calls=%fused_computation.11 | convolution fusion | flops 940572672 | bytes 5506048 | tf_op jit(solution)/shard_map/dot_general | solution.py:169
  (34 shorter events, 0.1 us)
Async XLA Ops:
  0.6 5.1 %copy-start.3 = (bf16[256,3584]{1,0:T(8,128)(2,1)S(1)}, bf16[256,3584]{1,0:T(8,128)(2,1)}, u32[]{:S(2)}) copy-start(bf16[256,3584]{1,0:T(8,128)(2,1)} %param.7) | copy-start | bytes 5505028
  14.0 114.7 %copy-start.2 = (bf16[1,3584,512]{2,1,0:T(8,128)(2,1)S(1)}, bf16[1,3584,512]{2,1,0:T(8,128)(2,1)}, u32[]{:S(2)}) copy-start(bf16[1,3584,512]{2,1,0:T(8,128)(2,1)} %param.11) | copy-start | bytes 11010052
  111.2 3.0 %copy-start = (bf16[64,8,2,3584]{3,1,2,0:T(8,128)(2,1)}, bf16[64,8,2,3584]{3,1,2,0:T(8,128)(2,1)S(1)}, u32[]{:S(2)}) copy-start(bf16[64,8,2,3584]{3,1,2,0:T(8,128)(2,1)S(1)} %all_to_all.10) | copy-start | bytes 22020100
  114.2 16.6 %copy-start.1 = (bf16[1,3584,512]{2,1,0:T(8,128)(2,1)S(1)}, bf16[1,3584,512]{2,1,0:T(8,128)(2,1)}, u32[]{:S(2)}) copy-start(bf16[1,3584,512]{2,1,0:T(8,128)(2,1)} %param.12) | copy-start | bytes 11010052
  114.2 14.5 %collective-permute-start = (bf16[64,8,2,3584]{3,1,2,0:T(8,128)(2,1)S(1)}, bf16[64,8,2,3584]{3,1,2,0:T(8,128)(2,1)S(1)}, u32[]{:S(2)}, u32[]{:S(2)}) collective-permute-start(bf16[64,8,2,3584]{3,1,2,0:T(8,128)(2,1)S(1)} %all_to_all.10), channel_id=1, source_target_pairs={{0,64},{64,0},{1,65},{65,1},{2,66},{66,2},{3,67},{67,3},{4,68},{68... | collective-permute-start | bytes 22020104 | tf_op jit(solution)/shard_map/ppermute | solution.py:152
  128.8 4.2 %copy-start.15 = (bf16[64,8,2,3584]{3,1,2,0:T(8,128)(2,1)}, bf16[64,8,2,3584]{3,1,2,0:T(8,128)(2,1)S(1)}, u32[]{:S(2)}) copy-start(bf16[64,8,2,3584]{3,1,2,0:T(8,128)(2,1)S(1)} %collective-permute-done) | copy-start | bytes 22020100
  130.9 2.1 copy-start.18
  130.9 2.8 %copy-start.16 = (bf16[1,512,3584]{2,1,0:T(8,128)(2,1)S(1)}, bf16[1,512,3584]{2,1,0:T(8,128)(2,1)}, u32[]{:S(2)}) copy-start(bf16[1,512,3584]{2,1,0:T(8,128)(2,1)} %param.13) | copy-start | bytes 11010052
  133.6 2.4 %copy-start.20 = (f32[512,512]{1,0:T(8,128)}, f32[512,512]{1,0:T(8,128)S(1)}, u32[]{:S(2)}) copy-start(f32[512,512]{1,0:T(8,128)S(1)} %fusion.18) | copy-start | bytes 3145732
  136.1 2.1 %copy-start.10 = (bf16[512,512]{1,0:T(8,128)(2,1)}, bf16[512,512]{1,0:T(8,128)(2,1)S(1)}, u32[]{:S(2)}) copy-start(bf16[512,512]{1,0:T(8,128)(2,1)S(1)} %get-tuple-element.7) | copy-start | bytes 1572868
  136.1 2.1 %copy-start.4 = (bf16[512,512]{1,0:T(8,128)(2,1)}, bf16[512,512]{1,0:T(8,128)(2,1)S(1)}, u32[]{:S(2)}) copy-start(bf16[512,512]{1,0:T(8,128)(2,1)S(1)} %get-tuple-element.6) | copy-start | bytes 1572868
  136.1 5.0 %slice-start = ((s8[7340032]{0:T(1024)(128)(4,1)}), s8[4194304]{0:T(1024)(128)(4,1)S(1)}, s32[]{:S(2)}) async-start(s8[7340032]{0:T(1024)(128)(4,1)} %bitcast.100), calls=%async_computation.2 | async-start | bytes 8388608
  138.2 2.9 %slice-start.1 = ((s8[7340032]{0:T(1024)(128)(4,1)}), s8[3145728]{0:T(1024)(128)(4,1)S(1)}, s32[]{:S(2)}) async-start(s8[7340032]{0:T(1024)(128)(4,1)} %bitcast.100), calls=%async_computation.3 | async-start | bytes 6291456
  140.5 9.8 %collective-permute-start.1 = (bf16[512,3584]{1,0:T(8,128)(2,1)S(1)}, bf16[512,3584]{1,0:T(8,128)(2,1)S(1)}, u32[]{:S(2)}, u32[]{:S(2)}) collective-permute-start(bf16[512,3584]{1,0:T(8,128)(2,1)S(1)} %add_convert_fusion.4), channel_id=1, source_target_pairs={{0,64},{64,0},{1,65},{65,1},{2,66},{66,2},{3,67},{67,3},{4,68},{68... | collective-permute-start | bytes 11010056 | tf_op jit(solution)/shard_map/ppermute | solution.py:161
  143.2 2.1 copy-start.6
  143.2 2.4 %copy-start.17 = (bf16[1,512,3584]{2,1,0:T(8,128)(2,1)S(1)}, bf16[1,512,3584]{2,1,0:T(8,128)(2,1)}, u32[]{:S(2)}) copy-start(bf16[1,512,3584]{2,1,0:T(8,128)(2,1)} %param.13) | copy-start | bytes 11010052
  145.6 2.4 %copy-start.8 = (f32[512,512]{1,0:T(8,128)}, f32[512,512]{1,0:T(8,128)S(1)}, u32[]{:S(2)}) copy-start(f32[512,512]{1,0:T(8,128)S(1)} %fusion.21) | copy-start | bytes 3145732
  148.0 2.2 %copy-start.12 = (bf16[512,512]{1,0:T(8,128)(2,1)}, bf16[512,512]{1,0:T(8,128)(2,1)S(1)}, u32[]{:S(2)}) copy-start(bf16[512,512]{1,0:T(8,128)(2,1)S(1)} %get-tuple-element.5) | copy-start | bytes 1572868
  148.1 2.2 %copy-start.14 = (bf16[512,512]{1,0:T(8,128)(2,1)}, bf16[512,512]{1,0:T(8,128)(2,1)S(1)}, u32[]{:S(2)}) copy-start(bf16[512,512]{1,0:T(8,128)(2,1)S(1)} %get-tuple-element.4) | copy-start | bytes 1572868
  154.2 13.5 %slice-start.2 = ((s8[7340032]{0:T(1024)(128)(4,1)}), s8[3145728]{0:T(1024)(128)(4,1)S(1)}, s32[]{:S(2)}) async-start(s8[7340032]{0:T(1024)(128)(4,1)} %bitcast.102), calls=%async_computation.4 | async-start | bytes 6291456
  154.2 54.8 %all-to-all-start.1 = ((bf16[64,8,3584]{2,1,0:T(8,128)(2,1)}), bf16[64,8,3584]{2,1,0:T(8,128)(2,1)}, u32[]{:S(2)}, u32[]{:S(2)}) async-start(bf16[64,8,3584]{2,1,0:T(8,128)(2,1)} %fusion.4), calls=%async_computation.1 | async-start | bytes 7340032 | tf_op jit(solution)/shard_map/all_to_all | solution.py:163
  160.3 7.4 %slice-start.3 = ((s8[7340032]{0:T(1024)(128)(4,1)}), s8[4194304]{0:T(1024)(128)(4,1)S(1)}, s32[]{:S(2)}) async-start(s8[7340032]{0:T(1024)(128)(4,1)} %bitcast.102), calls=%async_computation.5 | async-start | bytes 8388608
  160.3 7.4 %copy-start.13 = (bf16[512,512]{1,0:T(8,128)(2,1)S(1)}, bf16[512,512]{1,0:T(8,128)(2,1)}, u32[]{:S(2)}) copy-start(bf16[512,512]{1,0:T(8,128)(2,1)} %copy-done.12) | copy-start | bytes 1572868
  160.3 14.8 %slice-start.4 = ((s8[7340032]{0:T(1024)(128)(4,1)}), s8[4194304]{0:T(1024)(128)(4,1)S(1)}, s32[]{:S(2)}) async-start(s8[7340032]{0:T(1024)(128)(4,1)} %bitcast.109), calls=%async_computation.6 | async-start | bytes 8388608
  167.7 5.2 %copy-start.7 = (f32[512,512]{1,0:T(8,128)S(1)}, f32[512,512]{1,0:T(8,128)}, u32[]{:S(2)}) copy-start(f32[512,512]{1,0:T(8,128)} %copy-done.6) | copy-start | bytes 3145732
  167.7 5.2 %copy-start.9 = (f32[512,512]{1,0:T(8,128)S(1)}, f32[512,512]{1,0:T(8,128)}, u32[]{:S(2)}) copy-start(f32[512,512]{1,0:T(8,128)} %copy-done.8) | copy-start | bytes 3145732
  167.7 7.4 %slice-start.5 = ((s8[7340032]{0:T(1024)(128)(4,1)}), s8[3145728]{0:T(1024)(128)(4,1)S(1)}, s32[]{:S(2)}) async-start(s8[7340032]{0:T(1024)(128)(4,1)} %bitcast.109), calls=%async_computation.7 | async-start | bytes 6291456
  172.9 2.3 %copy-start.5 = (bf16[512,512]{1,0:T(8,128)(2,1)S(1)}, bf16[512,512]{1,0:T(8,128)(2,1)}, u32[]{:S(2)}) copy-start(bf16[512,512]{1,0:T(8,128)(2,1)} %copy-done.4) | copy-start | bytes 1572868
  172.9 9.6 %slice-start.6 = ((s8[7340032]{0:T(1024)(128)(4,1)}), s8[4194304]{0:T(1024)(128)(4,1)S(1)}, s32[]{:S(2)}) async-start(s8[7340032]{0:T(1024)(128)(4,1)} %bitcast.111), calls=%async_computation.8 | async-start | bytes 8388608
  175.2 7.3 %copy-start.11 = (bf16[512,512]{1,0:T(8,128)(2,1)S(1)}, bf16[512,512]{1,0:T(8,128)(2,1)}, u32[]{:S(2)}) copy-start(bf16[512,512]{1,0:T(8,128)(2,1)} %copy-done.10) | copy-start | bytes 1572868
  175.2 7.3 %slice-start.7 = ((s8[7340032]{0:T(1024)(128)(4,1)}), s8[3145728]{0:T(1024)(128)(4,1)S(1)}, s32[]{:S(2)}) async-start(s8[7340032]{0:T(1024)(128)(4,1)} %bitcast.111), calls=%async_computation.9 | async-start | bytes 6291456
  182.5 4.2 %copy-start.19 = (f32[512,512]{1,0:T(8,128)S(1)}, f32[512,512]{1,0:T(8,128)}, u32[]{:S(2)}) copy-start(f32[512,512]{1,0:T(8,128)} %copy-done.18) | copy-start | bytes 3145732
  182.5 4.2 %copy-start.21 = (f32[512,512]{1,0:T(8,128)S(1)}, f32[512,512]{1,0:T(8,128)}, u32[]{:S(2)}) copy-start(f32[512,512]{1,0:T(8,128)} %copy-done.20) | copy-start | bytes 3145732

commit v3 on v2

v3 whole, which is shorter than its diff:
```python
import jax
import jax.numpy as jnp
from jax import lax
from jax.sharding import PartitionSpec as P


def front_rows(rows_x, rows_cot, gate_w, up_w, down_w):
    gate_pre = jnp.dot(rows_x, gate_w, preferred_element_type=jnp.float32)
    up_pre = jnp.dot(rows_x, up_w, preferred_element_type=jnp.float32)
    sigmoid_gate = jax.nn.sigmoid(gate_pre)
    swish_gate = gate_pre * sigmoid_gate
    hidden = (swish_gate * up_pre).astype(jnp.bfloat16)
    d_hidden = lax.dot_general(
        rows_cot, down_w, (((1,), (1,)), ((), ())), preferred_element_type=jnp.float32
    )
    d_gate = (d_hidden * up_pre * sigmoid_gate * (1.0 + gate_pre * (1.0 - sigmoid_gate))).astype(
        jnp.bfloat16
    )
    d_up = (d_hidden * swish_gate).astype(jnp.bfloat16)
    return (hidden, d_gate, d_up, input_grads(d_gate, d_up, gate_w, up_w))


def input_grads(d_gate, d_up, gate_w, up_w):
    dx_part = lax.dot_general(
        d_gate, gate_w, (((1,), (1,)), ((), ())), preferred_element_type=jnp.float32
    )
    dx_part = dx_part + lax.dot_general(
        d_up, up_w, (((1,), (1,)), ((), ())), preferred_element_type=jnp.float32
    )
    return dx_part.astype(jnp.bfloat16)


def weight_sums(rows_x, rows_cot, hidden, d_gate, d_up):
    grad_gate = lax.dot_general(
        rows_x, d_gate, (((0,), (0,)), ((), ())), preferred_element_type=jnp.float32
    )
    grad_up = lax.dot_general(
        rows_x, d_up, (((0,), (0,)), ((), ())), preferred_element_type=jnp.float32
    )
    grad_down = lax.dot_general(
        hidden, rows_cot, (((0,), (0,)), ((), ())), preferred_element_type=jnp.float32
    )
    return (grad_gate, grad_up, grad_down)


def local(tokens, cotangent, expert_ids, gate_probs, w_gate, w_up, w_down):
    owners = lax.axis_size("expert")
    tok_rows = tokens.shape[0]
    model_width = tokens.shape[1]
    fanout = expert_ids.shape[1]
    capacity = max(2, 2 * tok_rows * fanout // owners)
    copies = tok_rows * fanout
    flat_ids = expert_ids.reshape(copies)
    onehot = (flat_ids[:, None] == jnp.arange(owners, dtype=jnp.int32)[None, :]).astype(jnp.int32)
    before = jnp.cumsum(onehot, axis=0) - onehot
    slot_rank = jnp.sum(before * onehot, axis=1)
    position = flat_ids * capacity + slot_rank
    copy_rows = tokens[:, None, :].reshape(copies, model_width)
    copy_tok_cot = cotangent[:, None, :].reshape(copies, model_width)
    copy_cots = (gate_probs * copy_tok_cot.astype(jnp.float32)).astype(jnp.bfloat16)
    placing = (jnp.arange(owners * capacity, dtype=jnp.int32)[:, None] == position[None, :]).astype(
        jnp.bfloat16
    )
    joined = jnp.concatenate([copy_rows, copy_cots], axis=1)
    sent = (
        jnp.dot(placing, joined, preferred_element_type=jnp.float32)
        .astype(jnp.bfloat16)
        .reshape(owners, capacity, 2 * model_width)
    )
    came = lax.all_to_all(sent, "expert", split_axis=0, concat_axis=0, tiled=True)
    swap = [(0, 1), (1, 0)]
    other = lax.ppermute(came, "dp", swap)
    half_slots = owners * capacity
    weights_own = (w_gate[0], w_up[0], w_down[0])
    came = came.reshape(half_slots, 2 * model_width)
    own_x = came[:, :model_width]
    own_cot = came[:, model_width:]
    own_h, own_dg, own_du = front_rows(own_x, own_cot, *weights_own)[:3]
    other = other.reshape(half_slots, 2 * model_width)
    oth_x = other[:, :model_width]
    oth_cot = other[:, model_width:]
    oth_h, oth_dg, oth_du, oth_dx = front_rows(oth_x, oth_cot, *weights_own)
    back = lax.ppermute(oth_dx, "dp", swap)
    own_dx = lax.optimization_barrier(input_grads(own_dg, own_du, weights_own[0], weights_own[1]))
    summed = (own_dx.astype(jnp.float32) + back.astype(jnp.float32)).astype(jnp.bfloat16)
    returned = lax.all_to_all(
        summed.reshape(owners, capacity, model_width), "expert", split_axis=0, concat_axis=0, tiled=True
    )
    sums_own = weight_sums(own_x, own_cot, own_h, own_dg, own_du)
    sums_oth = weight_sums(oth_x, oth_cot, oth_h, oth_dg, oth_du)
    grad_gate, grad_up, grad_down = (a + b for a, b in zip(sums_own, sums_oth))
    copy_grad = lax.dot_general(
        placing,
        returned.reshape(owners * capacity, model_width),
        (((0,), (0,)), ((), ())),
        preferred_element_type=jnp.float32,
    )
    grad_tokens = jnp.sum(copy_grad.reshape(tok_rows, fanout, model_width), axis=1).astype(
        jnp.bfloat16
    )
    return (
        grad_tokens,
        grad_gate.astype(jnp.bfloat16)[None],
        grad_up.astype(jnp.bfloat16)[None],
        grad_down.astype(jnp.bfloat16)[None],
    )


def solution(mesh):
    return jax.shard_map(
        local,
        mesh=mesh,
        in_specs=(
            P(("dp", "expert"), None),
            P(("dp", "expert"), None),
            P(("dp", "expert"), None),
            P(("dp", "expert"), None),
            P("expert", None, "dp"),
            P("expert", None, "dp"),
            P("expert", "dp", None),
        ),
        out_specs=(
            P(("dp", "expert"), None),
            P("expert", None, "dp"),
            P("expert", None, "dp"),
            P("expert", "dp", None),
        ),
        check_vma=False,
    )
```

time: 214 us -> 208 us (0.972)
  local copies, waits for them, and re-layouts: 8.47 us -> 3.61 us
  matrix products: 62.6 us -> 58.8 us
  other arithmetic: 4.89 us -> 7.6 us
    reshape x1 -> x0, local copies, waits for them, and re-layouts: 4.14 us -> none  [local(): sent = jnp.einsum('pc,cxd->pxd', placing, stacked, preferred_element_type...]
    dot_general x5, matrix products: 14.6 us -> 10.9 us  [the longest x2 4.21 us: input_grads(): lax.dot_general(d_up, up_w, (((1,), (1,)), ((), ())), preferred_element_t...]
    reshape x0 -> x1, other arithmetic: none -> 2.72 us  [local(): summed.reshape(owners, capacity, model_width)]
  transfers between devices with their start and end apart: 3 -> 3, of which waited for: 2 -> 2; matrix products, arithmetic and copies ran while one was open for 18% -> 20% of each run, Pallas kernels for 0% -> 0%
where the time goes in v3:
time: 208 us; the launch traced here: 207 us
  blocking collectives  97.2 us (47%)
  matrix products  58.8 us (28%)
  waiting for transfers between devices  29.2 us (14%)
  starting transfers between devices  9.97 us (5%)
  other arithmetic  7.6 us (4%)
  local copies, waits for them, and re-layouts  3.61 us (2%)
    all_to_all x1, blocking collectives, local(): lax.all_to_all(sent, 'expert', split_axis=0, concat_axis=0, tiled=True)  97.2 us
    all_to_all x1, waiting for transfers between devices, local(): lax.all_to_all(summed.reshape(owners, capacity, model_width), 'expert', s...  17.9 us
    dot_general x2, matrix products, weight_sums(): lax.dot_general(rows_x, d_up, (((0,), (0,)), ((), ())), preferred_element...  14.7 us
    ppermute x1, waiting for transfers between devices, local(): other = lax.ppermute(came, 'dp', swap)  11.3 us
    dot_general x2, matrix products, weight_sums(): lax.dot_general(rows_x, d_gate, (((0,), (0,)), ((), ())), preferred_eleme...  9.32 us
    dot_general x2, matrix products, weight_sums(): lax.dot_general(hidden, rows_cot, (((0,), (0,)), ((), ())), preferred_ele...  6.49 us
    all_to_all x1, starting transfers between devices, local(): lax.all_to_all(summed.reshape(owners, capacity, model_width), 'expert', s...  6.09 us
    dot_general x2, matrix products, front_rows(): lax.dot_general(rows_cot, down_w, (((1,), (1,)), ((), ())), preferred_ele...  4.78 us
  transfers between devices with their start and end apart: 3, of which 2 were waited for; matrix products, arithmetic and copies ran while one was open for 20% of the time, Pallas kernels for 0%

profile of v3, /device:TPU:1, one launch (start us, length us, event | category | flops | bytes accessed | tf_op | source)
XLA Modules:
  0.0 207.5 jit_solution(10837792788480327274)
XLA Ops:
  0.6 0.0 copy-start.3
  0.6 0.8 fusion.51
  1.5 0.6 reduce-window.6
  2.1 0.2 slice_reduce_fusion
  2.3 0.8 fusion.50
  3.1 0.7 multiply_add_fusion
  3.8 1.9 multiply_convert_fusion
  5.7 0.0 copy-done.3
  5.7 2.5 %fusion = bf16[64,8,7168]{2,1,0:T(8,128)(2,1)S(1)} fusion(bf16[256,3584]{1,0:T(8,128)(2,1)S(1)} %multiply_convert_fusion, bf16[256,3584]{1,0:T(8,128)(2,1)S(1)} %copy-done.3, s32[256]{0:T(256)S(1)} %multiply_add_fusion), kind=kOutput, calls=%fused_computation.1 | convolution fusion | flops 1890189312 | bytes 11011072 | tf_op jit(solution)/shard_map/dot_general | solution.py:66
  8.2 0.0 copy-start.2
  8.3 97.2 %all_to_all.10 = bf16[64,8,7168]{2,1,0:T(8,128)(2,1)S(1)} all-to-all(bf16[64,8,7168]{2,1,0:T(8,128)(2,1)S(1)} %fusion), channel_id=1, replica_groups=mesh['dp'=2,'expert'=64] {'expert'}, dimensions={0} | all-to-all | bytes 14680064 | tf_op jit(solution)/shard_map/all_to_all | solution.py:70
  105.5 3.3 %collective-permute-start = (bf16[64,8,7168]{2,1,0:T(8,128)(2,1)S(1)}, bf16[64,8,7168]{2,1,0:T(8,128)(2,1)S(1)}, u32[]{:S(2)}, u32[]{:S(2)}) collective-permute-start(bf16[64,8,7168]{2,1,0:T(8,128)(2,1)S(1)} %all_to_all.10), channel_id=1, source_target_pairs={{0,64},{64,0},{1,65},{65,1},{2,66},{66,2},{3,67},{67,3},{4,68},{68... | collective-permute-start | bytes 22020104 | tf_op jit(solution)/shard_map/ppermute | solution.py:72
  108.7 11.3 %collective-permute-done = bf16[64,8,7168]{2,1,0:T(8,128)(2,1)S(1)} collective-permute-done((bf16[64,8,7168]{2,1,0:T(8,128)(2,1)S(1)}, bf16[64,8,7168]{2,1,0:T(8,128)(2,1)S(1)}, u32[]{:S(2)}, u32[]{:S(2)}) %collective-permute-start) | collective-permute-done | bytes 7340064 | tf_op jit(solution)/shard_map/ppermute | solution.py:72
  120.0 0.0 copy-done.2
  120.0 2.1 fusion.11
  122.1 2.6 %copy-done.1 = bf16[1,3584,512]{2,1,0:T(8,128)(2,1)S(1)} copy-done((bf16[1,3584,512]{2,1,0:T(8,128)(2,1)S(1)}, bf16[1,3584,512]{2,1,0:T(8,128)(2,1)}, u32[]{:S(2)}) %copy-start.1) | copy-done | bytes 3670040
  124.7 2.1 fusion.18
  126.8 0.0 copy-done.15
  126.8 0.0 copy-done.18
  126.8 0.3 copy-done.16
  127.1 2.4 %multiply_convert_fusion.3 = (bf16[512,512]{1,0:T(8,128)(2,1)S(1)}, bf16[512,512]{1,0:T(8,128)(2,1)S(1)}) fusion(f32[512,512]{1,0:T(8,128)S(1)} %fusion.11, f32[512,512]{1,0:T(8,128)S(1)} %fusion.18, bf16[1,512,3584]{2,1,0:T(8,128)(2,1)S(1)} %copy-done.16, bf16[512,7168]{1,0:T(8,128)(2,1)S(1)} %bitcast.86), kind=kOutput, calls=%fused_computation.53 | convolution fusion | flops 1882456064 | bytes 10485760 | tf_op jit(solution)/shard_map/dot_general | solution.py:13
  129.5 0.0 copy-done.20
  129.5 0.0 copy-start.11
  129.5 0.0 copy-start.4
  129.6 2.1 %fusion.9 = f32[512,3584]{1,0:T(8,128)S(1)} fusion(bf16[512,512]{1,0:T(8,128)(2,1)S(1)} %get-tuple-element.7, bf16[1,3584,512]{2,1,0:T(8,128)(2,1)S(1)} %copy-done.2), kind=kOutput, calls=%fused_computation.17 | convolution fusion | flops 1879048192 | bytes 11534336 | tf_op jit(solution)/shard_map/dot_general | solution.py:24
  131.7 0.0 copy-done.11
  131.7 0.0 copy-done.4
  131.7 2.1 %add_convert_fusion.4 = bf16[512,3584]{1,0:T(8,128)(2,1)S(1)} fusion(f32[512,3584]{1,0:T(8,128)S(1)} %fusion.9, bf16[512,512]{1,0:T(8,128)(2,1)S(1)} %get-tuple-element.6, bf16[1,3584,512]{2,1,0:T(8,128)(2,1)S(1)} %copy-done.1), kind=kOutput, calls=%fused_computation.6 | convolution fusion | flops 1882718208 | bytes 15204352 | tf_op jit(solution)/shard_map/dot_general | solution.py:27
  133.8 0.6 collective-permute-start.1
  134.4 2.1 fusion.15
  136.5 0.0 copy-start.7
  136.5 0.0 copy-start.17
  136.5 2.1 fusion.21
  138.6 0.0 copy-done
  138.6 0.0 copy-done.7
  138.6 0.3 copy-done.17
  138.9 2.4 %multiply_convert_fusion.5 = (bf16[512,512]{1,0:T(8,128)(2,1)S(1)}, bf16[512,512]{1,0:T(8,128)(2,1)S(1)}) fusion(f32[512,512]{1,0:T(8,128)S(1)} %fusion.15, f32[512,512]{1,0:T(8,128)S(1)} %fusion.21, bf16[1,512,3584]{2,1,0:T(8,128)(2,1)S(1)} %copy-done.17, bf16[512,7168]{1,0:T(8,128)(2,1)S(1)} %bitcast.74), kind=kOutput, calls=%fused_computation.57 | convolution fusion | flops 1882456064 | bytes 10485760 | tf_op jit(solution)/shard_map/dot_general | solution.py:13
  141.3 0.0 copy-done.9
  141.3 0.0 copy-start.13
  141.3 0.0 copy-start.6
  141.3 2.1 %fusion.13 = f32[512,3584]{1,0:T(8,128)S(1)} fusion(bf16[512,512]{1,0:T(8,128)(2,1)S(1)} %get-tuple-element.5, bf16[1,3584,512]{2,1,0:T(8,128)(2,1)S(1)} %copy-done.2), kind=kOutput, calls=%fused_computation.21 | convolution fusion | flops 1879048192 | bytes 11534336 | tf_op jit(solution)/shard_map/dot_general | solution.py:24
  143.5 2.1 %add_convert_fusion.5 = bf16[512,3584]{1,0:T(8,128)(2,1)S(1)} fusion(f32[512,3584]{1,0:T(8,128)S(1)} %fusion.13, bf16[512,512]{1,0:T(8,128)(2,1)S(1)} %get-tuple-element.4, bf16[1,3584,512]{2,1,0:T(8,128)(2,1)S(1)} %copy-done.1), kind=kOutput, calls=%fused_computation.7 | convolution fusion | flops 1882718208 | bytes 15204352 | tf_op jit(solution)/shard_map/dot_general | solution.py:27
  145.6 0.0 collective-permute-done.1
  145.6 2.7 %fusion.4 = bf16[64,8,3584]{2,1,0:T(8,128)(2,1)} fusion(bf16[512,3584]{1,0:T(8,128)(2,1)S(1)} %collective-permute-done.1, bf16[512,3584]{1,0:T(8,128)(2,1)S(1)} %add_convert_fusion.5), kind=kLoop, calls=%fused_computation.12 | loop fusion | flops 7340032 | bytes 11010048 | tf_op jit(solution)/shard_map/reshape | solution.py:87
  148.3 6.1 %all-to-all-start.1 = ((bf16[64,8,3584]{2,1,0:T(8,128)(2,1)}), bf16[64,8,3584]{2,1,0:T(8,128)(2,1)}, u32[]{:S(2)}, u32[]{:S(2)}) async-start(bf16[64,8,3584]{2,1,0:T(8,128)(2,1)} %fusion.4), calls=%async_computation.1 | async-start | bytes 7340032 | tf_op jit(solution)/shard_map/all_to_all | solution.py:86
  154.4 0.0 slice-start.1
  154.4 0.0 copy-start.14
  154.4 0.0 slice-start.2
  154.4 7.4 %fusion.36 = f32[3584,512]{1,0:T(8,128)} fusion(bf16[512,512]{1,0:T(8,128)(2,1)} %copy-done.6, bf16[512,7168]{1,0:T(8,128)(2,1)} %bitcast.75), kind=kOutput, calls=%fused_computation.45 | convolution fusion | flops 1879048192 | bytes 11534336 | tf_op jit(solution)/shard_map/dot_general | solution.py:37
  161.8 0.0 slice-done.1
  161.8 0.0 copy-start.8
  161.8 0.0 copy-start.10
  161.8 0.0 slice-start.3
  161.8 5.1 %fusion.38 = f32[3584,512]{1,0:T(8,128)} fusion(bf16[512,512]{1,0:T(8,128)(2,1)S(1)} %copy-done.14, bf16[512,7168]{1,0:T(8,128)(2,1)S(1)} %bitcast.78), kind=kOutput, calls=%fused_computation.47 | convolution fusion | flops 1879048192 | bytes 11534336 | tf_op jit(solution)/shard_map/dot_general | solution.py:34
  167.0 0.0 copy-done.8
  167.0 2.2 %fusion.29 = f32[512,3584]{1,0:T(8,128)S(1)} fusion(bf16[512,7168]{1,0:T(8,128)(2,1)S(1)} %bitcast.79, f32[512,512]{1,0:T(8,128)S(1)} %copy-done.10, f32[512,512]{1,0:T(8,128)S(1)} %copy-done.8), kind=kOutput, calls=%fused_computation.38 | convolution fusion | flops 1880621056 | bytes 13107200 | tf_op jit(solution)/shard_map/dot_general | solution.py:40
  169.3 0.0 copy-start.12
  169.3 0.0 slice-start.5
  169.3 7.3 %fusion.2 = bf16[1,3584,512]{2,1,0:T(8,128)(2,1)} fusion(f32[3584,512]{1,0:T(8,128)} %fusion.36, bf16[512,512]{1,0:T(8,128)(2,1)S(1)} %copy-done.5, bf16[512,7168]{1,0:T(8,128)(2,1)S(1)} %bitcast.89), kind=kOutput, calls=%fused_computation.9 | convolution fusion | flops 1882718208 | bytes 15204352 | tf_op jit(solution)/shard_map/dot_general | solution.py:37
  176.7 4.2 %fusion.1 = bf16[1,3584,512]{2,1,0:T(8,128)(2,1)} fusion(f32[3584,512]{1,0:T(8,128)S(1)} %bitcast.93, bf16[512,512]{1,0:T(8,128)(2,1)S(1)} %copy-done.12, bf16[512,7168]{1,0:T(8,128)(2,1)S(1)} %bitcast.90), kind=kOutput, calls=%fused_computation.8 | convolution fusion | flops 1882718208 | bytes 15204352 | tf_op jit(solution)/shard_map/dot_general | solution.py:34
  180.8 0.0 copy-done.21
  180.8 4.3 %fusion.3 = bf16[1,512,3584]{2,1,0:T(8,128)(2,1)} fusion(f32[512,3584]{1,0:T(8,128)S(1)} %fusion.29, bf16[512,7168]{1,0:T(8,128)(2,1)S(1)} %bitcast.91, f32[512,512]{1,0:T(8,128)S(1)} %copy-done.21, f32[512,512]{1,0:T(8,128)S(1)} %copy-done.19), kind=kOutput, calls=%fused_computation.10 | convolution fusion | flops 1884291072 | bytes 16777216 | tf_op jit(solution)/shard_map/dot_general | solution.py:40
  185.1 17.9 %all-to-all-done.1 = bf16[64,8,3584]{2,1,0:T(8,128)(2,1)} async-done(((bf16[64,8,3584]{2,1,0:T(8,128)(2,1)}), bf16[64,8,3584]{2,1,0:T(8,128)(2,1)}, u32[]{:S(2)}, u32[]{:S(2)}) %all-to-all-start.1) | async-done | bytes 3670048 | tf_op jit(solution)/shard_map/all_to_all | solution.py:86
  203.0 4.4 %convolution_convert_fusion.1 = bf16[256,3584]{1,0:T(8,128)(2,1)} fusion(bf16[64,8,3584]{2,1,0:T(8,128)(2,1)} %all-to-all-done.1, s32[256]{0:T(256)S(1)} %multiply_add_fusion), kind=kOutput, calls=%fused_computation.11 | convolution fusion | flops 940572672 | bytes 5506048 | tf_op jit(solution)/shard_map/dot_general | solution.py:92
  (29 shorter events, 0.1 us)
Async XLA Ops:
  0.6 5.1 %copy-start.3 = (bf16[256,3584]{1,0:T(8,128)(2,1)S(1)}, bf16[256,3584]{1,0:T(8,128)(2,1)}, u32[]{:S(2)}) copy-start(bf16[256,3584]{1,0:T(8,128)(2,1)} %param.7) | copy-start | bytes 5505028
  8.2 111.8 %copy-start.2 = (bf16[1,3584,512]{2,1,0:T(8,128)(2,1)S(1)}, bf16[1,3584,512]{2,1,0:T(8,128)(2,1)}, u32[]{:S(2)}) copy-start(bf16[1,3584,512]{2,1,0:T(8,128)(2,1)} %param.11) | copy-start | bytes 11010052
  105.5 33.1 %copy-start = (bf16[64,8,7168]{2,1,0:T(8,128)(2,1)}, bf16[64,8,7168]{2,1,0:T(8,128)(2,1)S(1)}, u32[]{:S(2)}) copy-start(bf16[64,8,7168]{2,1,0:T(8,128)(2,1)S(1)} %all_to_all.10) | copy-start | bytes 22020100
  105.5 14.5 %collective-permute-start = (bf16[64,8,7168]{2,1,0:T(8,128)(2,1)S(1)}, bf16[64,8,7168]{2,1,0:T(8,128)(2,1)S(1)}, u32[]{:S(2)}, u32[]{:S(2)}) collective-permute-start(bf16[64,8,7168]{2,1,0:T(8,128)(2,1)S(1)} %all_to_all.10), channel_id=1, source_target_pairs={{0,64},{64,0},{1,65},{65,1},{2,66},{66,2},{3,67},{67,3},{4,68},{68... | collective-permute-start | bytes 22020104 | tf_op jit(solution)/shard_map/ppermute | solution.py:72
  120.0 6.8 %copy-start.15 = (bf16[64,8,7168]{2,1,0:T(8,128)(2,1)}, bf16[64,8,7168]{2,1,0:T(8,128)(2,1)S(1)}, u32[]{:S(2)}) copy-start(bf16[64,8,7168]{2,1,0:T(8,128)(2,1)S(1)} %collective-permute-done) | copy-start | bytes 22020100
  120.0 4.7 %copy-start.1 = (bf16[1,3584,512]{2,1,0:T(8,128)(2,1)S(1)}, bf16[1,3584,512]{2,1,0:T(8,128)(2,1)}, u32[]{:S(2)}) copy-start(bf16[1,3584,512]{2,1,0:T(8,128)(2,1)} %param.12) | copy-start | bytes 11010052
  124.7 2.1 %copy-start.18 = (f32[512,512]{1,0:T(8,128)}, f32[512,512]{1,0:T(8,128)S(1)}, u32[]{:S(2)}) copy-start(f32[512,512]{1,0:T(8,128)S(1)} %fusion.11) | copy-start | bytes 3145732
  124.7 2.4 %copy-start.16 = (bf16[1,512,3584]{2,1,0:T(8,128)(2,1)S(1)}, bf16[1,512,3584]{2,1,0:T(8,128)(2,1)}, u32[]{:S(2)}) copy-start(bf16[1,512,3584]{2,1,0:T(8,128)(2,1)} %param.13) | copy-start | bytes 11010052
  127.1 2.4 %copy-start.20 = (f32[512,512]{1,0:T(8,128)}, f32[512,512]{1,0:T(8,128)S(1)}, u32[]{:S(2)}) copy-start(f32[512,512]{1,0:T(8,128)S(1)} %fusion.18) | copy-start | bytes 3145732
  129.5 2.1 %copy-start.11 = (bf16[512,512]{1,0:T(8,128)(2,1)}, bf16[512,512]{1,0:T(8,128)(2,1)S(1)}, u32[]{:S(2)}) copy-start(bf16[512,512]{1,0:T(8,128)(2,1)S(1)} %get-tuple-element.7) | copy-start | bytes 1572868
  129.5 2.1 %copy-start.4 = (bf16[512,512]{1,0:T(8,128)(2,1)}, bf16[512,512]{1,0:T(8,128)(2,1)S(1)}, u32[]{:S(2)}) copy-start(bf16[512,512]{1,0:T(8,128)(2,1)S(1)} %get-tuple-element.6) | copy-start | bytes 1572868
  133.8 11.8 %collective-permute-start.1 = (bf16[512,3584]{1,0:T(8,128)(2,1)S(1)}, bf16[512,3584]{1,0:T(8,128)(2,1)S(1)}, u32[]{:S(2)}, u32[]{:S(2)}) collective-permute-start(bf16[512,3584]{1,0:T(8,128)(2,1)S(1)} %add_convert_fusion.4), channel_id=1, source_target_pairs={{0,64},{64,0},{1,65},{65,1},{2,66},{66,2},{3,67},{67,3},{4,68},{68... | collective-permute-start | bytes 11010056 | tf_op jit(solution)/shard_map/ppermute | solution.py:83
  136.5 2.1 %copy-start.7 = (f32[512,512]{1,0:T(8,128)}, f32[512,512]{1,0:T(8,128)S(1)}, u32[]{:S(2)}) copy-start(f32[512,512]{1,0:T(8,128)S(1)} %fusion.15) | copy-start | bytes 3145732
  136.5 2.4 %copy-start.17 = (bf16[1,512,3584]{2,1,0:T(8,128)(2,1)S(1)}, bf16[1,512,3584]{2,1,0:T(8,128)(2,1)}, u32[]{:S(2)}) copy-start(bf16[1,512,3584]{2,1,0:T(8,128)(2,1)} %param.13) | copy-start | bytes 11010052
  138.9 2.4 %copy-start.9 = (f32[512,512]{1,0:T(8,128)}, f32[512,512]{1,0:T(8,128)S(1)}, u32[]{:S(2)}) copy-start(f32[512,512]{1,0:T(8,128)S(1)} %fusion.21) | copy-start | bytes 3145732
  141.3 2.1 %copy-start.13 = (bf16[512,512]{1,0:T(8,128)(2,1)}, bf16[512,512]{1,0:T(8,128)(2,1)S(1)}, u32[]{:S(2)}) copy-start(bf16[512,512]{1,0:T(8,128)(2,1)S(1)} %get-tuple-element.5) | copy-start | bytes 1572868
  141.3 2.1 %copy-start.6 = (bf16[512,512]{1,0:T(8,128)(2,1)}, bf16[512,512]{1,0:T(8,128)(2,1)S(1)}, u32[]{:S(2)}) copy-start(bf16[512,512]{1,0:T(8,128)(2,1)S(1)} %get-tuple-element.4) | copy-start | bytes 1572868
  148.3 13.5 %slice-start = ((s8[7340032]{0:T(1024)(128)(4,1)}), s8[3145728]{0:T(1024)(128)(4,1)S(1)}, s32[]{:S(2)}) async-start(s8[7340032]{0:T(1024)(128)(4,1)} %bitcast.76), calls=%async_computation.2 | async-start | bytes 6291456
  148.3 54.7 %all-to-all-start.1 = ((bf16[64,8,3584]{2,1,0:T(8,128)(2,1)}), bf16[64,8,3584]{2,1,0:T(8,128)(2,1)}, u32[]{:S(2)}, u32[]{:S(2)}) async-start(bf16[64,8,3584]{2,1,0:T(8,128)(2,1)} %fusion.4), calls=%async_computation.1 | async-start | bytes 7340032 | tf_op jit(solution)/shard_map/all_to_all | solution.py:86
  154.4 7.4 %slice-start.1 = ((s8[7340032]{0:T(1024)(128)(4,1)}), s8[4194304]{0:T(1024)(128)(4,1)S(1)}, s32[]{:S(2)}) async-start(s8[7340032]{0:T(1024)(128)(4,1)} %bitcast.76), calls=%async_computation.3 | async-start | bytes 8388608
  154.4 7.4 %copy-start.14 = (bf16[512,512]{1,0:T(8,128)(2,1)S(1)}, bf16[512,512]{1,0:T(8,128)(2,1)}, u32[]{:S(2)}) copy-start(bf16[512,512]{1,0:T(8,128)(2,1)} %copy-done.13) | copy-start | bytes 1572868
  154.4 14.8 %slice-start.2 = ((s8[7340032]{0:T(1024)(128)(4,1)}), s8[4194304]{0:T(1024)(128)(4,1)S(1)}, s32[]{:S(2)}) async-start(s8[7340032]{0:T(1024)(128)(4,1)} %bitcast.87), calls=%async_computation.4 | async-start | bytes 8388608
  161.8 5.2 %copy-start.8 = (f32[512,512]{1,0:T(8,128)S(1)}, f32[512,512]{1,0:T(8,128)}, u32[]{:S(2)}) copy-start(f32[512,512]{1,0:T(8,128)} %copy-done.7) | copy-start | bytes 3145732
  161.8 5.2 %copy-start.10 = (f32[512,512]{1,0:T(8,128)S(1)}, f32[512,512]{1,0:T(8,128)}, u32[]{:S(2)}) copy-start(f32[512,512]{1,0:T(8,128)} %copy-done.9) | copy-start | bytes 3145732
  161.8 7.4 %slice-start.3 = ((s8[7340032]{0:T(1024)(128)(4,1)}), s8[3145728]{0:T(1024)(128)(4,1)S(1)}, s32[]{:S(2)}) async-start(s8[7340032]{0:T(1024)(128)(4,1)} %bitcast.87), calls=%async_computation.5 | async-start | bytes 6291456
  167.0 2.3 %copy-start.5 = (bf16[512,512]{1,0:T(8,128)(2,1)S(1)}, bf16[512,512]{1,0:T(8,128)(2,1)}, u32[]{:S(2)}) copy-start(bf16[512,512]{1,0:T(8,128)(2,1)} %copy-done.4) | copy-start | bytes 1572868
  167.0 9.6 %slice-start.4 = ((s8[7340032]{0:T(1024)(128)(4,1)}), s8[4194304]{0:T(1024)(128)(4,1)S(1)}, s32[]{:S(2)}) async-start(s8[7340032]{0:T(1024)(128)(4,1)} %bitcast.92), calls=%async_computation.6 | async-start | bytes 8388608
  169.3 7.3 %copy-start.12 = (bf16[512,512]{1,0:T(8,128)(2,1)S(1)}, bf16[512,512]{1,0:T(8,128)(2,1)}, u32[]{:S(2)}) copy-start(bf16[512,512]{1,0:T(8,128)(2,1)} %copy-done.11) | copy-start | bytes 1572868
  169.3 7.3 %slice-start.5 = ((s8[7340032]{0:T(1024)(128)(4,1)}), s8[3145728]{0:T(1024)(128)(4,1)S(1)}, s32[]{:S(2)}) async-start(s8[7340032]{0:T(1024)(128)(4,1)} %bitcast.92), calls=%async_computation.7 | async-start | bytes 6291456
  176.6 4.2 %copy-start.19 = (f32[512,512]{1,0:T(8,128)S(1)}, f32[512,512]{1,0:T(8,128)}, u32[]{:S(2)}) copy-start(f32[512,512]{1,0:T(8,128)} %copy-done.18) | copy-start | bytes 3145732
  176.7 4.2 %copy-start.21 = (f32[512,512]{1,0:T(8,128)S(1)}, f32[512,512]{1,0:T(8,128)}, u32[]{:S(2)}) copy-start(f32[512,512]{1,0:T(8,128)} %copy-done.20) | copy-start | bytes 3145732

commit v4 on v3

--- a/solution.py
+++ b/solution.py
@@ -81,8 +81,13 @@
     oth_cot = other[:, model_width:]
     oth_h, oth_dg, oth_du, oth_dx = front_rows(oth_x, oth_cot, *weights_own)
     back = lax.ppermute(oth_dx, "dp", swap)
-    own_dx = lax.optimization_barrier(input_grads(own_dg, own_du, weights_own[0], weights_own[1]))
-    summed = (own_dx.astype(jnp.float32) + back.astype(jnp.float32)).astype(jnp.bfloat16)
+    own_dx = lax.dot_general(
+        own_dg, weights_own[0], (((1,), (1,)), ((), ())), preferred_element_type=jnp.float32
+    )
+    own_dx = own_dx + lax.dot_general(
+        own_du, weights_own[1], (((1,), (1,)), ((), ())), preferred_element_type=jnp.float32
+    )
+    summed = (own_dx + back.astype(jnp.float32)).astype(jnp.bfloat16)
     returned = lax.all_to_all(
         summed.reshape(owners, capacity, model_width), "expert", split_axis=0, concat_axis=0, tiled=True
     )

time: 208 us -> 207 us (level)
  other arithmetic: 7.6 us -> 4.89 us
  matrix products: 58.8 us -> 60.9 us
    dot_general x0 -> x2, matrix products: none -> 6.09 us  [the longest x1 3.94 us: local(): lax.dot_general(own_du, weights_own[1], (((1,), (1,)), ((), ())), preferr...]
    reshape x1 -> x0, other arithmetic: 2.72 us -> none  [local(): summed.reshape(owners, capacity, model_width)]
    dot_general x2 -> x1, matrix products: 4.2 us -> 2.1 us  [input_grads(): lax.dot_general(d_gate, gate_w, (((1,), (1,)), ((), ())), preferred_eleme...]
    dot_general x2 -> x1, matrix products: 4.21 us -> 2.22 us  [input_grads(): lax.dot_general(d_up, up_w, (((1,), (1,)), ((), ())), preferred_element_t...]
  transfers between devices with their start and end apart: 3 -> 3, of which waited for: 2 -> 2; matrix products, arithmetic and copies ran while one was open for 20% -> 19% of each run, Pallas kernels for 0% -> 0%
where the time goes in v4:
time: 207 us
  blocking collectives  97.2 us (47%)
  matrix products  60.9 us (29%)
  waiting for transfers between devices  29.2 us (14%)
  starting transfers between devices  9.98 us (5%)
  other arithmetic  4.89 us (2%)
  local copies, waits for them, and re-layouts  3.58 us (2%)
    all_to_all x1, blocking collectives, local(): lax.all_to_all(sent, 'expert', split_axis=0, concat_axis=0, tiled=True)  97.2 us
    all_to_all x1, waiting for transfers between devices, local(): lax.all_to_all(summed.reshape(owners, capacity, model_width), 'expert', s...  17.9 us
    dot_general x2, matrix products, weight_sums(): lax.dot_general(rows_x, d_up, (((0,), (0,)), ((), ())), preferred_element...  14.7 us
    ppermute x1, waiting for transfers between devices, local(): other = lax.ppermute(came, 'dp', swap)  11.3 us
    dot_general x2, matrix products, weight_sums(): lax.dot_general(rows_x, d_gate, (((0,), (0,)), ((), ())), preferred_eleme...  9.32 us
    dot_general x2, matrix products, weight_sums(): lax.dot_general(hidden, rows_cot, (((0,), (0,)), ((), ())), preferred_ele...  6.5 us
    all_to_all x1, starting transfers between devices, local(): lax.all_to_all(summed.reshape(owners, capacity, model_width), 'expert', s...  6.09 us
    dot_general x2, matrix products, front_rows(): lax.dot_general(rows_cot, down_w, (((1,), (1,)), ((), ())), preferred_ele...  4.8 us
  transfers between devices with their start and end apart: 3, of which 2 were waited for; matrix products, arithmetic and copies ran while one was open for 19% of the time, Pallas kernels for 0%

profile of v4, /device:TPU:1, one launch (start us, length us, event | category | flops | bytes accessed | tf_op | source)
XLA Modules:
  0.0 206.8 jit_solution(5144270149352491207)
XLA Ops:
  0.6 0.0 copy-start.3
  0.6 0.8 fusion.51
  1.5 0.6 reduce-window.6
  2.1 0.2 slice_reduce_fusion
  2.3 0.8 fusion.50
  3.1 0.7 multiply_add_fusion
  3.8 1.9 multiply_convert_fusion
  5.7 0.0 copy-done.3
  5.7 2.5 %fusion = bf16[64,8,7168]{2,1,0:T(8,128)(2,1)S(1)} fusion(bf16[256,3584]{1,0:T(8,128)(2,1)S(1)} %multiply_convert_fusion, bf16[256,3584]{1,0:T(8,128)(2,1)S(1)} %copy-done.3, s32[256]{0:T(256)S(1)} %multiply_add_fusion), kind=kOutput, calls=%fused_computation.1 | convolution fusion | flops 1890189312 | bytes 11011072 | tf_op jit(solution)/shard_map/dot_general | solution.py:66
  8.2 0.0 copy-start.2
  8.3 97.2 %all_to_all.10 = bf16[64,8,7168]{2,1,0:T(8,128)(2,1)S(1)} all-to-all(bf16[64,8,7168]{2,1,0:T(8,128)(2,1)S(1)} %fusion), channel_id=1, replica_groups=mesh['dp'=2,'expert'=64] {'expert'}, dimensions={0} | all-to-all | bytes 14680064 | tf_op jit(solution)/shard_map/all_to_all | solution.py:70
  105.5 3.3 %collective-permute-start = (bf16[64,8,7168]{2,1,0:T(8,128)(2,1)S(1)}, bf16[64,8,7168]{2,1,0:T(8,128)(2,1)S(1)}, u32[]{:S(2)}, u32[]{:S(2)}) collective-permute-start(bf16[64,8,7168]{2,1,0:T(8,128)(2,1)S(1)} %all_to_all.10), channel_id=1, source_target_pairs={{0,64},{64,0},{1,65},{65,1},{2,66},{66,2},{3,67},{67,3},{4,68},{68... | collective-permute-start | bytes 22020104 | tf_op jit(solution)/shard_map/ppermute | solution.py:72
  108.7 11.3 %collective-permute-done = bf16[64,8,7168]{2,1,0:T(8,128)(2,1)S(1)} collective-permute-done((bf16[64,8,7168]{2,1,0:T(8,128)(2,1)S(1)}, bf16[64,8,7168]{2,1,0:T(8,128)(2,1)S(1)}, u32[]{:S(2)}, u32[]{:S(2)}) %collective-permute-start) | collective-permute-done | bytes 7340064 | tf_op jit(solution)/shard_map/ppermute | solution.py:72
  120.0 0.0 copy-done.2
  120.0 2.1 %fusion.11 = f32[512,512]{1,0:T(8,128)S(1)} fusion(bf16[1,3584,512]{2,1,0:T(8,128)(2,1)S(1)} %copy-done.2, bf16[512,7168]{1,0:T(8,128)(2,1)S(1)} %bitcast.84), kind=kOutput, calls=%fused_computation.18 | convolution fusion | flops 1879048192 | bytes 8388608 | tf_op jit(solution)/shard_map/dot_general | solution.py:8
  122.1 2.6 %copy-done.1 = bf16[1,3584,512]{2,1,0:T(8,128)(2,1)S(1)} copy-done((bf16[1,3584,512]{2,1,0:T(8,128)(2,1)S(1)}, bf16[1,3584,512]{2,1,0:T(8,128)(2,1)}, u32[]{:S(2)}) %copy-start.1) | copy-done | bytes 3670040
  124.7 2.1 fusion.18
  126.8 0.0 copy-done.15
  126.8 0.0 copy-done.18
  126.8 0.3 copy-done.16
  127.1 2.4 %multiply_convert_fusion.3 = (bf16[512,512]{1,0:T(8,128)(2,1)S(1)}, bf16[512,512]{1,0:T(8,128)(2,1)S(1)}) fusion(f32[512,512]{1,0:T(8,128)S(1)} %fusion.11, f32[512,512]{1,0:T(8,128)S(1)} %fusion.18, bf16[1,512,3584]{2,1,0:T(8,128)(2,1)S(1)} %copy-done.16, bf16[512,7168]{1,0:T(8,128)(2,1)S(1)} %bitcast.86), kind=kOutput, calls=%fused_computation.52 | convolution fusion | flops 1882456064 | bytes 10485760 | tf_op jit(solution)/shard_map/dot_general | solution.py:13
  129.5 0.0 copy-done.20
  129.5 0.0 copy-start.10
  129.5 0.0 copy-start.4
  129.6 2.1 %fusion.9 = f32[512,3584]{1,0:T(8,128)S(1)} fusion(bf16[512,512]{1,0:T(8,128)(2,1)S(1)} %get-tuple-element.7, bf16[1,3584,512]{2,1,0:T(8,128)(2,1)S(1)} %copy-done.2), kind=kOutput, calls=%fused_computation.16 | convolution fusion | flops 1879048192 | bytes 11534336 | tf_op jit(solution)/shard_map/dot_general | solution.py:24
  131.7 0.0 copy-done.10
  131.7 0.0 copy-done.4
  131.7 2.2 %add_convert_fusion.4 = bf16[512,3584]{1,0:T(8,128)(2,1)S(1)} fusion(f32[512,3584]{1,0:T(8,128)S(1)} %fusion.9, bf16[512,512]{1,0:T(8,128)(2,1)S(1)} %get-tuple-element.6, bf16[1,3584,512]{2,1,0:T(8,128)(2,1)S(1)} %copy-done.1), kind=kOutput, calls=%fused_computation.6 | convolution fusion | flops 1882718208 | bytes 15204352 | tf_op jit(solution)/shard_map/dot_general | solution.py:27
  133.9 0.6 collective-permute-start.1
  134.5 2.1 %fusion.15 = f32[512,512]{1,0:T(8,128)S(1)} fusion(bf16[1,3584,512]{2,1,0:T(8,128)(2,1)S(1)} %copy-done.2, bf16[512,7168]{1,0:T(8,128)(2,1)S(1)} %bitcast.72), kind=kOutput, calls=%fused_computation.22 | convolution fusion | flops 1879048192 | bytes 8388608 | tf_op jit(solution)/shard_map/dot_general | solution.py:8
  136.6 0.0 copy-start.6
  136.6 0.0 copy-start.17
  136.6 2.1 fusion.21
  138.7 0.0 copy-done
  138.7 0.0 copy-done.6
  138.7 0.3 copy-done.17
  139.1 2.4 %multiply_convert_fusion.5 = (bf16[512,512]{1,0:T(8,128)(2,1)S(1)}, bf16[512,512]{1,0:T(8,128)(2,1)S(1)}) fusion(f32[512,512]{1,0:T(8,128)S(1)} %fusion.15, f32[512,512]{1,0:T(8,128)S(1)} %fusion.21, bf16[1,512,3584]{2,1,0:T(8,128)(2,1)S(1)} %copy-done.17, bf16[512,7168]{1,0:T(8,128)(2,1)S(1)} %bitcast.74), kind=kOutput, calls=%fused_computation.56 | convolution fusion | flops 1882456064 | bytes 10485760 | tf_op jit(solution)/shard_map/dot_general | solution.py:13
  141.5 0.0 copy-start.12
  141.5 2.1 %fusion.13 = f32[512,3584]{1,0:T(8,128)S(1)} fusion(bf16[512,512]{1,0:T(8,128)(2,1)S(1)} %get-tuple-element.5, bf16[1,3584,512]{2,1,0:T(8,128)(2,1)S(1)} %copy-done.2), kind=kOutput, calls=%fused_computation.20 | convolution fusion | flops 1879048192 | bytes 11534336 | tf_op jit(solution)/shard_map/dot_general | solution.py:84
  143.7 0.0 collective-permute-done.1
  143.7 3.9 %fusion.1 = bf16[64,8,3584]{2,1,0:T(8,128)(2,1)} fusion(bf16[512,3584]{1,0:T(8,128)(2,1)S(1)} %collective-permute-done.1, f32[512,3584]{1,0:T(8,128)S(1)} %fusion.13, bf16[512,512]{1,0:T(8,128)(2,1)S(1)} %get-tuple-element.4, bf16[1,3584,512]{2,1,0:T(8,128)(2,1)S(1)} %copy-done.1), kind=kOutput, calls=%fused_computation.7 | convolution fusion | flops 1886388224 | bytes 18874368 | tf_op jit(solution)/shard_map/dot_general | solution.py:87
  147.6 6.1 %all-to-all-start.1 = ((bf16[64,8,3584]{2,1,0:T(8,128)(2,1)}), bf16[64,8,3584]{2,1,0:T(8,128)(2,1)}, u32[]{:S(2)}, u32[]{:S(2)}) async-start(bf16[64,8,3584]{2,1,0:T(8,128)(2,1)} %fusion.1), calls=%async_computation.1 | async-start | bytes 7340032 | tf_op jit(solution)/shard_map/all_to_all | solution.py:91
  153.7 0.0 slice-start.1
  153.7 0.0 copy-start.13
  153.8 0.0 slice-start.2
  153.8 7.4 %fusion.36 = f32[3584,512]{1,0:T(8,128)} fusion(bf16[512,512]{1,0:T(8,128)(2,1)} %copy-done.14, bf16[512,7168]{1,0:T(8,128)(2,1)} %bitcast.75), kind=kOutput, calls=%fused_computation.44 | convolution fusion | flops 1879048192 | bytes 11534336 | tf_op jit(solution)/shard_map/dot_general | solution.py:37
  161.1 0.0 slice-done
  161.1 0.0 copy-done.13
  161.1 0.0 copy-start.7
  161.2 0.0 copy-start.9
  161.2 0.0 slice-start.3
  161.2 5.1 %fusion.38 = f32[3584,512]{1,0:T(8,128)} fusion(bf16[512,512]{1,0:T(8,128)(2,1)S(1)} %copy-done.13, bf16[512,7168]{1,0:T(8,128)(2,1)S(1)} %bitcast.78), kind=kOutput, calls=%fused_computation.46 | convolution fusion | flops 1879048192 | bytes 11534336 | tf_op jit(solution)/shard_map/dot_general | solution.py:34
  166.3 2.2 %fusion.29 = f32[512,3584]{1,0:T(8,128)S(1)} fusion(bf16[512,7168]{1,0:T(8,128)(2,1)S(1)} %bitcast.79, f32[512,512]{1,0:T(8,128)S(1)} %copy-done.9, f32[512,512]{1,0:T(8,128)S(1)} %copy-done.7), kind=kOutput, calls=%fused_computation.37 | convolution fusion | flops 1880621056 | bytes 13107200 | tf_op jit(solution)/shard_map/dot_general | solution.py:40
  168.6 0.0 slice-done.2
  168.6 0.0 slice-done.3
  168.6 0.0 copy-done.5
  168.6 0.0 copy-start.11
  168.6 0.0 slice-start.5
  168.6 7.3 %fusion.3 = bf16[1,3584,512]{2,1,0:T(8,128)(2,1)} fusion(f32[3584,512]{1,0:T(8,128)} %fusion.36, bf16[512,512]{1,0:T(8,128)(2,1)S(1)} %copy-done.5, bf16[512,7168]{1,0:T(8,128)(2,1)S(1)} %bitcast.89), kind=kOutput, calls=%fused_computation.9 | convolution fusion | flops 1882718208 | bytes 15204352 | tf_op jit(solution)/shard_map/dot_general | solution.py:37
  176.0 0.0 slice-done.4
  176.0 4.2 %fusion.2 = bf16[1,3584,512]{2,1,0:T(8,128)(2,1)} fusion(f32[3584,512]{1,0:T(8,128)S(1)} %bitcast.93, bf16[512,512]{1,0:T(8,128)(2,1)S(1)} %copy-done.11, bf16[512,7168]{1,0:T(8,128)(2,1)S(1)} %bitcast.90), kind=kOutput, calls=%fused_computation.8 | convolution fusion | flops 1882718208 | bytes 15204352 | tf_op jit(solution)/shard_map/dot_general | solution.py:34
  180.2 4.3 %fusion.4 = bf16[1,512,3584]{2,1,0:T(8,128)(2,1)} fusion(f32[512,3584]{1,0:T(8,128)S(1)} %fusion.29, bf16[512,7168]{1,0:T(8,128)(2,1)S(1)} %bitcast.91, f32[512,512]{1,0:T(8,128)S(1)} %copy-done.21, f32[512,512]{1,0:T(8,128)S(1)} %copy-done.19), kind=kOutput, calls=%fused_computation.10 | convolution fusion | flops 1884291072 | bytes 16777216 | tf_op jit(solution)/shard_map/dot_general | solution.py:40
  184.4 17.9 %all-to-all-done.1 = bf16[64,8,3584]{2,1,0:T(8,128)(2,1)} async-done(((bf16[64,8,3584]{2,1,0:T(8,128)(2,1)}), bf16[64,8,3584]{2,1,0:T(8,128)(2,1)}, u32[]{:S(2)}, u32[]{:S(2)}) %all-to-all-start.1) | async-done | bytes 3670048 | tf_op jit(solution)/shard_map/all_to_all | solution.py:91
  202.4 4.4 %convolution_convert_fusion.1 = bf16[256,3584]{1,0:T(8,128)(2,1)} fusion(bf16[64,8,3584]{2,1,0:T(8,128)(2,1)} %all-to-all-done.1, s32[256]{0:T(256)S(1)} %multiply_add_fusion), kind=kOutput, calls=%fused_computation.11 | convolution fusion | flops 940572672 | bytes 5506048 | tf_op jit(solution)/shard_map/dot_general | solution.py:97
  (28 shorter events, 0.1 us)
Async XLA Ops:
  0.6 5.1 %copy-start.3 = (bf16[256,3584]{1,0:T(8,128)(2,1)S(1)}, bf16[256,3584]{1,0:T(8,128)(2,1)}, u32[]{:S(2)}) copy-start(bf16[256,3584]{1,0:T(8,128)(2,1)} %param.7) | copy-start | bytes 5505028
  8.2 111.8 %copy-start.2 = (bf16[1,3584,512]{2,1,0:T(8,128)(2,1)S(1)}, bf16[1,3584,512]{2,1,0:T(8,128)(2,1)}, u32[]{:S(2)}) copy-start(bf16[1,3584,512]{2,1,0:T(8,128)(2,1)} %param.11) | copy-start | bytes 11010052
  105.5 33.2 %copy-start = (bf16[64,8,7168]{2,1,0:T(8,128)(2,1)}, bf16[64,8,7168]{2,1,0:T(8,128)(2,1)S(1)}, u32[]{:S(2)}) copy-start(bf16[64,8,7168]{2,1,0:T(8,128)(2,1)S(1)} %all_to_all.10) | copy-start | bytes 22020100
  105.5 14.5 %collective-permute-start = (bf16[64,8,7168]{2,1,0:T(8,128)(2,1)S(1)}, bf16[64,8,7168]{2,1,0:T(8,128)(2,1)S(1)}, u32[]{:S(2)}, u32[]{:S(2)}) collective-permute-start(bf16[64,8,7168]{2,1,0:T(8,128)(2,1)S(1)} %all_to_all.10), channel_id=1, source_target_pairs={{0,64},{64,0},{1,65},{65,1},{2,66},{66,2},{3,67},{67,3},{4,68},{68... | collective-permute-start | bytes 22020104 | tf_op jit(solution)/shard_map/ppermute | solution.py:72
  120.0 6.8 %copy-start.15 = (bf16[64,8,7168]{2,1,0:T(8,128)(2,1)}, bf16[64,8,7168]{2,1,0:T(8,128)(2,1)S(1)}, u32[]{:S(2)}) copy-start(bf16[64,8,7168]{2,1,0:T(8,128)(2,1)S(1)} %collective-permute-done) | copy-start | bytes 22020100
  120.0 4.7 %copy-start.1 = (bf16[1,3584,512]{2,1,0:T(8,128)(2,1)S(1)}, bf16[1,3584,512]{2,1,0:T(8,128)(2,1)}, u32[]{:S(2)}) copy-start(bf16[1,3584,512]{2,1,0:T(8,128)(2,1)} %param.12) | copy-start | bytes 11010052
  124.7 2.1 %copy-start.18 = (f32[512,512]{1,0:T(8,128)}, f32[512,512]{1,0:T(8,128)S(1)}, u32[]{:S(2)}) copy-start(f32[512,512]{1,0:T(8,128)S(1)} %fusion.11) | copy-start | bytes 3145732
  124.7 2.4 %copy-start.16 = (bf16[1,512,3584]{2,1,0:T(8,128)(2,1)S(1)}, bf16[1,512,3584]{2,1,0:T(8,128)(2,1)}, u32[]{:S(2)}) copy-start(bf16[1,512,3584]{2,1,0:T(8,128)(2,1)} %param.13) | copy-start | bytes 11010052
  127.1 2.4 %copy-start.20 = (f32[512,512]{1,0:T(8,128)}, f32[512,512]{1,0:T(8,128)S(1)}, u32[]{:S(2)}) copy-start(f32[512,512]{1,0:T(8,128)S(1)} %fusion.18) | copy-start | bytes 3145732
  129.5 2.1 %copy-start.10 = (bf16[512,512]{1,0:T(8,128)(2,1)}, bf16[512,512]{1,0:T(8,128)(2,1)S(1)}, u32[]{:S(2)}) copy-start(bf16[512,512]{1,0:T(8,128)(2,1)S(1)} %get-tuple-element.7) | copy-start | bytes 1572868
  129.5 2.1 %copy-start.4 = (bf16[512,512]{1,0:T(8,128)(2,1)}, bf16[512,512]{1,0:T(8,128)(2,1)S(1)}, u32[]{:S(2)}) copy-start(bf16[512,512]{1,0:T(8,128)(2,1)S(1)} %get-tuple-element.6) | copy-start | bytes 1572868
  133.9 9.8 %collective-permute-start.1 = (bf16[512,3584]{1,0:T(8,128)(2,1)S(1)}, bf16[512,3584]{1,0:T(8,128)(2,1)S(1)}, u32[]{:S(2)}, u32[]{:S(2)}) collective-permute-start(bf16[512,3584]{1,0:T(8,128)(2,1)S(1)} %add_convert_fusion.4), channel_id=1, source_target_pairs={{0,64},{64,0},{1,65},{65,1},{2,66},{66,2},{3,67},{67,3},{4,68},{68... | collective-permute-start | bytes 11010056 | tf_op jit(solution)/shard_map/ppermute | solution.py:83
  136.6 2.1 %copy-start.6 = (f32[512,512]{1,0:T(8,128)}, f32[512,512]{1,0:T(8,128)S(1)}, u32[]{:S(2)}) copy-start(f32[512,512]{1,0:T(8,128)S(1)} %fusion.15) | copy-start | bytes 3145732
  136.6 2.4 %copy-start.17 = (bf16[1,512,3584]{2,1,0:T(8,128)(2,1)S(1)}, bf16[1,512,3584]{2,1,0:T(8,128)(2,1)}, u32[]{:S(2)}) copy-start(bf16[1,512,3584]{2,1,0:T(8,128)(2,1)} %param.13) | copy-start | bytes 11010052
  139.1 2.4 %copy-start.8 = (f32[512,512]{1,0:T(8,128)}, f32[512,512]{1,0:T(8,128)S(1)}, u32[]{:S(2)}) copy-start(f32[512,512]{1,0:T(8,128)S(1)} %fusion.21) | copy-start | bytes 3145732
  141.5 2.2 %copy-start.12 = (bf16[512,512]{1,0:T(8,128)(2,1)}, bf16[512,512]{1,0:T(8,128)(2,1)S(1)}, u32[]{:S(2)}) copy-start(bf16[512,512]{1,0:T(8,128)(2,1)S(1)} %get-tuple-element.5) | copy-start | bytes 1572868
  141.5 2.2 %copy-start.14 = (bf16[512,512]{1,0:T(8,128)(2,1)}, bf16[512,512]{1,0:T(8,128)(2,1)S(1)}, u32[]{:S(2)}) copy-start(bf16[512,512]{1,0:T(8,128)(2,1)S(1)} %get-tuple-element.4) | copy-start | bytes 1572868
  147.6 13.5 %slice-start = ((s8[7340032]{0:T(1024)(128)(4,1)}), s8[3145728]{0:T(1024)(128)(4,1)S(1)}, s32[]{:S(2)}) async-start(s8[7340032]{0:T(1024)(128)(4,1)} %bitcast.76), calls=%async_computation.2 | async-start | bytes 6291456
  147.6 54.8 %all-to-all-start.1 = ((bf16[64,8,3584]{2,1,0:T(8,128)(2,1)}), bf16[64,8,3584]{2,1,0:T(8,128)(2,1)}, u32[]{:S(2)}, u32[]{:S(2)}) async-start(bf16[64,8,3584]{2,1,0:T(8,128)(2,1)} %fusion.1), calls=%async_computation.1 | async-start | bytes 7340032 | tf_op jit(solution)/shard_map/all_to_all | solution.py:91
  153.7 7.4 %slice-start.1 = ((s8[7340032]{0:T(1024)(128)(4,1)}), s8[4194304]{0:T(1024)(128)(4,1)S(1)}, s32[]{:S(2)}) async-start(s8[7340032]{0:T(1024)(128)(4,1)} %bitcast.76), calls=%async_computation.3 | async-start | bytes 8388608
  153.7 7.4 %copy-start.13 = (bf16[512,512]{1,0:T(8,128)(2,1)S(1)}, bf16[512,512]{1,0:T(8,128)(2,1)}, u32[]{:S(2)}) copy-start(bf16[512,512]{1,0:T(8,128)(2,1)} %copy-done.12) | copy-start | bytes 1572868
  153.8 14.8 %slice-start.2 = ((s8[7340032]{0:T(1024)(128)(4,1)}), s8[4194304]{0:T(1024)(128)(4,1)S(1)}, s32[]{:S(2)}) async-start(s8[7340032]{0:T(1024)(128)(4,1)} %bitcast.87), calls=%async_computation.4 | async-start | bytes 8388608
  161.1 5.2 %copy-start.7 = (f32[512,512]{1,0:T(8,128)S(1)}, f32[512,512]{1,0:T(8,128)}, u32[]{:S(2)}) copy-start(f32[512,512]{1,0:T(8,128)} %copy-done.6) | copy-start | bytes 3145732
  161.2 5.2 %copy-start.9 = (f32[512,512]{1,0:T(8,128)S(1)}, f32[512,512]{1,0:T(8,128)}, u32[]{:S(2)}) copy-start(f32[512,512]{1,0:T(8,128)} %copy-done.8) | copy-start | bytes 3145732
  161.2 7.4 %slice-start.3 = ((s8[7340032]{0:T(1024)(128)(4,1)}), s8[3145728]{0:T(1024)(128)(4,1)S(1)}, s32[]{:S(2)}) async-start(s8[7340032]{0:T(1024)(128)(4,1)} %bitcast.87), calls=%async_computation.5 | async-start | bytes 6291456
  166.3 2.3 %copy-start.5 = (bf16[512,512]{1,0:T(8,128)(2,1)S(1)}, bf16[512,512]{1,0:T(8,128)(2,1)}, u32[]{:S(2)}) copy-start(bf16[512,512]{1,0:T(8,128)(2,1)} %copy-done.4) | copy-start | bytes 1572868
  166.3 9.6 %slice-start.4 = ((s8[7340032]{0:T(1024)(128)(4,1)}), s8[4194304]{0:T(1024)(128)(4,1)S(1)}, s32[]{:S(2)}) async-start(s8[7340032]{0:T(1024)(128)(4,1)} %bitcast.92), calls=%async_computation.6 | async-start | bytes 8388608
  168.6 7.3 %copy-start.11 = (bf16[512,512]{1,0:T(8,128)(2,1)S(1)}, bf16[512,512]{1,0:T(8,128)(2,1)}, u32[]{:S(2)}) copy-start(bf16[512,512]{1,0:T(8,128)(2,1)} %copy-done.10) | copy-start | bytes 1572868
  168.6 7.3 %slice-start.5 = ((s8[7340032]{0:T(1024)(128)(4,1)}), s8[3145728]{0:T(1024)(128)(4,1)S(1)}, s32[]{:S(2)}) async-start(s8[7340032]{0:T(1024)(128)(4,1)} %bitcast.92), calls=%async_computation.7 | async-start | bytes 6291456
  176.0 4.2 %copy-start.19 = (f32[512,512]{1,0:T(8,128)S(1)}, f32[512,512]{1,0:T(8,128)}, u32[]{:S(2)}) copy-start(f32[512,512]{1,0:T(8,128)} %copy-done.18) | copy-start | bytes 3145732
  176.0 4.2 %copy-start.21 = (f32[512,512]{1,0:T(8,128)S(1)}, f32[512,512]{1,0:T(8,128)}, u32[]{:S(2)}) copy-start(f32[512,512]{1,0:T(8,128)} %copy-done.20) | copy-start | bytes 3145732

commit v5 on v4

--- a/solution.py
+++ b/solution.py
@@ -94,10 +94,12 @@
     sums_own = weight_sums(own_x, own_cot, own_h, own_dg, own_du)
     sums_oth = weight_sums(oth_x, oth_cot, oth_h, oth_dg, oth_du)
     grad_gate, grad_up, grad_down = (a + b for a, b in zip(sums_own, sums_oth))
-    copy_grad = lax.dot_general(
-        placing,
+    gathering = (position[:, None] == jnp.arange(owners * capacity, dtype=jnp.int32)[None, :]).astype(
+        jnp.bfloat16
+    )
+    copy_grad = jnp.dot(
+        gathering,
         returned.reshape(owners * capacity, model_width),
-        (((0,), (0,)), ((), ())),
         preferred_element_type=jnp.float32,
     )
     grad_tokens = jnp.sum(copy_grad.reshape(tok_rows, fanout, model_width), axis=1).astype(

time: 207 us -> 207 us (level)
  no operation moved by 1% of the time
where the time goes in v5:
time: 207 us
  blocking collectives  97.2 us (47%)
  matrix products  60.9 us (29%)
  waiting for transfers between devices  29.3 us (14%)
  starting transfers between devices  9.99 us (5%)
  other arithmetic  4.89 us (2%)
  local copies, waits for them, and re-layouts  3.58 us (2%)
    all_to_all x1, blocking collectives, local(): lax.all_to_all(sent, 'expert', split_axis=0, concat_axis=0, tiled=True)  97.2 us
    all_to_all x1, waiting for transfers between devices, local(): lax.all_to_all(summed.reshape(owners, capacity, model_width), 'expert', s...  18 us
    dot_general x2, matrix products, weight_sums(): lax.dot_general(rows_x, d_up, (((0,), (0,)), ((), ())), preferred_element...  14.7 us
    ppermute x1, waiting for transfers between devices, local(): other = lax.ppermute(came, 'dp', swap)  11.3 us
    dot_general x2, matrix products, weight_sums(): lax.dot_general(rows_x, d_gate, (((0,), (0,)), ((), ())), preferred_eleme...  9.31 us
    dot_general x2, matrix products, weight_sums(): lax.dot_general(hidden, rows_cot, (((0,), (0,)), ((), ())), preferred_ele...  6.49 us
    all_to_all x1, starting transfers between devices, local(): lax.all_to_all(summed.reshape(owners, capacity, model_width), 'expert', s...  6.09 us
    dot_general x2, matrix products, front_rows(): lax.dot_general(rows_cot, down_w, (((1,), (1,)), ((), ())), preferred_ele...  4.81 us
  transfers between devices with their start and end apart: 3, of which 2 were waited for; matrix products, arithmetic and copies ran while one was open for 19% of the time, Pallas kernels for 0%

profile of v5, /device:TPU:1, one launch (start us, length us, event | category | flops | bytes accessed | tf_op | source)
XLA Modules:
  0.0 206.9 jit_solution(499006520616906039)
XLA Ops:
  0.6 0.0 copy-start.3
  0.6 0.8 fusion.51
  1.5 0.6 reduce-window.6
  2.1 0.2 slice_reduce_fusion
  2.3 0.8 fusion.50
  3.1 0.7 multiply_add_fusion
  3.8 1.9 multiply_convert_fusion
  5.7 0.0 copy-done.3
  5.7 2.5 %fusion = bf16[64,8,7168]{2,1,0:T(8,128)(2,1)S(1)} fusion(bf16[256,3584]{1,0:T(8,128)(2,1)S(1)} %multiply_convert_fusion, bf16[256,3584]{1,0:T(8,128)(2,1)S(1)} %copy-done.3, s32[256]{0:T(256)S(1)} %multiply_add_fusion), kind=kOutput, calls=%fused_computation.1 | convolution fusion | flops 1890189312 | bytes 11011072 | tf_op jit(solution)/shard_map/dot_general | solution.py:66
  8.2 0.0 copy-start.2
  8.3 97.2 %all_to_all.10 = bf16[64,8,7168]{2,1,0:T(8,128)(2,1)S(1)} all-to-all(bf16[64,8,7168]{2,1,0:T(8,128)(2,1)S(1)} %fusion), channel_id=1, replica_groups=mesh['dp'=2,'expert'=64] {'expert'}, dimensions={0} | all-to-all | bytes 14680064 | tf_op jit(solution)/shard_map/all_to_all | solution.py:70
  105.5 3.3 %collective-permute-start = (bf16[64,8,7168]{2,1,0:T(8,128)(2,1)S(1)}, bf16[64,8,7168]{2,1,0:T(8,128)(2,1)S(1)}, u32[]{:S(2)}, u32[]{:S(2)}) collective-permute-start(bf16[64,8,7168]{2,1,0:T(8,128)(2,1)S(1)} %all_to_all.10), channel_id=1, source_target_pairs={{0,64},{64,0},{1,65},{65,1},{2,66},{66,2},{3,67},{67,3},{4,68},{68... | collective-permute-start | bytes 22020104 | tf_op jit(solution)/shard_map/ppermute | solution.py:72
  108.7 11.3 %collective-permute-done = bf16[64,8,7168]{2,1,0:T(8,128)(2,1)S(1)} collective-permute-done((bf16[64,8,7168]{2,1,0:T(8,128)(2,1)S(1)}, bf16[64,8,7168]{2,1,0:T(8,128)(2,1)S(1)}, u32[]{:S(2)}, u32[]{:S(2)}) %collective-permute-start) | collective-permute-done | bytes 7340064 | tf_op jit(solution)/shard_map/ppermute | solution.py:72
  120.0 0.0 copy-done.2
  120.0 2.1 %fusion.11 = f32[512,512]{1,0:T(8,128)S(1)} fusion(bf16[1,3584,512]{2,1,0:T(8,128)(2,1)S(1)} %copy-done.2, bf16[512,7168]{1,0:T(8,128)(2,1)S(1)} %bitcast.88), kind=kOutput, calls=%fused_computation.18 | convolution fusion | flops 1879048192 | bytes 8388608 | tf_op jit(solution)/shard_map/dot_general | solution.py:8
  122.1 2.6 %copy-done.1 = bf16[1,3584,512]{2,1,0:T(8,128)(2,1)S(1)} copy-done((bf16[1,3584,512]{2,1,0:T(8,128)(2,1)S(1)}, bf16[1,3584,512]{2,1,0:T(8,128)(2,1)}, u32[]{:S(2)}) %copy-start.1) | copy-done | bytes 3670040
  124.7 2.1 fusion.18
  126.8 0.0 copy-done.16
  126.8 0.0 copy-done.19
  126.8 0.3 copy-done.17
  127.1 2.4 %multiply_convert_fusion.3 = (bf16[512,512]{1,0:T(8,128)(2,1)S(1)}, bf16[512,512]{1,0:T(8,128)(2,1)S(1)}) fusion(f32[512,512]{1,0:T(8,128)S(1)} %fusion.11, f32[512,512]{1,0:T(8,128)S(1)} %fusion.18, bf16[1,512,3584]{2,1,0:T(8,128)(2,1)S(1)} %copy-done.17, bf16[512,7168]{1,0:T(8,128)(2,1)S(1)} %bitcast.90), kind=kOutput, calls=%fused_computation.52 | convolution fusion | flops 1882456064 | bytes 10485760 | tf_op jit(solution)/shard_map/dot_general | solution.py:13
  129.5 0.0 copy-done.21
  129.5 0.0 copy-start.10
  129.6 0.0 copy-start.4
  129.6 2.1 %fusion.9 = f32[512,3584]{1,0:T(8,128)S(1)} fusion(bf16[512,512]{1,0:T(8,128)(2,1)S(1)} %get-tuple-element.7, bf16[1,3584,512]{2,1,0:T(8,128)(2,1)S(1)} %copy-done.2), kind=kOutput, calls=%fused_computation.16 | convolution fusion | flops 1879048192 | bytes 11534336 | tf_op jit(solution)/shard_map/dot_general | solution.py:24
  131.7 0.0 copy-done.10
  131.7 0.0 copy-done.4
  131.7 0.0 copy-start.15
  131.7 2.2 %add_convert_fusion.4 = bf16[512,3584]{1,0:T(8,128)(2,1)S(1)} fusion(f32[512,3584]{1,0:T(8,128)S(1)} %fusion.9, bf16[512,512]{1,0:T(8,128)(2,1)S(1)} %get-tuple-element.6, bf16[1,3584,512]{2,1,0:T(8,128)(2,1)S(1)} %copy-done.1), kind=kOutput, calls=%fused_computation.6 | convolution fusion | flops 1882718208 | bytes 15204352 | tf_op jit(solution)/shard_map/dot_general | solution.py:27
  133.9 0.6 collective-permute-start.1
  134.6 0.0 copy-done.15
  134.6 2.1 %fusion.15 = f32[512,512]{1,0:T(8,128)S(1)} fusion(bf16[1,3584,512]{2,1,0:T(8,128)(2,1)S(1)} %copy-done.2, bf16[512,7168]{1,0:T(8,128)(2,1)S(1)} %bitcast.74), kind=kOutput, calls=%fused_computation.22 | convolution fusion | flops 1879048192 | bytes 8388608 | tf_op jit(solution)/shard_map/dot_general | solution.py:8
  136.7 0.0 copy-start.6
  136.7 0.0 copy-start.18
  136.7 2.1 fusion.21
  138.7 0.0 copy-done
  138.8 0.0 copy-done.6
  138.8 0.3 copy-done.18
  139.1 2.4 %multiply_convert_fusion.5 = (bf16[512,512]{1,0:T(8,128)(2,1)S(1)}, bf16[512,512]{1,0:T(8,128)(2,1)S(1)}) fusion(f32[512,512]{1,0:T(8,128)S(1)} %fusion.15, f32[512,512]{1,0:T(8,128)S(1)} %fusion.21, bf16[1,512,3584]{2,1,0:T(8,128)(2,1)S(1)} %copy-done.18, bf16[512,7168]{1,0:T(8,128)(2,1)S(1)} %bitcast.76), kind=kOutput, calls=%fused_computation.56 | convolution fusion | flops 1882456064 | bytes 10485760 | tf_op jit(solution)/shard_map/dot_general | solution.py:13
  141.5 0.0 copy-done.8
  141.5 0.0 copy-start.12
  141.5 0.0 copy-start.14
  141.5 2.1 %fusion.13 = f32[512,3584]{1,0:T(8,128)S(1)} fusion(bf16[512,512]{1,0:T(8,128)(2,1)S(1)} %get-tuple-element.5, bf16[1,3584,512]{2,1,0:T(8,128)(2,1)S(1)} %copy-done.2), kind=kOutput, calls=%fused_computation.20 | convolution fusion | flops 1879048192 | bytes 11534336 | tf_op jit(solution)/shard_map/dot_general | solution.py:84
  143.7 0.0 collective-permute-done.1
  143.7 3.9 %fusion.1 = bf16[64,8,3584]{2,1,0:T(8,128)(2,1)} fusion(bf16[512,3584]{1,0:T(8,128)(2,1)S(1)} %collective-permute-done.1, f32[512,3584]{1,0:T(8,128)S(1)} %fusion.13, bf16[512,512]{1,0:T(8,128)(2,1)S(1)} %get-tuple-element.4, bf16[1,3584,512]{2,1,0:T(8,128)(2,1)S(1)} %copy-done.1), kind=kOutput, calls=%fused_computation.7 | convolution fusion | flops 1886388224 | bytes 18874368 | tf_op jit(solution)/shard_map/dot_general | solution.py:87
  147.7 6.1 %all-to-all-start.1 = ((bf16[64,8,3584]{2,1,0:T(8,128)(2,1)}), bf16[64,8,3584]{2,1,0:T(8,128)(2,1)}, u32[]{:S(2)}, u32[]{:S(2)}) async-start(bf16[64,8,3584]{2,1,0:T(8,128)(2,1)} %fusion.1), calls=%async_computation.1 | async-start | bytes 7340032 | tf_op jit(solution)/shard_map/all_to_all | solution.py:91
  153.8 0.0 slice-start.1
  153.8 0.0 copy-start.13
  153.8 0.0 slice-start.2
  153.8 7.4 %fusion.36 = f32[3584,512]{1,0:T(8,128)} fusion(bf16[512,512]{1,0:T(8,128)(2,1)} %copy-done.14, bf16[512,7168]{1,0:T(8,128)(2,1)} %bitcast.77), kind=kOutput, calls=%fused_computation.44 | convolution fusion | flops 1879048192 | bytes 11534336 | tf_op jit(solution)/shard_map/dot_general | solution.py:37
  161.2 0.0 copy-start.7
  161.2 0.0 copy-start.9
  161.2 0.0 slice-start.3
  161.2 5.1 %fusion.38 = f32[3584,512]{1,0:T(8,128)} fusion(bf16[512,512]{1,0:T(8,128)(2,1)S(1)} %copy-done.13, bf16[512,7168]{1,0:T(8,128)(2,1)S(1)} %bitcast.80), kind=kOutput, calls=%fused_computation.46 | convolution fusion | flops 1879048192 | bytes 11534336 | tf_op jit(solution)/shard_map/dot_general | solution.py:34
  166.4 2.2 %fusion.29 = f32[512,3584]{1,0:T(8,128)S(1)} fusion(bf16[512,7168]{1,0:T(8,128)(2,1)S(1)} %bitcast.81, f32[512,512]{1,0:T(8,128)S(1)} %copy-done.9, f32[512,512]{1,0:T(8,128)S(1)} %copy-done.7), kind=kOutput, calls=%fused_computation.37 | convolution fusion | flops 1880621056 | bytes 13107200 | tf_op jit(solution)/shard_map/dot_general | solution.py:40
  168.6 0.0 copy-start.11
  168.7 0.0 slice-start.5
  168.7 7.3 %fusion.3 = bf16[1,3584,512]{2,1,0:T(8,128)(2,1)} fusion(f32[3584,512]{1,0:T(8,128)} %fusion.36, bf16[512,512]{1,0:T(8,128)(2,1)S(1)} %copy-done.5, bf16[512,7168]{1,0:T(8,128)(2,1)S(1)} %bitcast.93), kind=kOutput, calls=%fused_computation.9 | convolution fusion | flops 1882718208 | bytes 15204352 | tf_op jit(solution)/shard_map/dot_general | solution.py:37
  176.0 0.0 slice-done.4
  176.0 4.2 %fusion.2 = bf16[1,3584,512]{2,1,0:T(8,128)(2,1)} fusion(f32[3584,512]{1,0:T(8,128)S(1)} %bitcast.97, bf16[512,512]{1,0:T(8,128)(2,1)S(1)} %copy-done.11, bf16[512,7168]{1,0:T(8,128)(2,1)S(1)} %bitcast.94), kind=kOutput, calls=%fused_computation.8 | convolution fusion | flops 1882718208 | bytes 15204352 | tf_op jit(solution)/shard_map/dot_general | solution.py:34
  180.2 0.0 copy-done.22
  180.2 4.3 %fusion.4 = bf16[1,512,3584]{2,1,0:T(8,128)(2,1)} fusion(f32[512,3584]{1,0:T(8,128)S(1)} %fusion.29, bf16[512,7168]{1,0:T(8,128)(2,1)S(1)} %bitcast.95, f32[512,512]{1,0:T(8,128)S(1)} %copy-done.22, f32[512,512]{1,0:T(8,128)S(1)} %copy-done.20), kind=kOutput, calls=%fused_computation.10 | convolution fusion | flops 1884291072 | bytes 16777216 | tf_op jit(solution)/shard_map/dot_general | solution.py:40
  184.5 18.0 %all-to-all-done.1 = bf16[64,8,3584]{2,1,0:T(8,128)(2,1)} async-done(((bf16[64,8,3584]{2,1,0:T(8,128)(2,1)}), bf16[64,8,3584]{2,1,0:T(8,128)(2,1)}, u32[]{:S(2)}, u32[]{:S(2)}) %all-to-all-start.1) | async-done | bytes 3670048 | tf_op jit(solution)/shard_map/all_to_all | solution.py:91
  202.5 4.4 %convolution_convert_fusion.1 = bf16[256,3584]{1,0:T(8,128)(2,1)} fusion(bf16[64,8,3584]{2,1,0:T(8,128)(2,1)} %all-to-all-done.1, s32[256]{0:T(256)S(1)} %bitcast.86), kind=kOutput, calls=%fused_computation.11 | convolution fusion | flops 940572672 | bytes 5506048 | tf_op jit(solution)/shard_map/dot_general | solution.py:100
  (31 shorter events, 0.1 us)
Async XLA Ops:
  0.6 5.1 %copy-start.3 = (bf16[256,3584]{1,0:T(8,128)(2,1)S(1)}, bf16[256,3584]{1,0:T(8,128)(2,1)}, u32[]{:S(2)}) copy-start(bf16[256,3584]{1,0:T(8,128)(2,1)} %param.7) | copy-start | bytes 5505028
  8.2 111.8 %copy-start.2 = (bf16[1,3584,512]{2,1,0:T(8,128)(2,1)S(1)}, bf16[1,3584,512]{2,1,0:T(8,128)(2,1)}, u32[]{:S(2)}) copy-start(bf16[1,3584,512]{2,1,0:T(8,128)(2,1)} %param.11) | copy-start | bytes 11010052
  105.5 33.3 %copy-start = (bf16[64,8,7168]{2,1,0:T(8,128)(2,1)}, bf16[64,8,7168]{2,1,0:T(8,128)(2,1)S(1)}, u32[]{:S(2)}) copy-start(bf16[64,8,7168]{2,1,0:T(8,128)(2,1)S(1)} %all_to_all.10) | copy-start | bytes 22020100
  105.5 14.5 %collective-permute-start = (bf16[64,8,7168]{2,1,0:T(8,128)(2,1)S(1)}, bf16[64,8,7168]{2,1,0:T(8,128)(2,1)S(1)}, u32[]{:S(2)}, u32[]{:S(2)}) collective-permute-start(bf16[64,8,7168]{2,1,0:T(8,128)(2,1)S(1)} %all_to_all.10), channel_id=1, source_target_pairs={{0,64},{64,0},{1,65},{65,1},{2,66},{66,2},{3,67},{67,3},{4,68},{68... | collective-permute-start | bytes 22020104 | tf_op jit(solution)/shard_map/ppermute | solution.py:72
  120.0 6.8 %copy-start.16 = (bf16[64,8,7168]{2,1,0:T(8,128)(2,1)}, bf16[64,8,7168]{2,1,0:T(8,128)(2,1)S(1)}, u32[]{:S(2)}) copy-start(bf16[64,8,7168]{2,1,0:T(8,128)(2,1)S(1)} %collective-permute-done) | copy-start | bytes 22020100
  120.0 4.7 %copy-start.1 = (bf16[1,3584,512]{2,1,0:T(8,128)(2,1)S(1)}, bf16[1,3584,512]{2,1,0:T(8,128)(2,1)}, u32[]{:S(2)}) copy-start(bf16[1,3584,512]{2,1,0:T(8,128)(2,1)} %param.12) | copy-start | bytes 11010052
  124.7 2.1 %copy-start.19 = (f32[512,512]{1,0:T(8,128)}, f32[512,512]{1,0:T(8,128)S(1)}, u32[]{:S(2)}) copy-start(f32[512,512]{1,0:T(8,128)S(1)} %fusion.11) | copy-start | bytes 3145732
  124.7 2.4 %copy-start.17 = (bf16[1,512,3584]{2,1,0:T(8,128)(2,1)S(1)}, bf16[1,512,3584]{2,1,0:T(8,128)(2,1)}, u32[]{:S(2)}) copy-start(bf16[1,512,3584]{2,1,0:T(8,128)(2,1)} %param.13) | copy-start | bytes 11010052
  127.1 2.4 %copy-start.21 = (f32[512,512]{1,0:T(8,128)}, f32[512,512]{1,0:T(8,128)S(1)}, u32[]{:S(2)}) copy-start(f32[512,512]{1,0:T(8,128)S(1)} %fusion.18) | copy-start | bytes 3145732
  129.5 2.1 %copy-start.10 = (bf16[512,512]{1,0:T(8,128)(2,1)}, bf16[512,512]{1,0:T(8,128)(2,1)S(1)}, u32[]{:S(2)}) copy-start(bf16[512,512]{1,0:T(8,128)(2,1)S(1)} %get-tuple-element.7) | copy-start | bytes 1572868
  129.6 2.1 %copy-start.4 = (bf16[512,512]{1,0:T(8,128)(2,1)}, bf16[512,512]{1,0:T(8,128)(2,1)S(1)}, u32[]{:S(2)}) copy-start(bf16[512,512]{1,0:T(8,128)(2,1)S(1)} %get-tuple-element.6) | copy-start | bytes 1572868
  131.7 2.9 %copy-start.15 = (s32[256,1]{0,1:T(1,128)S(1)}, s32[256,1]{0,1:T(1,128)}, u32[]{:S(2)}) copy-start(s32[256,1]{0,1:T(1,128)} %param.9) | copy-start | bytes 3076
  133.9 9.8 %collective-permute-start.1 = (bf16[512,3584]{1,0:T(8,128)(2,1)S(1)}, bf16[512,3584]{1,0:T(8,128)(2,1)S(1)}, u32[]{:S(2)}, u32[]{:S(2)}) collective-permute-start(bf16[512,3584]{1,0:T(8,128)(2,1)S(1)} %add_convert_fusion.4), channel_id=1, source_target_pairs={{0,64},{64,0},{1,65},{65,1},{2,66},{66,2},{3,67},{67,3},{4,68},{68... | collective-permute-start | bytes 11010056 | tf_op jit(solution)/shard_map/ppermute | solution.py:83
  136.7 2.1 %copy-start.6 = (f32[512,512]{1,0:T(8,128)}, f32[512,512]{1,0:T(8,128)S(1)}, u32[]{:S(2)}) copy-start(f32[512,512]{1,0:T(8,128)S(1)} %fusion.15) | copy-start | bytes 3145732
  136.7 2.4 %copy-start.18 = (bf16[1,512,3584]{2,1,0:T(8,128)(2,1)S(1)}, bf16[1,512,3584]{2,1,0:T(8,128)(2,1)}, u32[]{:S(2)}) copy-start(bf16[1,512,3584]{2,1,0:T(8,128)(2,1)} %param.13) | copy-start | bytes 11010052
  139.1 2.4 %copy-start.8 = (f32[512,512]{1,0:T(8,128)}, f32[512,512]{1,0:T(8,128)S(1)}, u32[]{:S(2)}) copy-start(f32[512,512]{1,0:T(8,128)S(1)} %fusion.21) | copy-start | bytes 3145732
  141.5 2.2 %copy-start.12 = (bf16[512,512]{1,0:T(8,128)(2,1)}, bf16[512,512]{1,0:T(8,128)(2,1)S(1)}, u32[]{:S(2)}) copy-start(bf16[512,512]{1,0:T(8,128)(2,1)S(1)} %get-tuple-element.5) | copy-start | bytes 1572868
  141.5 2.2 %copy-start.14 = (bf16[512,512]{1,0:T(8,128)(2,1)}, bf16[512,512]{1,0:T(8,128)(2,1)S(1)}, u32[]{:S(2)}) copy-start(bf16[512,512]{1,0:T(8,128)(2,1)S(1)} %get-tuple-element.4) | copy-start | bytes 1572868
  147.7 13.5 %slice-start = ((s8[7340032]{0:T(1024)(128)(4,1)}), s8[3145728]{0:T(1024)(128)(4,1)S(1)}, s32[]{:S(2)}) async-start(s8[7340032]{0:T(1024)(128)(4,1)} %bitcast.78), calls=%async_computation.2 | async-start | bytes 6291456
  147.7 54.8 %all-to-all-start.1 = ((bf16[64,8,3584]{2,1,0:T(8,128)(2,1)}), bf16[64,8,3584]{2,1,0:T(8,128)(2,1)}, u32[]{:S(2)}, u32[]{:S(2)}) async-start(bf16[64,8,3584]{2,1,0:T(8,128)(2,1)} %fusion.1), calls=%async_computation.1 | async-start | bytes 7340032 | tf_op jit(solution)/shard_map/all_to_all | solution.py:91
  153.8 7.4 %slice-start.1 = ((s8[7340032]{0:T(1024)(128)(4,1)}), s8[4194304]{0:T(1024)(128)(4,1)S(1)}, s32[]{:S(2)}) async-start(s8[7340032]{0:T(1024)(128)(4,1)} %bitcast.78), calls=%async_computation.3 | async-start | bytes 8388608
  153.8 7.4 %copy-start.13 = (bf16[512,512]{1,0:T(8,128)(2,1)S(1)}, bf16[512,512]{1,0:T(8,128)(2,1)}, u32[]{:S(2)}) copy-start(bf16[512,512]{1,0:T(8,128)(2,1)} %copy-done.12) | copy-start | bytes 1572868
  153.8 14.8 %slice-start.2 = ((s8[7340032]{0:T(1024)(128)(4,1)}), s8[4194304]{0:T(1024)(128)(4,1)S(1)}, s32[]{:S(2)}) async-start(s8[7340032]{0:T(1024)(128)(4,1)} %bitcast.91), calls=%async_computation.4 | async-start | bytes 8388608
  161.2 5.2 %copy-start.7 = (f32[512,512]{1,0:T(8,128)S(1)}, f32[512,512]{1,0:T(8,128)}, u32[]{:S(2)}) copy-start(f32[512,512]{1,0:T(8,128)} %copy-done.6) | copy-start | bytes 3145732
  161.2 5.2 %copy-start.9 = (f32[512,512]{1,0:T(8,128)S(1)}, f32[512,512]{1,0:T(8,128)}, u32[]{:S(2)}) copy-start(f32[512,512]{1,0:T(8,128)} %copy-done.8) | copy-start | bytes 3145732
  161.2 7.4 %slice-start.3 = ((s8[7340032]{0:T(1024)(128)(4,1)}), s8[3145728]{0:T(1024)(128)(4,1)S(1)}, s32[]{:S(2)}) async-start(s8[7340032]{0:T(1024)(128)(4,1)} %bitcast.91), calls=%async_computation.5 | async-start | bytes 6291456
  166.4 2.3 %copy-start.5 = (bf16[512,512]{1,0:T(8,128)(2,1)S(1)}, bf16[512,512]{1,0:T(8,128)(2,1)}, u32[]{:S(2)}) copy-start(bf16[512,512]{1,0:T(8,128)(2,1)} %copy-done.4) | copy-start | bytes 1572868
  166.4 9.6 %slice-start.4 = ((s8[7340032]{0:T(1024)(128)(4,1)}), s8[4194304]{0:T(1024)(128)(4,1)S(1)}, s32[]{:S(2)}) async-start(s8[7340032]{0:T(1024)(128)(4,1)} %bitcast.96), calls=%async_computation.6 | async-start | bytes 8388608
  168.6 7.3 %copy-start.11 = (bf16[512,512]{1,0:T(8,128)(2,1)S(1)}, bf16[512,512]{1,0:T(8,128)(2,1)}, u32[]{:S(2)}) copy-start(bf16[512,512]{1,0:T(8,128)(2,1)} %copy-done.10) | copy-start | bytes 1572868
  168.7 7.3 %slice-start.5 = ((s8[7340032]{0:T(1024)(128)(4,1)}), s8[3145728]{0:T(1024)(128)(4,1)S(1)}, s32[]{:S(2)}) async-start(s8[7340032]{0:T(1024)(128)(4,1)} %bitcast.96), calls=%async_computation.7 | async-start | bytes 6291456
  176.0 4.2 %copy-start.20 = (f32[512,512]{1,0:T(8,128)S(1)}, f32[512,512]{1,0:T(8,128)}, u32[]{:S(2)}) copy-start(f32[512,512]{1,0:T(8,128)} %copy-done.19) | copy-start | bytes 3145732
  176.0 4.2 %copy-start.22 = (f32[512,512]{1,0:T(8,128)S(1)}, f32[512,512]{1,0:T(8,128)}, u32[]{:S(2)}) copy-start(f32[512,512]{1,0:T(8,128)} %copy-done.21) | copy-start | bytes 3145732

commit v6 on v5

--- a/solution.py
+++ b/solution.py
@@ -79,8 +79,13 @@
     other = other.reshape(half_slots, 2 * model_width)
     oth_x = other[:, :model_width]
     oth_cot = other[:, model_width:]
-    oth_h, oth_dg, oth_du, oth_dx = front_rows(oth_x, oth_cot, *weights_own)
-    back = lax.ppermute(oth_dx, "dp", swap)
+    oth_h, oth_dg, oth_du = front_rows(oth_x, oth_cot, *weights_own)[:3]
+    split = half_slots // 2
+    dx_first = input_grads(oth_dg[:split], oth_du[:split], weights_own[0], weights_own[1])
+    back_first = lax.ppermute(dx_first, "dp", swap)
+    dx_second = input_grads(oth_dg[split:], oth_du[split:], weights_own[0], weights_own[1])
+    back_second = lax.ppermute(dx_second, "dp", swap)
+    back = jnp.concatenate([back_first, back_second], axis=0)
     own_dx = lax.dot_general(
         own_dg, weights_own[0], (((1,), (1,)), ((), ())), preferred_element_type=jnp.float32
     )
@@ -94,8 +99,10 @@
     sums_own = weight_sums(own_x, own_cot, own_h, own_dg, own_du)
     sums_oth = weight_sums(oth_x, oth_cot, oth_h, oth_dg, oth_du)
     grad_gate, grad_up, grad_down = (a + b for a, b in zip(sums_own, sums_oth))
-    gathering = (position[:, None] == jnp.arange(owners * capacity, dtype=jnp.int32)[None, :]).astype(
-        jnp.bfloat16
+    gathering = lax.optimization_barrier(
+        (position[:, None] == jnp.arange(owners * capacity, dtype=jnp.int32)[None, :]).astype(
+            jnp.bfloat16
+        )
     )
     copy_grad = jnp.dot(
         gathering,

time: 207 us -> 205 us (level)
  waiting for transfers between devices: 29.3 us -> 26.1 us
    ppermute x1, waiting for transfers between devices: 11.3 us -> 9.08 us  [local(): other = lax.ppermute(came, 'dp', swap)]
  transfers between devices with their start and end apart: 3 -> 4, of which waited for: 2 -> 2; matrix products, arithmetic and copies ran while one was open for 19% -> 20% of each run, Pallas kernels for 0% -> 0%
where the time goes in v6:
time: 205 us; the launch traced here: 204 us
  blocking collectives  97.2 us (47%)
  matrix products  61.7 us (30%)
  waiting for transfers between devices  26.1 us (13%)
  starting transfers between devices  10.2 us (5%)
  other arithmetic  5 us (2%)
  local copies, waits for them, and re-layouts  3.27 us (2%)
    all_to_all x1, blocking collectives, local(): lax.all_to_all(sent, 'expert', split_axis=0, concat_axis=0, tiled=True)  97.2 us
    all_to_all x1, waiting for transfers between devices, local(): lax.all_to_all(summed.reshape(owners, capacity, model_width), 'expert', s...  17 us
    dot_general x2, matrix products, weight_sums(): lax.dot_general(rows_x, d_up, (((0,), (0,)), ((), ())), preferred_element...  14.7 us
    dot_general x2, matrix products, weight_sums(): lax.dot_general(rows_x, d_gate, (((0,), (0,)), ((), ())), preferred_eleme...  9.32 us
    ppermute x1, waiting for transfers between devices, local(): other = lax.ppermute(came, 'dp', swap)  9.08 us
    dot_general x2, matrix products, weight_sums(): lax.dot_general(hidden, rows_cot, (((0,), (0,)), ((), ())), preferred_ele...  6.45 us
    all_to_all x1, starting transfers between devices, local(): lax.all_to_all(summed.reshape(owners, capacity, model_width), 'expert', s...  6.09 us
    dot_general x2, matrix products, front_rows(): gate_pre = jnp.dot(rows_x, gate_w, preferred_element_type=jnp.float32)  5.41 us
  transfers between devices with their start and end apart: 4, of which 2 were waited for; matrix products, arithmetic and copies ran while one was open for 20% of the time, Pallas kernels for 0%

profile of v6, /device:TPU:1, one launch (start us, length us, event | category | flops | bytes accessed | tf_op | source)
XLA Modules:
  0.0 204.5 jit_solution(5227593446462653254)
XLA Ops:
  0.6 0.0 copy-start.3
  0.6 0.8 fusion.63
  1.5 0.6 reduce-window.6
  2.1 0.2 slice_reduce_fusion
  2.3 0.8 fusion.62
  3.1 0.7 multiply_add_fusion
  3.8 1.9 multiply_convert_fusion
  5.7 0.0 copy-done.3
  5.7 2.5 %fusion = bf16[64,8,7168]{2,1,0:T(8,128)(2,1)S(1)} fusion(bf16[256,3584]{1,0:T(8,128)(2,1)S(1)} %multiply_convert_fusion, bf16[256,3584]{1,0:T(8,128)(2,1)S(1)} %copy-done.3, s32[256]{0:T(256)S(1)} %multiply_add_fusion), kind=kOutput, calls=%fused_computation.1 | convolution fusion | flops 1890189312 | bytes 11011072 | tf_op jit(solution)/shard_map/dot_general | solution.py:66
  8.2 0.0 copy-start.14
  8.3 0.0 copy-start
  8.3 97.2 %all_to_all.10 = bf16[64,8,7168]{2,1,0:T(8,128)(2,1)S(1)} all-to-all(bf16[64,8,7168]{2,1,0:T(8,128)(2,1)S(1)} %fusion), channel_id=1, replica_groups=mesh['dp'=2,'expert'=64] {'expert'}, dimensions={0} | all-to-all | bytes 14680064 | tf_op jit(solution)/shard_map/all_to_all | solution.py:70
  105.5 3.3 %collective-permute-start = (bf16[64,8,7168]{2,1,0:T(8,128)(2,1)S(1)}, bf16[64,8,7168]{2,1,0:T(8,128)(2,1)S(1)}, u32[]{:S(2)}, u32[]{:S(2)}) collective-permute-start(bf16[64,8,7168]{2,1,0:T(8,128)(2,1)S(1)} %all_to_all.10), channel_id=1, source_target_pairs={{0,64},{64,0},{1,65},{65,1},{2,66},{66,2},{3,67},{67,3},{4,68},{68... | collective-permute-start | bytes 22020104 | tf_op jit(solution)/shard_map/ppermute | solution.py:72
  108.7 0.0 copy-done.14
  108.7 0.1 fusion.52
  108.9 2.1 %fusion.29 = f32[512,512]{1,0:T(8,128)S(1)} fusion(bf16[1,3584,512]{2,1,0:T(8,128)(2,1)S(1)} %copy-done, bf16[512,7168]{1,0:T(8,128)(2,1)S(1)} %bitcast.79), kind=kOutput, calls=%fused_computation.35 | convolution fusion | flops 1879048192 | bytes 8388608 | tf_op jit(solution)/shard_map/dot_general | solution.py:9
  110.9 0.0 copy-start.4
  110.9 9.1 %collective-permute-done = bf16[64,8,7168]{2,1,0:T(8,128)(2,1)S(1)} collective-permute-done((bf16[64,8,7168]{2,1,0:T(8,128)(2,1)S(1)}, bf16[64,8,7168]{2,1,0:T(8,128)(2,1)S(1)}, u32[]{:S(2)}, u32[]{:S(2)}) %collective-permute-start) | collective-permute-done | bytes 7340064 | tf_op jit(solution)/shard_map/ppermute | solution.py:72
  120.0 2.1 %fusion.25 = f32[512,512]{1,0:T(8,128)S(1)} fusion(bf16[1,3584,512]{2,1,0:T(8,128)(2,1)S(1)} %copy-done, bf16[512,7168]{1,0:T(8,128)(2,1)S(1)} %bitcast.93), kind=kOutput, calls=%fused_computation.31 | convolution fusion | flops 1879048192 | bytes 8388608 | tf_op jit(solution)/shard_map/dot_general | solution.py:9
  122.1 2.6 %copy-done.1 = bf16[1,3584,512]{2,1,0:T(8,128)(2,1)S(1)} copy-done((bf16[1,3584,512]{2,1,0:T(8,128)(2,1)S(1)}, bf16[1,3584,512]{2,1,0:T(8,128)(2,1)}, u32[]{:S(2)}) %copy-start.1) | copy-done | bytes 3670040
  124.7 2.1 %fusion.15 = f32[512,512]{1,0:T(8,128)S(1)} fusion(bf16[1,3584,512]{2,1,0:T(8,128)(2,1)S(1)} %copy-done.1, bf16[512,7168]{1,0:T(8,128)(2,1)S(1)} %bitcast.94), kind=kOutput, calls=%fused_computation.23 | convolution fusion | flops 1879048192 | bytes 8388608 | tf_op jit(solution)/shard_map/dot_general | solution.py:8
  126.8 0.3 copy-done.16
  127.1 2.4 %multiply_convert_fusion.3 = (bf16[512,512]{1,0:T(8,128)(2,1)S(1)}, bf16[512,512]{1,0:T(8,128)(2,1)S(1)}) fusion(f32[512,512]{1,0:T(8,128)S(1)} %fusion.15, f32[512,512]{1,0:T(8,128)S(1)} %fusion.25, bf16[1,512,3584]{2,1,0:T(8,128)(2,1)S(1)} %copy-done.16, bf16[512,7168]{1,0:T(8,128)(2,1)S(1)} %bitcast.95), kind=kOutput, calls=%fused_computation.59 | convolution fusion | flops 1882456064 | bytes 10485760 | tf_op jit(solution)/shard_map/dot_general | solution.py:13
  129.5 0.0 copy-done.19
  129.5 0.0 copy-start.12
  129.6 1.1 fusion.13
  130.7 1.1 fusion.11
  131.9 1.2 fusion.4
  133.0 0.6 collective-permute-start.1
  133.7 0.0 copy-done.7
  133.7 1.1 fusion.5
  134.8 0.2 collective-permute-start.2
  135.0 2.1 %fusion.33 = f32[512,512]{1,0:T(8,128)S(1)} fusion(bf16[1,512,3584]{2,1,0:T(8,128)(2,1)S(1)} %copy-done.16, bf16[512,7168]{1,0:T(8,128)(2,1)S(1)} %bitcast.80), kind=kOutput, calls=%fused_computation.39 | convolution fusion | flops 1879048192 | bytes 8388608 | tf_op jit(solution)/shard_map/dot_general | solution.py:13
  137.1 0.0 copy-done.2
  137.1 0.0 copy-done.4
  137.2 3.4 %multiply_convert_fusion.6 = (bf16[512,512]{1,0:T(8,128)(2,1)S(1)}, bf16[512,512]{1,0:T(8,128)(2,1)S(1)}, f32[512,512]{1,0:T(8,128)}) fusion(f32[512,512]{1,0:T(8,128)S(1)} %fusion.33, f32[512,512]{1,0:T(8,128)S(1)} %fusion.29, bf16[1,3584,512]{2,1,0:T(8,128)(2,1)S(1)} %copy-done.1, bf16[512,7168]{1,0:T(8,128)(2,1)S(1)} %bitcast.81), kind=kOutput, calls=%fused_computation.64 | convolution fusion | flops 1882456064 | bytes 11534336 | tf_op jit(solution)/shard_map/dot_general | solution.py:8
  140.5 2.1 %fusion.27 = f32[512,3584]{1,0:T(8,128)S(1)} fusion(bf16[512,512]{1,0:T(8,128)(2,1)S(1)} %get-tuple-element.5, bf16[1,3584,512]{2,1,0:T(8,128)(2,1)S(1)} %copy-done), kind=kOutput, calls=%fused_computation.33 | convolution fusion | flops 1879048192 | bytes 11534336 | tf_op jit(solution)/shard_map/dot_general | solution.py:92
  142.6 0.0 collective-permute-done.1
  142.6 0.0 collective-permute-done.2
  142.6 0.0 copy-done.9
  142.7 3.7 %fusion.6 = bf16[64,8,3584]{2,1,0:T(8,128)(2,1)} fusion(f32[512,3584]{1,0:T(8,128)S(1)} %fusion.27, bf16[256,3584]{1,0:T(8,128)(2,1)S(1)} %collective-permute-done.2, bf16[256,3584]{1,0:T(8,128)(2,1)S(1)} %collective-permute-done.1, bf16[512,512]{1,0:T(8,128)(2,1)S(1)} %get-tuple-element.4, bf16[1,3584,512]{2,1,0:T(8,128)(2,1)S(1)} %copy-done.1), kind=kOutput, calls=%fused_computation.14 | convolution fusion | flops 1891893248 | bytes 18874368 | tf_op jit(solution)/shard_map/dot_general | solution.py:89
  146.4 6.1 %all-to-all-start.1 = ((bf16[64,8,3584]{2,1,0:T(8,128)(2,1)}), bf16[64,8,3584]{2,1,0:T(8,128)(2,1)}, u32[]{:S(2)}, u32[]{:S(2)}) async-start(bf16[64,8,3584]{2,1,0:T(8,128)(2,1)} %fusion.6), calls=%async_computation.1 | async-start | bytes 7340032 | tf_op jit(solution)/shard_map/all_to_all | solution.py:96
  152.5 0.0 slice-start.1
  152.5 0.0 copy-start.10
  152.5 0.0 slice-start.2
  152.5 7.4 %fusion.44 = f32[3584,512]{1,0:T(8,128)} fusion(bf16[512,512]{1,0:T(8,128)(2,1)} %copy-done.11, bf16[512,7168]{1,0:T(8,128)(2,1)} %bitcast.82), kind=kOutput, calls=%fused_computation.51 | convolution fusion | flops 1879048192 | bytes 11534336 | tf_op jit(solution)/shard_map/dot_general | solution.py:37
  159.9 0.0 slice-done
  159.9 0.0 copy-start.5
  159.9 0.0 copy-start.6
  159.9 0.0 slice-start.3
  159.9 5.1 %fusion.46 = f32[3584,512]{1,0:T(8,128)} fusion(bf16[512,512]{1,0:T(8,128)(2,1)S(1)} %copy-done.10, bf16[512,7168]{1,0:T(8,128)(2,1)S(1)} %bitcast.85), kind=kOutput, calls=%fused_computation.53 | convolution fusion | flops 1879048192 | bytes 11534336 | tf_op jit(solution)/shard_map/dot_general | solution.py:34
  165.1 2.2 %fusion.37 = f32[512,3584]{1,0:T(8,128)S(1)} fusion(bf16[512,7168]{1,0:T(8,128)(2,1)S(1)} %bitcast.86, f32[512,512]{1,0:T(8,128)S(1)} %copy-done.5, f32[512,512]{1,0:T(8,128)S(1)} %copy-done.6), kind=kOutput, calls=%fused_computation.44 | convolution fusion | flops 1880621056 | bytes 13107200 | tf_op jit(solution)/shard_map/dot_general | solution.py:40
  167.3 0.0 slice-done.2
  167.3 0.0 slice-done.3
  167.3 0.0 copy-done.8
  167.3 0.0 copy-start.13
  167.3 0.0 slice-start.5
  167.3 7.3 %fusion.2 = bf16[1,3584,512]{2,1,0:T(8,128)(2,1)} fusion(f32[3584,512]{1,0:T(8,128)} %fusion.44, bf16[512,512]{1,0:T(8,128)(2,1)S(1)} %copy-done.8, bf16[512,7168]{1,0:T(8,128)(2,1)S(1)} %bitcast.98), kind=kOutput, calls=%fused_computation.9 | convolution fusion | flops 1882718208 | bytes 15204352 | tf_op jit(solution)/shard_map/dot_general | solution.py:37
  174.7 0.0 copy-start.18
  174.7 0.0 copy-start.20
  174.7 4.2 %fusion.1 = bf16[1,3584,512]{2,1,0:T(8,128)(2,1)} fusion(f32[3584,512]{1,0:T(8,128)S(1)} %bitcast.102, bf16[512,512]{1,0:T(8,128)(2,1)S(1)} %copy-done.13, bf16[512,7168]{1,0:T(8,128)(2,1)S(1)} %bitcast.99), kind=kOutput, calls=%fused_computation.8 | convolution fusion | flops 1882718208 | bytes 15204352 | tf_op jit(solution)/shard_map/dot_general | solution.py:34
  178.9 4.3 %fusion.3 = bf16[1,512,3584]{2,1,0:T(8,128)(2,1)} fusion(f32[512,3584]{1,0:T(8,128)S(1)} %fusion.37, bf16[512,7168]{1,0:T(8,128)(2,1)S(1)} %bitcast.100, f32[512,512]{1,0:T(8,128)S(1)} %copy-done.18, f32[512,512]{1,0:T(8,128)S(1)} %copy-done.20), kind=kOutput, calls=%fused_computation.10 | convolution fusion | flops 1884291072 | bytes 16777216 | tf_op jit(solution)/shard_map/dot_general | solution.py:40
  183.1 17.0 %all-to-all-done.1 = bf16[64,8,3584]{2,1,0:T(8,128)(2,1)} async-done(((bf16[64,8,3584]{2,1,0:T(8,128)(2,1)}), bf16[64,8,3584]{2,1,0:T(8,128)(2,1)}, u32[]{:S(2)}, u32[]{:S(2)}) %all-to-all-start.1) | async-done | bytes 3670048 | tf_op jit(solution)/shard_map/all_to_all | solution.py:96
  200.1 4.4 %convolution_convert_fusion.1 = bf16[256,3584]{1,0:T(8,128)(2,1)} fusion(bf16[256,512]{1,0:T(8,128)(2,1)S(1)} %fusion.52, bf16[64,8,3584]{2,1,0:T(8,128)(2,1)} %all-to-all-done.1), kind=kOutput, calls=%fused_computation.13 | convolution fusion | flops 940441600 | bytes 5767168 | tf_op jit(solution)/shard_map/dot_general | solution.py:107
  (32 shorter events, 0.1 us)
Async XLA Ops:
  0.6 5.1 %copy-start.3 = (bf16[256,3584]{1,0:T(8,128)(2,1)S(1)}, bf16[256,3584]{1,0:T(8,128)(2,1)}, u32[]{:S(2)}) copy-start(bf16[256,3584]{1,0:T(8,128)(2,1)} %param.7) | copy-start | bytes 5505028
  8.2 100.5 %copy-start.14 = (s32[256,1]{0,1:T(1,128)S(1)}, s32[256,1]{0,1:T(1,128)}, u32[]{:S(2)}) copy-start(s32[256,1]{0,1:T(1,128)} %param.9) | copy-start | bytes 3076
  8.3 100.6 %copy-start = (bf16[1,3584,512]{2,1,0:T(8,128)(2,1)S(1)}, bf16[1,3584,512]{2,1,0:T(8,128)(2,1)}, u32[]{:S(2)}) copy-start(bf16[1,3584,512]{2,1,0:T(8,128)(2,1)} %param.12) | copy-start | bytes 11010052
  105.5 31.7 %copy-start.2 = (bf16[64,8,7168]{2,1,0:T(8,128)(2,1)}, bf16[64,8,7168]{2,1,0:T(8,128)(2,1)S(1)}, u32[]{:S(2)}) copy-start(bf16[64,8,7168]{2,1,0:T(8,128)(2,1)S(1)} %all_to_all.10) | copy-start | bytes 22020100
  105.5 14.5 %collective-permute-start = (bf16[64,8,7168]{2,1,0:T(8,128)(2,1)S(1)}, bf16[64,8,7168]{2,1,0:T(8,128)(2,1)S(1)}, u32[]{:S(2)}, u32[]{:S(2)}) collective-permute-start(bf16[64,8,7168]{2,1,0:T(8,128)(2,1)S(1)} %all_to_all.10), channel_id=1, source_target_pairs={{0,64},{64,0},{1,65},{65,1},{2,66},{66,2},{3,67},{67,3},{4,68},{68... | collective-permute-start | bytes 22020104 | tf_op jit(solution)/shard_map/ppermute | solution.py:72
  110.9 26.2 %copy-start.4 = (f32[512,512]{1,0:T(8,128)}, f32[512,512]{1,0:T(8,128)S(1)}, u32[]{:S(2)}) copy-start(f32[512,512]{1,0:T(8,128)S(1)} %fusion.29) | copy-start | bytes 3145732
  120.0 6.8 %copy-start.15 = (bf16[64,8,7168]{2,1,0:T(8,128)(2,1)}, bf16[64,8,7168]{2,1,0:T(8,128)(2,1)S(1)}, u32[]{:S(2)}) copy-start(bf16[64,8,7168]{2,1,0:T(8,128)(2,1)S(1)} %collective-permute-done) | copy-start | bytes 22020100
  120.0 4.7 %copy-start.1 = (bf16[1,3584,512]{2,1,0:T(8,128)(2,1)S(1)}, bf16[1,3584,512]{2,1,0:T(8,128)(2,1)}, u32[]{:S(2)}) copy-start(bf16[1,3584,512]{2,1,0:T(8,128)(2,1)} %param.11) | copy-start | bytes 11010052
  124.7 2.1 %copy-start.17 = (f32[512,512]{1,0:T(8,128)}, f32[512,512]{1,0:T(8,128)S(1)}, u32[]{:S(2)}) copy-start(f32[512,512]{1,0:T(8,128)S(1)} %fusion.25) | copy-start | bytes 3145732
  124.7 2.4 %copy-start.16 = (bf16[1,512,3584]{2,1,0:T(8,128)(2,1)S(1)}, bf16[1,512,3584]{2,1,0:T(8,128)(2,1)}, u32[]{:S(2)}) copy-start(bf16[1,512,3584]{2,1,0:T(8,128)(2,1)} %param.13) | copy-start | bytes 11010052
  127.1 2.4 %copy-start.19 = (f32[512,512]{1,0:T(8,128)}, f32[512,512]{1,0:T(8,128)S(1)}, u32[]{:S(2)}) copy-start(f32[512,512]{1,0:T(8,128)S(1)} %fusion.15) | copy-start | bytes 3145732
  129.5 1.2 copy-start.12
  129.6 4.1 %copy-start.7 = (bf16[512,512]{1,0:T(8,128)(2,1)}, bf16[512,512]{1,0:T(8,128)(2,1)S(1)}, u32[]{:S(2)}) copy-start(bf16[512,512]{1,0:T(8,128)(2,1)S(1)} %get-tuple-element.6) | copy-start | bytes 1572868
  133.0 9.6 %collective-permute-start.1 = (bf16[256,3584]{1,0:T(8,128)(2,1)S(1)}, bf16[256,3584]{1,0:T(8,128)(2,1)S(1)}, u32[]{:S(2)}, u32[]{:S(2)}) collective-permute-start(bf16[256,3584]{1,0:T(8,128)(2,1)S(1)} %fusion.4), channel_id=1, source_target_pairs={{0,64},{64,0},{1,65},{65,1},{2,66},{66,2},{3,67},{67,3},{4,68},{68... | collective-permute-start | bytes 5505032 | tf_op jit(solution)/shard_map/ppermute | solution.py:85
  134.8 7.8 %collective-permute-start.2 = (bf16[256,3584]{1,0:T(8,128)(2,1)S(1)}, bf16[256,3584]{1,0:T(8,128)(2,1)S(1)}, u32[]{:S(2)}, u32[]{:S(2)}) collective-permute-start(bf16[256,3584]{1,0:T(8,128)(2,1)S(1)} %fusion.5), channel_id=1, source_target_pairs={{0,64},{64,0},{1,65},{65,1},{2,66},{66,2},{3,67},{67,3},{4,68},{68... | collective-permute-start | bytes 5505032 | tf_op jit(solution)/shard_map/ppermute | solution.py:87
  140.5 2.1 %copy-start.11 = (bf16[512,512]{1,0:T(8,128)(2,1)}, bf16[512,512]{1,0:T(8,128)(2,1)S(1)}, u32[]{:S(2)}) copy-start(bf16[512,512]{1,0:T(8,128)(2,1)S(1)} %get-tuple-element.5) | copy-start | bytes 1572868
  140.5 2.1 %copy-start.9 = (bf16[512,512]{1,0:T(8,128)(2,1)}, bf16[512,512]{1,0:T(8,128)(2,1)S(1)}, u32[]{:S(2)}) copy-start(bf16[512,512]{1,0:T(8,128)(2,1)S(1)} %get-tuple-element.4) | copy-start | bytes 1572868
  146.4 13.5 %slice-start = ((s8[7340032]{0:T(1024)(128)(4,1)}), s8[3145728]{0:T(1024)(128)(4,1)S(1)}, s32[]{:S(2)}) async-start(s8[7340032]{0:T(1024)(128)(4,1)} %bitcast.83), calls=%async_computation.2 | async-start | bytes 6291456
  146.4 53.7 %all-to-all-start.1 = ((bf16[64,8,3584]{2,1,0:T(8,128)(2,1)}), bf16[64,8,3584]{2,1,0:T(8,128)(2,1)}, u32[]{:S(2)}, u32[]{:S(2)}) async-start(bf16[64,8,3584]{2,1,0:T(8,128)(2,1)} %fusion.6), calls=%async_computation.1 | async-start | bytes 7340032 | tf_op jit(solution)/shard_map/all_to_all | solution.py:96
  152.5 7.4 %slice-start.1 = ((s8[7340032]{0:T(1024)(128)(4,1)}), s8[4194304]{0:T(1024)(128)(4,1)S(1)}, s32[]{:S(2)}) async-start(s8[7340032]{0:T(1024)(128)(4,1)} %bitcast.83), calls=%async_computation.3 | async-start | bytes 8388608
  152.5 7.4 %copy-start.10 = (bf16[512,512]{1,0:T(8,128)(2,1)S(1)}, bf16[512,512]{1,0:T(8,128)(2,1)}, u32[]{:S(2)}) copy-start(bf16[512,512]{1,0:T(8,128)(2,1)} %copy-done.9) | copy-start | bytes 1572868
  152.5 14.8 %slice-start.2 = ((s8[7340032]{0:T(1024)(128)(4,1)}), s8[4194304]{0:T(1024)(128)(4,1)S(1)}, s32[]{:S(2)}) async-start(s8[7340032]{0:T(1024)(128)(4,1)} %bitcast.96), calls=%async_computation.4 | async-start | bytes 8388608
  159.9 5.2 %copy-start.5 = (f32[512,512]{1,0:T(8,128)S(1)}, f32[512,512]{1,0:T(8,128)}, u32[]{:S(2)}) copy-start(f32[512,512]{1,0:T(8,128)} %copy-done.4) | copy-start | bytes 3145732
  159.9 5.2 %copy-start.6 = (f32[512,512]{1,0:T(8,128)S(1)}, f32[512,512]{1,0:T(8,128)}, u32[]{:S(2)}) copy-start(f32[512,512]{1,0:T(8,128)} %get-tuple-element.8) | copy-start | bytes 3145732
  159.9 7.4 %slice-start.3 = ((s8[7340032]{0:T(1024)(128)(4,1)}), s8[3145728]{0:T(1024)(128)(4,1)S(1)}, s32[]{:S(2)}) async-start(s8[7340032]{0:T(1024)(128)(4,1)} %bitcast.96), calls=%async_computation.5 | async-start | bytes 6291456
  165.1 2.2 %copy-start.8 = (bf16[512,512]{1,0:T(8,128)(2,1)S(1)}, bf16[512,512]{1,0:T(8,128)(2,1)}, u32[]{:S(2)}) copy-start(bf16[512,512]{1,0:T(8,128)(2,1)} %copy-done.7) | copy-start | bytes 1572868
  165.1 9.6 %slice-start.4 = ((s8[7340032]{0:T(1024)(128)(4,1)}), s8[4194304]{0:T(1024)(128)(4,1)S(1)}, s32[]{:S(2)}) async-start(s8[7340032]{0:T(1024)(128)(4,1)} %bitcast.101), calls=%async_computation.6 | async-start | bytes 8388608
  167.3 7.3 %copy-start.13 = (bf16[512,512]{1,0:T(8,128)(2,1)S(1)}, bf16[512,512]{1,0:T(8,128)(2,1)}, u32[]{:S(2)}) copy-start(bf16[512,512]{1,0:T(8,128)(2,1)} %copy-done.12) | copy-start | bytes 1572868
  167.3 7.3 %slice-start.5 = ((s8[7340032]{0:T(1024)(128)(4,1)}), s8[3145728]{0:T(1024)(128)(4,1)S(1)}, s32[]{:S(2)}) async-start(s8[7340032]{0:T(1024)(128)(4,1)} %bitcast.101), calls=%async_computation.7 | async-start | bytes 6291456
  174.7 4.2 %copy-start.18 = (f32[512,512]{1,0:T(8,128)S(1)}, f32[512,512]{1,0:T(8,128)}, u32[]{:S(2)}) copy-start(f32[512,512]{1,0:T(8,128)} %copy-done.17) | copy-start | bytes 3145732
  174.7 4.2 %copy-start.20 = (f32[512,512]{1,0:T(8,128)S(1)}, f32[512,512]{1,0:T(8,128)}, u32[]{:S(2)}) copy-start(f32[512,512]{1,0:T(8,128)} %copy-done.19) | copy-start | bytes 3145732

commit v7 on v6

--- a/solution.py
+++ b/solution.py
@@ -51,9 +51,11 @@
     capacity = max(2, 2 * tok_rows * fanout // owners)
     copies = tok_rows * fanout
     flat_ids = expert_ids.reshape(copies)
-    onehot = (flat_ids[:, None] == jnp.arange(owners, dtype=jnp.int32)[None, :]).astype(jnp.int32)
-    before = jnp.cumsum(onehot, axis=0) - onehot
-    slot_rank = jnp.sum(before * onehot, axis=1)
+    onehot = (flat_ids[:, None] == jnp.arange(owners, dtype=jnp.int32)[None, :]).astype(jnp.bfloat16)
+    order = jnp.arange(copies, dtype=jnp.int32)
+    earlier = (order[None, :] < order[:, None]).astype(jnp.bfloat16)
+    before = jnp.dot(earlier, onehot, preferred_element_type=jnp.float32)
+    slot_rank = jnp.sum(before * onehot.astype(jnp.float32), axis=1).astype(jnp.int32)
     position = flat_ids * capacity + slot_rank
     copy_rows = tokens[:, None, :].reshape(copies, model_width)
     copy_tok_cot = cotangent[:, None, :].reshape(copies, model_width)

time: 205 us -> 204 us (level)
  other arithmetic: 5 us -> 2.76 us
where the time goes in v7:
time: 204 us; the launch traced here: 203 us
  blocking collectives  97.2 us (48%)
  matrix products  62.9 us (31%)
  waiting for transfers between devices  26 us (13%)
  starting transfers between devices  10.2 us (5%)
  local copies, waits for them, and re-layouts  3.08 us (2%)
  other arithmetic  2.76 us (1%)
    all_to_all x1, blocking collectives, local(): lax.all_to_all(sent, 'expert', split_axis=0, concat_axis=0, tiled=True)  97.2 us
    all_to_all x1, waiting for transfers between devices, local(): lax.all_to_all(summed.reshape(owners, capacity, model_width), 'expert', s...  16.9 us
    dot_general x2, matrix products, weight_sums(): lax.dot_general(rows_x, d_up, (((0,), (0,)), ((), ())), preferred_element...  14.7 us
    dot_general x2, matrix products, weight_sums(): lax.dot_general(rows_x, d_gate, (((0,), (0,)), ((), ())), preferred_eleme...  9.31 us
    ppermute x1, waiting for transfers between devices, local(): other = lax.ppermute(came, 'dp', swap)  9.08 us
    dot_general x2, matrix products, weight_sums(): lax.dot_general(hidden, rows_cot, (((0,), (0,)), ((), ())), preferred_ele...  6.53 us
    all_to_all x1, starting transfers between devices, local(): lax.all_to_all(summed.reshape(owners, capacity, model_width), 'expert', s...  6.09 us
    dot_general x2, matrix products, front_rows(): gate_pre = jnp.dot(rows_x, gate_w, preferred_element_type=jnp.float32)  5.41 us
  transfers between devices with their start and end apart: 4, of which 2 were waited for; matrix products, arithmetic and copies ran while one was open for 20% of the time, Pallas kernels for 0%

profile of v7, /device:TPU:1, one launch (start us, length us, event | category | flops | bytes accessed | tf_op | source)
XLA Modules:
  0.0 203.1 jit_solution(4695330913693448611)
XLA Ops:
  0.6 0.0 copy-start.3
  0.6 1.0 fusion.50
  1.7 0.7 multiply_add_fusion
  2.4 1.9 multiply_convert_fusion
  4.3 0.0 copy-done.3
  4.3 2.6 %fusion = bf16[64,8,7168]{2,1,0:T(8,128)(2,1)S(1)} fusion(bf16[256,3584]{1,0:T(8,128)(2,1)S(1)} %multiply_convert_fusion, bf16[256,3584]{1,0:T(8,128)(2,1)S(1)} %copy-done.3, s32[256]{0:T(256)S(1)} %multiply_add_fusion), kind=kOutput, calls=%fused_computation.1 | convolution fusion | flops 1890189312 | bytes 11011072 | tf_op jit(solution)/shard_map/dot_general | solution.py:68
  6.9 0.0 copy-start.14
  6.9 0.0 copy-start
  6.9 97.2 %all_to_all.10 = bf16[64,8,7168]{2,1,0:T(8,128)(2,1)S(1)} all-to-all(bf16[64,8,7168]{2,1,0:T(8,128)(2,1)S(1)} %fusion), channel_id=1, replica_groups=mesh['dp'=2,'expert'=64] {'expert'}, dimensions={0} | all-to-all | bytes 14680064 | tf_op jit(solution)/shard_map/all_to_all | solution.py:72
  104.1 3.3 %collective-permute-start = (bf16[64,8,7168]{2,1,0:T(8,128)(2,1)S(1)}, bf16[64,8,7168]{2,1,0:T(8,128)(2,1)S(1)}, u32[]{:S(2)}, u32[]{:S(2)}) collective-permute-start(bf16[64,8,7168]{2,1,0:T(8,128)(2,1)S(1)} %all_to_all.10), channel_id=1, source_target_pairs={{0,64},{64,0},{1,65},{65,1},{2,66},{66,2},{3,67},{67,3},{4,68},{68... | collective-permute-start | bytes 22020104 | tf_op jit(solution)/shard_map/ppermute | solution.py:74
  107.4 0.0 copy-done.14
  107.4 0.1 fusion.53
  107.5 0.0 copy-done
  107.5 2.1 %fusion.29 = f32[512,512]{1,0:T(8,128)S(1)} fusion(bf16[1,3584,512]{2,1,0:T(8,128)(2,1)S(1)} %copy-done, bf16[512,7168]{1,0:T(8,128)(2,1)S(1)} %bitcast.59), kind=kOutput, calls=%fused_computation.35 | convolution fusion | flops 1879048192 | bytes 8388608 | tf_op jit(solution)/shard_map/dot_general | solution.py:9
  109.6 0.0 copy-start.4
  109.6 9.1 %collective-permute-done = bf16[64,8,7168]{2,1,0:T(8,128)(2,1)S(1)} collective-permute-done((bf16[64,8,7168]{2,1,0:T(8,128)(2,1)S(1)}, bf16[64,8,7168]{2,1,0:T(8,128)(2,1)S(1)}, u32[]{:S(2)}, u32[]{:S(2)}) %collective-permute-start) | collective-permute-done | bytes 7340064 | tf_op jit(solution)/shard_map/ppermute | solution.py:74
  118.7 2.1 %fusion.25 = f32[512,512]{1,0:T(8,128)S(1)} fusion(bf16[1,3584,512]{2,1,0:T(8,128)(2,1)S(1)} %copy-done, bf16[512,7168]{1,0:T(8,128)(2,1)S(1)} %bitcast.72), kind=kOutput, calls=%fused_computation.31 | convolution fusion | flops 1879048192 | bytes 8388608 | tf_op jit(solution)/shard_map/dot_general | solution.py:9
  120.7 2.6 %copy-done.1 = bf16[1,3584,512]{2,1,0:T(8,128)(2,1)S(1)} copy-done((bf16[1,3584,512]{2,1,0:T(8,128)(2,1)S(1)}, bf16[1,3584,512]{2,1,0:T(8,128)(2,1)}, u32[]{:S(2)}) %copy-start.1) | copy-done | bytes 3670040
  123.4 2.1 %fusion.15 = f32[512,512]{1,0:T(8,128)S(1)} fusion(bf16[1,3584,512]{2,1,0:T(8,128)(2,1)S(1)} %copy-done.1, bf16[512,7168]{1,0:T(8,128)(2,1)S(1)} %bitcast.73), kind=kOutput, calls=%fused_computation.23 | convolution fusion | flops 1879048192 | bytes 8388608 | tf_op jit(solution)/shard_map/dot_general | solution.py:8
  125.4 0.0 copy-done.15
  125.4 0.0 copy-done.17
  125.4 0.3 copy-done.16
  125.8 2.4 %multiply_convert_fusion.3 = (bf16[512,512]{1,0:T(8,128)(2,1)S(1)}, bf16[512,512]{1,0:T(8,128)(2,1)S(1)}) fusion(f32[512,512]{1,0:T(8,128)S(1)} %fusion.15, f32[512,512]{1,0:T(8,128)S(1)} %fusion.25, bf16[1,512,3584]{2,1,0:T(8,128)(2,1)S(1)} %copy-done.16, bf16[512,7168]{1,0:T(8,128)(2,1)S(1)} %bitcast.74), kind=kOutput, calls=%fused_computation.61 | convolution fusion | flops 1882456064 | bytes 10485760 | tf_op jit(solution)/shard_map/dot_general | solution.py:13
  128.2 0.0 copy-done.19
  128.2 0.0 copy-start.12
  128.2 0.0 copy-start.7
  128.2 1.1 fusion.13
  129.4 0.0 copy-done.12
  129.4 1.1 fusion.11
  130.5 1.2 fusion.4
  131.7 0.6 collective-permute-start.1
  132.3 0.0 copy-done.7
  132.3 1.2 fusion.5
  133.5 0.2 collective-permute-start.2
  133.7 2.1 %fusion.33 = f32[512,512]{1,0:T(8,128)S(1)} fusion(bf16[1,512,3584]{2,1,0:T(8,128)(2,1)S(1)} %copy-done.16, bf16[512,7168]{1,0:T(8,128)(2,1)S(1)} %bitcast.60), kind=kOutput, calls=%fused_computation.39 | convolution fusion | flops 1879048192 | bytes 8388608 | tf_op jit(solution)/shard_map/dot_general | solution.py:13
  135.8 0.0 copy-done.2
  135.8 0.0 copy-done.4
  135.8 3.4 %multiply_convert_fusion.6 = (bf16[512,512]{1,0:T(8,128)(2,1)S(1)}, bf16[512,512]{1,0:T(8,128)(2,1)S(1)}, f32[512,512]{1,0:T(8,128)}) fusion(f32[512,512]{1,0:T(8,128)S(1)} %fusion.33, f32[512,512]{1,0:T(8,128)S(1)} %fusion.29, bf16[1,3584,512]{2,1,0:T(8,128)(2,1)S(1)} %copy-done.1, bf16[512,7168]{1,0:T(8,128)(2,1)S(1)} %bitcast.61), kind=kOutput, calls=%fused_computation.66 | convolution fusion | flops 1882456064 | bytes 11534336 | tf_op jit(solution)/shard_map/dot_general | solution.py:8
  139.2 2.1 %fusion.27 = f32[512,3584]{1,0:T(8,128)S(1)} fusion(bf16[512,512]{1,0:T(8,128)(2,1)S(1)} %get-tuple-element.5, bf16[1,3584,512]{2,1,0:T(8,128)(2,1)S(1)} %copy-done), kind=kOutput, calls=%fused_computation.33 | convolution fusion | flops 1879048192 | bytes 11534336 | tf_op jit(solution)/shard_map/dot_general | solution.py:94
  141.3 0.0 copy-done.11
  141.3 0.0 collective-permute-done.1
  141.3 0.0 collective-permute-done.2
  141.3 0.0 copy-done.9
  141.3 3.7 %fusion.6 = bf16[64,8,3584]{2,1,0:T(8,128)(2,1)} fusion(f32[512,3584]{1,0:T(8,128)S(1)} %fusion.27, bf16[256,3584]{1,0:T(8,128)(2,1)S(1)} %collective-permute-done.2, bf16[256,3584]{1,0:T(8,128)(2,1)S(1)} %collective-permute-done.1, bf16[512,512]{1,0:T(8,128)(2,1)S(1)} %get-tuple-element.4, bf16[1,3584,512]{2,1,0:T(8,128)(2,1)S(1)} %copy-done.1), kind=kOutput, calls=%fused_computation.14 | convolution fusion | flops 1891893248 | bytes 18874368 | tf_op jit(solution)/shard_map/dot_general | solution.py:91
  145.0 6.1 %all-to-all-start.1 = ((bf16[64,8,3584]{2,1,0:T(8,128)(2,1)}), bf16[64,8,3584]{2,1,0:T(8,128)(2,1)}, u32[]{:S(2)}, u32[]{:S(2)}) async-start(bf16[64,8,3584]{2,1,0:T(8,128)(2,1)} %fusion.6), calls=%async_computation.1 | async-start | bytes 7340032 | tf_op jit(solution)/shard_map/all_to_all | solution.py:98
  151.1 0.0 slice-start.1
  151.1 0.0 copy-start.10
  151.1 0.0 slice-start.2
  151.1 7.4 %fusion.44 = f32[3584,512]{1,0:T(8,128)} fusion(bf16[512,512]{1,0:T(8,128)(2,1)} %copy-done.11, bf16[512,7168]{1,0:T(8,128)(2,1)} %bitcast.62), kind=kOutput, calls=%fused_computation.51 | convolution fusion | flops 1879048192 | bytes 11534336 | tf_op jit(solution)/shard_map/dot_general | solution.py:37
  158.5 0.0 slice-done
  158.5 0.0 copy-start.5
  158.5 0.0 copy-start.6
  158.5 0.0 slice-start.3
  158.6 5.1 %fusion.46 = f32[3584,512]{1,0:T(8,128)} fusion(bf16[512,512]{1,0:T(8,128)(2,1)S(1)} %copy-done.10, bf16[512,7168]{1,0:T(8,128)(2,1)S(1)} %bitcast.65), kind=kOutput, calls=%fused_computation.53 | convolution fusion | flops 1879048192 | bytes 11534336 | tf_op jit(solution)/shard_map/dot_general | solution.py:34
  163.7 0.0 copy-done.6
  163.7 2.3 %fusion.37 = f32[512,3584]{1,0:T(8,128)S(1)} fusion(bf16[512,7168]{1,0:T(8,128)(2,1)S(1)} %bitcast.66, f32[512,512]{1,0:T(8,128)S(1)} %copy-done.5, f32[512,512]{1,0:T(8,128)S(1)} %copy-done.6), kind=kOutput, calls=%fused_computation.44 | convolution fusion | flops 1880621056 | bytes 13107200 | tf_op jit(solution)/shard_map/dot_general | solution.py:40
  166.0 0.0 copy-start.13
  166.0 0.0 slice-start.5
  166.0 7.3 %fusion.2 = bf16[1,3584,512]{2,1,0:T(8,128)(2,1)} fusion(f32[3584,512]{1,0:T(8,128)} %fusion.44, bf16[512,512]{1,0:T(8,128)(2,1)S(1)} %copy-done.8, bf16[512,7168]{1,0:T(8,128)(2,1)S(1)} %bitcast.77), kind=kOutput, calls=%fused_computation.9 | convolution fusion | flops 1882718208 | bytes 15204352 | tf_op jit(solution)/shard_map/dot_general | solution.py:37
  173.4 4.2 %fusion.1 = bf16[1,3584,512]{2,1,0:T(8,128)(2,1)} fusion(f32[3584,512]{1,0:T(8,128)S(1)} %bitcast.81, bf16[512,512]{1,0:T(8,128)(2,1)S(1)} %copy-done.13, bf16[512,7168]{1,0:T(8,128)(2,1)S(1)} %bitcast.78), kind=kOutput, calls=%fused_computation.8 | convolution fusion | flops 1882718208 | bytes 15204352 | tf_op jit(solution)/shard_map/dot_general | solution.py:34
  177.6 0.0 copy-done.20
  177.6 4.3 %fusion.3 = bf16[1,512,3584]{2,1,0:T(8,128)(2,1)} fusion(f32[512,3584]{1,0:T(8,128)S(1)} %fusion.37, bf16[512,7168]{1,0:T(8,128)(2,1)S(1)} %bitcast.79, f32[512,512]{1,0:T(8,128)S(1)} %copy-done.18, f32[512,512]{1,0:T(8,128)S(1)} %copy-done.20), kind=kOutput, calls=%fused_computation.10 | convolution fusion | flops 1884291072 | bytes 16777216 | tf_op jit(solution)/shard_map/dot_general | solution.py:40
  181.8 16.9 %all-to-all-done.1 = bf16[64,8,3584]{2,1,0:T(8,128)(2,1)} async-done(((bf16[64,8,3584]{2,1,0:T(8,128)(2,1)}), bf16[64,8,3584]{2,1,0:T(8,128)(2,1)}, u32[]{:S(2)}, u32[]{:S(2)}) %all-to-all-start.1) | async-done | bytes 3670048 | tf_op jit(solution)/shard_map/all_to_all | solution.py:98
  198.7 4.4 %convolution_convert_fusion.1 = bf16[256,3584]{1,0:T(8,128)(2,1)} fusion(bf16[256,512]{1,0:T(8,128)(2,1)S(1)} %fusion.53, bf16[64,8,3584]{2,1,0:T(8,128)(2,1)} %all-to-all-done.1), kind=kOutput, calls=%fused_computation.13 | convolution fusion | flops 940441600 | bytes 5767168 | tf_op jit(solution)/shard_map/dot_general | solution.py:109
  (28 shorter events, 0.1 us)
Async XLA Ops:
  0.6 3.7 %copy-start.3 = (bf16[256,3584]{1,0:T(8,128)(2,1)S(1)}, bf16[256,3584]{1,0:T(8,128)(2,1)}, u32[]{:S(2)}) copy-start(bf16[256,3584]{1,0:T(8,128)(2,1)} %param.7) | copy-start | bytes 5505028
  6.9 100.5 %copy-start.14 = (s32[256,1]{0,1:T(1,128)S(1)}, s32[256,1]{0,1:T(1,128)}, u32[]{:S(2)}) copy-start(s32[256,1]{0,1:T(1,128)} %param.9) | copy-start | bytes 3076
  6.9 100.6 %copy-start = (bf16[1,3584,512]{2,1,0:T(8,128)(2,1)S(1)}, bf16[1,3584,512]{2,1,0:T(8,128)(2,1)}, u32[]{:S(2)}) copy-start(bf16[1,3584,512]{2,1,0:T(8,128)(2,1)} %param.12) | copy-start | bytes 11010052
  104.1 31.7 %copy-start.2 = (bf16[64,8,7168]{2,1,0:T(8,128)(2,1)}, bf16[64,8,7168]{2,1,0:T(8,128)(2,1)S(1)}, u32[]{:S(2)}) copy-start(bf16[64,8,7168]{2,1,0:T(8,128)(2,1)S(1)} %all_to_all.10) | copy-start | bytes 22020100
  104.1 14.5 %collective-permute-start = (bf16[64,8,7168]{2,1,0:T(8,128)(2,1)S(1)}, bf16[64,8,7168]{2,1,0:T(8,128)(2,1)S(1)}, u32[]{:S(2)}, u32[]{:S(2)}) collective-permute-start(bf16[64,8,7168]{2,1,0:T(8,128)(2,1)S(1)} %all_to_all.10), channel_id=1, source_target_pairs={{0,64},{64,0},{1,65},{65,1},{2,66},{66,2},{3,67},{67,3},{4,68},{68... | collective-permute-start | bytes 22020104 | tf_op jit(solution)/shard_map/ppermute | solution.py:74
  109.6 26.2 %copy-start.4 = (f32[512,512]{1,0:T(8,128)}, f32[512,512]{1,0:T(8,128)S(1)}, u32[]{:S(2)}) copy-start(f32[512,512]{1,0:T(8,128)S(1)} %fusion.29) | copy-start | bytes 3145732
  118.7 6.8 %copy-start.15 = (bf16[64,8,7168]{2,1,0:T(8,128)(2,1)}, bf16[64,8,7168]{2,1,0:T(8,128)(2,1)S(1)}, u32[]{:S(2)}) copy-start(bf16[64,8,7168]{2,1,0:T(8,128)(2,1)S(1)} %collective-permute-done) | copy-start | bytes 22020100
  118.7 4.7 %copy-start.1 = (bf16[1,3584,512]{2,1,0:T(8,128)(2,1)S(1)}, bf16[1,3584,512]{2,1,0:T(8,128)(2,1)}, u32[]{:S(2)}) copy-start(bf16[1,3584,512]{2,1,0:T(8,128)(2,1)} %param.11) | copy-start | bytes 11010052
  123.4 2.1 %copy-start.17 = (f32[512,512]{1,0:T(8,128)}, f32[512,512]{1,0:T(8,128)S(1)}, u32[]{:S(2)}) copy-start(f32[512,512]{1,0:T(8,128)S(1)} %fusion.25) | copy-start | bytes 3145732
  123.4 2.4 %copy-start.16 = (bf16[1,512,3584]{2,1,0:T(8,128)(2,1)S(1)}, bf16[1,512,3584]{2,1,0:T(8,128)(2,1)}, u32[]{:S(2)}) copy-start(bf16[1,512,3584]{2,1,0:T(8,128)(2,1)} %param.13) | copy-start | bytes 11010052
  125.8 2.4 %copy-start.19 = (f32[512,512]{1,0:T(8,128)}, f32[512,512]{1,0:T(8,128)S(1)}, u32[]{:S(2)}) copy-start(f32[512,512]{1,0:T(8,128)S(1)} %fusion.15) | copy-start | bytes 3145732
  128.2 1.2 copy-start.12
  128.2 4.1 %copy-start.7 = (bf16[512,512]{1,0:T(8,128)(2,1)}, bf16[512,512]{1,0:T(8,128)(2,1)S(1)}, u32[]{:S(2)}) copy-start(bf16[512,512]{1,0:T(8,128)(2,1)S(1)} %get-tuple-element.6) | copy-start | bytes 1572868
  131.7 9.6 %collective-permute-start.1 = (bf16[256,3584]{1,0:T(8,128)(2,1)S(1)}, bf16[256,3584]{1,0:T(8,128)(2,1)S(1)}, u32[]{:S(2)}, u32[]{:S(2)}) collective-permute-start(bf16[256,3584]{1,0:T(8,128)(2,1)S(1)} %fusion.4), channel_id=1, source_target_pairs={{0,64},{64,0},{1,65},{65,1},{2,66},{66,2},{3,67},{67,3},{4,68},{68... | collective-permute-start | bytes 5505032 | tf_op jit(solution)/shard_map/ppermute | solution.py:87
  133.5 7.8 %collective-permute-start.2 = (bf16[256,3584]{1,0:T(8,128)(2,1)S(1)}, bf16[256,3584]{1,0:T(8,128)(2,1)S(1)}, u32[]{:S(2)}, u32[]{:S(2)}) collective-permute-start(bf16[256,3584]{1,0:T(8,128)(2,1)S(1)} %fusion.5), channel_id=1, source_target_pairs={{0,64},{64,0},{1,65},{65,1},{2,66},{66,2},{3,67},{67,3},{4,68},{68... | collective-permute-start | bytes 5505032 | tf_op jit(solution)/shard_map/ppermute | solution.py:89
  139.2 2.1 %copy-start.11 = (bf16[512,512]{1,0:T(8,128)(2,1)}, bf16[512,512]{1,0:T(8,128)(2,1)S(1)}, u32[]{:S(2)}) copy-start(bf16[512,512]{1,0:T(8,128)(2,1)S(1)} %get-tuple-element.5) | copy-start | bytes 1572868
  139.2 2.1 %copy-start.9 = (bf16[512,512]{1,0:T(8,128)(2,1)}, bf16[512,512]{1,0:T(8,128)(2,1)S(1)}, u32[]{:S(2)}) copy-start(bf16[512,512]{1,0:T(8,128)(2,1)S(1)} %get-tuple-element.4) | copy-start | bytes 1572868
  145.0 13.5 %slice-start = ((s8[7340032]{0:T(1024)(128)(4,1)}), s8[3145728]{0:T(1024)(128)(4,1)S(1)}, s32[]{:S(2)}) async-start(s8[7340032]{0:T(1024)(128)(4,1)} %bitcast.63), calls=%async_computation.2 | async-start | bytes 6291456
  145.0 53.7 %all-to-all-start.1 = ((bf16[64,8,3584]{2,1,0:T(8,128)(2,1)}), bf16[64,8,3584]{2,1,0:T(8,128)(2,1)}, u32[]{:S(2)}, u32[]{:S(2)}) async-start(bf16[64,8,3584]{2,1,0:T(8,128)(2,1)} %fusion.6), calls=%async_computation.1 | async-start | bytes 7340032 | tf_op jit(solution)/shard_map/all_to_all | solution.py:98
  151.1 7.4 %slice-start.1 = ((s8[7340032]{0:T(1024)(128)(4,1)}), s8[4194304]{0:T(1024)(128)(4,1)S(1)}, s32[]{:S(2)}) async-start(s8[7340032]{0:T(1024)(128)(4,1)} %bitcast.63), calls=%async_computation.3 | async-start | bytes 8388608
  151.1 7.4 %copy-start.10 = (bf16[512,512]{1,0:T(8,128)(2,1)S(1)}, bf16[512,512]{1,0:T(8,128)(2,1)}, u32[]{:S(2)}) copy-start(bf16[512,512]{1,0:T(8,128)(2,1)} %copy-done.9) | copy-start | bytes 1572868
  151.1 14.8 %slice-start.2 = ((s8[7340032]{0:T(1024)(128)(4,1)}), s8[4194304]{0:T(1024)(128)(4,1)S(1)}, s32[]{:S(2)}) async-start(s8[7340032]{0:T(1024)(128)(4,1)} %bitcast.75), calls=%async_computation.4 | async-start | bytes 8388608
  158.5 5.2 %copy-start.5 = (f32[512,512]{1,0:T(8,128)S(1)}, f32[512,512]{1,0:T(8,128)}, u32[]{:S(2)}) copy-start(f32[512,512]{1,0:T(8,128)} %copy-done.4) | copy-start | bytes 3145732
  158.5 5.2 %copy-start.6 = (f32[512,512]{1,0:T(8,128)S(1)}, f32[512,512]{1,0:T(8,128)}, u32[]{:S(2)}) copy-start(f32[512,512]{1,0:T(8,128)} %get-tuple-element.8) | copy-start | bytes 3145732
  158.5 7.4 %slice-start.3 = ((s8[7340032]{0:T(1024)(128)(4,1)}), s8[3145728]{0:T(1024)(128)(4,1)S(1)}, s32[]{:S(2)}) async-start(s8[7340032]{0:T(1024)(128)(4,1)} %bitcast.75), calls=%async_computation.5 | async-start | bytes 6291456
  163.7 2.3 %copy-start.8 = (bf16[512,512]{1,0:T(8,128)(2,1)S(1)}, bf16[512,512]{1,0:T(8,128)(2,1)}, u32[]{:S(2)}) copy-start(bf16[512,512]{1,0:T(8,128)(2,1)} %copy-done.7) | copy-start | bytes 1572868
  163.7 9.7 %slice-start.4 = ((s8[7340032]{0:T(1024)(128)(4,1)}), s8[4194304]{0:T(1024)(128)(4,1)S(1)}, s32[]{:S(2)}) async-start(s8[7340032]{0:T(1024)(128)(4,1)} %bitcast.80), calls=%async_computation.6 | async-start | bytes 8388608
  166.0 7.3 %copy-start.13 = (bf16[512,512]{1,0:T(8,128)(2,1)S(1)}, bf16[512,512]{1,0:T(8,128)(2,1)}, u32[]{:S(2)}) copy-start(bf16[512,512]{1,0:T(8,128)(2,1)} %copy-done.12) | copy-start | bytes 1572868
  166.0 7.3 %slice-start.5 = ((s8[7340032]{0:T(1024)(128)(4,1)}), s8[3145728]{0:T(1024)(128)(4,1)S(1)}, s32[]{:S(2)}) async-start(s8[7340032]{0:T(1024)(128)(4,1)} %bitcast.80), calls=%async_computation.7 | async-start | bytes 6291456
  173.4 4.2 %copy-start.18 = (f32[512,512]{1,0:T(8,128)S(1)}, f32[512,512]{1,0:T(8,128)}, u32[]{:S(2)}) copy-start(f32[512,512]{1,0:T(8,128)} %copy-done.17) | copy-start | bytes 3145732
  173.4 4.2 %copy-start.20 = (f32[512,512]{1,0:T(8,128)S(1)}, f32[512,512]{1,0:T(8,128)}, u32[]{:S(2)}) copy-start(f32[512,512]{1,0:T(8,128)} %copy-done.19) | copy-start | bytes 3145732

commit v8 on v7

--- a/solution.py
+++ b/solution.py
@@ -59,13 +59,15 @@
     position = flat_ids * capacity + slot_rank
     copy_rows = tokens[:, None, :].reshape(copies, model_width)
     copy_tok_cot = cotangent[:, None, :].reshape(copies, model_width)
-    copy_cots = (gate_probs * copy_tok_cot.astype(jnp.float32)).astype(jnp.bfloat16)
     placing = (jnp.arange(owners * capacity, dtype=jnp.int32)[:, None] == position[None, :]).astype(
         jnp.bfloat16
     )
-    joined = jnp.concatenate([copy_rows, copy_cots], axis=1)
+    joined = jnp.concatenate([copy_rows, copy_tok_cot], axis=1)
+    slot_gate = jnp.sum(placing.astype(jnp.float32) * gate_probs.reshape(1, copies), axis=1)
+    picked = jnp.dot(placing, joined, preferred_element_type=jnp.float32)
+    is_cot = jnp.arange(2 * model_width, dtype=jnp.int32)[None, :] >= model_width
     sent = (
-        jnp.dot(placing, joined, preferred_element_type=jnp.float32)
+        jnp.where(is_cot, picked * slot_gate[:, None], picked)
         .astype(jnp.bfloat16)
         .reshape(owners, capacity, 2 * model_width)
     )

time: 204 us -> 204 us (level)
  no operation moved by 1% of the time
where the time goes in v8:
time: 204 us
  blocking collectives  97.2 us (48%)
  matrix products  64.7 us (32%)
  waiting for transfers between devices  26 us (13%)
  starting transfers between devices  10.2 us (5%)
  local copies, waits for them, and re-layouts  3.11 us (2%)
    all_to_all x1, blocking collectives, local(): lax.all_to_all(sent, 'expert', split_axis=0, concat_axis=0, tiled=True)  97.2 us
    all_to_all x1, waiting for transfers between devices, local(): lax.all_to_all(summed.reshape(owners, capacity, model_width), 'expert', s...  17 us
    dot_general x2, matrix products, weight_sums(): lax.dot_general(rows_x, d_up, (((0,), (0,)), ((), ())), preferred_element...  14.7 us
    dot_general x2, matrix products, weight_sums(): lax.dot_general(rows_x, d_gate, (((0,), (0,)), ((), ())), preferred_eleme...  9.32 us
    ppermute x1, waiting for transfers between devices, local(): other = lax.ppermute(came, 'dp', swap)  9.08 us
    dot_general x2, matrix products, weight_sums(): lax.dot_general(hidden, rows_cot, (((0,), (0,)), ((), ())), preferred_ele...  6.46 us
    all_to_all x1, starting transfers between devices, local(): lax.all_to_all(summed.reshape(owners, capacity, model_width), 'expert', s...  6.1 us
    dot_general x2, matrix products, front_rows(): gate_pre = jnp.dot(rows_x, gate_w, preferred_element_type=jnp.float32)  5.39 us
  transfers between devices with their start and end apart: 4, of which 2 were waited for; matrix products, arithmetic and copies ran while one was open for 20% of the time, Pallas kernels for 0%

profile of v8, /device:TPU:1, one launch (start us, length us, event | category | flops | bytes accessed | tf_op | source)
XLA Modules:
  0.0 203.9 jit_solution(17161981018811289954)
XLA Ops:
  0.6 1.0 fusion.51
  1.6 0.7 multiply_add_fusion
  2.3 0.8 multiply_reduce_fusion
  3.1 4.5 %fusion.1 = bf16[64,8,7168]{2,1,0:T(8,128)(2,1)S(1)} fusion(f32[512]{0:T(512)S(1)} %multiply_reduce_fusion, pred[7168]{0:T(1024)(128)(4,1)S(1)} %iota_compare_fusion.7, bf16[256,3584]{1,0:T(8,128)(2,1)} %param.8, bf16[256,3584]{1,0:T(8,128)(2,1)} %param.7, s32[256]{0:T(256)S(1)} %multiply_add_fusion), kind=kOutput, calls=%fused_computation.2 | convolution fusion | flops 1897529344 | bytes 11020288 | tf_op jit(solution)/shard_map/dot_general | solution.py:67
  7.6 0.0 copy-start.13
  7.6 0.0 copy-start
  7.7 97.2 %all_to_all.10 = bf16[64,8,7168]{2,1,0:T(8,128)(2,1)S(1)} all-to-all(bf16[64,8,7168]{2,1,0:T(8,128)(2,1)S(1)} %fusion.1), channel_id=1, replica_groups=mesh['dp'=2,'expert'=64] {'expert'}, dimensions={0} | all-to-all | bytes 14680064 | tf_op jit(solution)/shard_map/all_to_all | solution.py:74
  104.8 3.3 %collective-permute-start = (bf16[64,8,7168]{2,1,0:T(8,128)(2,1)S(1)}, bf16[64,8,7168]{2,1,0:T(8,128)(2,1)S(1)}, u32[]{:S(2)}, u32[]{:S(2)}) collective-permute-start(bf16[64,8,7168]{2,1,0:T(8,128)(2,1)S(1)} %all_to_all.10), channel_id=1, source_target_pairs={{0,64},{64,0},{1,65},{65,1},{2,66},{66,2},{3,67},{67,3},{4,68},{68... | collective-permute-start | bytes 22020104 | tf_op jit(solution)/shard_map/ppermute | solution.py:76
  108.1 0.0 copy-done.13
  108.1 0.1 fusion.55
  108.2 0.0 copy-done
  108.2 2.1 %fusion.30 = f32[512,512]{1,0:T(8,128)S(1)} fusion(bf16[1,3584,512]{2,1,0:T(8,128)(2,1)S(1)} %copy-done, bf16[512,7168]{1,0:T(8,128)(2,1)S(1)} %bitcast.59), kind=kOutput, calls=%fused_computation.36 | convolution fusion | flops 1879048192 | bytes 8388608 | tf_op jit(solution)/shard_map/dot_general | solution.py:9
  110.3 0.0 copy-start.3
  110.3 9.1 %collective-permute-done = bf16[64,8,7168]{2,1,0:T(8,128)(2,1)S(1)} collective-permute-done((bf16[64,8,7168]{2,1,0:T(8,128)(2,1)S(1)}, bf16[64,8,7168]{2,1,0:T(8,128)(2,1)S(1)}, u32[]{:S(2)}, u32[]{:S(2)}) %collective-permute-start) | collective-permute-done | bytes 7340064 | tf_op jit(solution)/shard_map/ppermute | solution.py:76
  119.4 2.1 %fusion.26 = f32[512,512]{1,0:T(8,128)S(1)} fusion(bf16[1,3584,512]{2,1,0:T(8,128)(2,1)S(1)} %copy-done, bf16[512,7168]{1,0:T(8,128)(2,1)S(1)} %bitcast.72), kind=kOutput, calls=%fused_computation.32 | convolution fusion | flops 1879048192 | bytes 8388608 | tf_op jit(solution)/shard_map/dot_general | solution.py:9
  121.4 2.6 %copy-done.1 = bf16[1,3584,512]{2,1,0:T(8,128)(2,1)S(1)} copy-done((bf16[1,3584,512]{2,1,0:T(8,128)(2,1)S(1)}, bf16[1,3584,512]{2,1,0:T(8,128)(2,1)}, u32[]{:S(2)}) %copy-start.1) | copy-done | bytes 3670040
  124.1 2.1 %fusion.16 = f32[512,512]{1,0:T(8,128)S(1)} fusion(bf16[1,3584,512]{2,1,0:T(8,128)(2,1)S(1)} %copy-done.1, bf16[512,7168]{1,0:T(8,128)(2,1)S(1)} %bitcast.73), kind=kOutput, calls=%fused_computation.24 | convolution fusion | flops 1879048192 | bytes 8388608 | tf_op jit(solution)/shard_map/dot_general | solution.py:8
  126.1 0.0 copy-done.14
  126.1 0.0 copy-done.17
  126.2 0.3 copy-done.15
  126.5 2.4 %multiply_convert_fusion.2 = (bf16[512,512]{1,0:T(8,128)(2,1)S(1)}, bf16[512,512]{1,0:T(8,128)(2,1)S(1)}) fusion(f32[512,512]{1,0:T(8,128)S(1)} %fusion.16, f32[512,512]{1,0:T(8,128)S(1)} %fusion.26, bf16[1,512,3584]{2,1,0:T(8,128)(2,1)S(1)} %copy-done.15, bf16[512,7168]{1,0:T(8,128)(2,1)S(1)} %bitcast.74), kind=kOutput, calls=%fused_computation.61 | convolution fusion | flops 1882456064 | bytes 10485760 | tf_op jit(solution)/shard_map/dot_general | solution.py:13
  128.9 0.0 copy-done.19
  128.9 0.0 copy-start.11
  128.9 0.0 copy-start.6
  128.9 1.1 fusion.14
  130.1 0.0 copy-done.11
  130.1 1.1 fusion.12
  131.2 1.1 fusion.5
  132.4 0.0 copy-start.16
  132.4 0.6 collective-permute-start.1
  133.0 0.0 copy-done.6
  133.0 1.1 fusion.6
  134.2 0.2 collective-permute-start.2
  134.4 0.0 copy-done.16
  134.4 2.1 %fusion.34 = f32[512,512]{1,0:T(8,128)S(1)} fusion(bf16[1,512,3584]{2,1,0:T(8,128)(2,1)S(1)} %copy-done.16, bf16[512,7168]{1,0:T(8,128)(2,1)S(1)} %bitcast.60), kind=kOutput, calls=%fused_computation.40 | convolution fusion | flops 1879048192 | bytes 8388608 | tf_op jit(solution)/shard_map/dot_general | solution.py:13
  136.5 0.0 copy-done.2
  136.6 3.3 %multiply_convert_fusion.5 = (bf16[512,512]{1,0:T(8,128)(2,1)S(1)}, bf16[512,512]{1,0:T(8,128)(2,1)S(1)}, f32[512,512]{1,0:T(8,128)}) fusion(f32[512,512]{1,0:T(8,128)S(1)} %fusion.34, f32[512,512]{1,0:T(8,128)S(1)} %fusion.30, bf16[1,3584,512]{2,1,0:T(8,128)(2,1)S(1)} %copy-done.1, bf16[512,7168]{1,0:T(8,128)(2,1)S(1)} %bitcast.61), kind=kOutput, calls=%fused_computation.66 | convolution fusion | flops 1882456064 | bytes 11534336 | tf_op jit(solution)/shard_map/dot_general | solution.py:8
  139.9 2.1 %fusion.28 = f32[512,3584]{1,0:T(8,128)S(1)} fusion(bf16[512,512]{1,0:T(8,128)(2,1)S(1)} %get-tuple-element.5, bf16[1,3584,512]{2,1,0:T(8,128)(2,1)S(1)} %copy-done), kind=kOutput, calls=%fused_computation.34 | convolution fusion | flops 1879048192 | bytes 11534336 | tf_op jit(solution)/shard_map/dot_general | solution.py:96
  142.0 0.0 collective-permute-done.1
  142.0 0.0 collective-permute-done.2
  142.0 3.7 %fusion.7 = bf16[64,8,3584]{2,1,0:T(8,128)(2,1)} fusion(f32[512,3584]{1,0:T(8,128)S(1)} %fusion.28, bf16[256,3584]{1,0:T(8,128)(2,1)S(1)} %collective-permute-done.2, bf16[256,3584]{1,0:T(8,128)(2,1)S(1)} %collective-permute-done.1, bf16[512,512]{1,0:T(8,128)(2,1)S(1)} %get-tuple-element.4, bf16[1,3584,512]{2,1,0:T(8,128)(2,1)S(1)} %copy-done.1), kind=kOutput, calls=%fused_computation.15 | convolution fusion | flops 1891893248 | bytes 18874368 | tf_op jit(solution)/shard_map/dot_general | solution.py:93
  145.7 6.1 %all-to-all-start.1 = ((bf16[64,8,3584]{2,1,0:T(8,128)(2,1)}), bf16[64,8,3584]{2,1,0:T(8,128)(2,1)}, u32[]{:S(2)}, u32[]{:S(2)}) async-start(bf16[64,8,3584]{2,1,0:T(8,128)(2,1)} %fusion.7), calls=%async_computation.1 | async-start | bytes 7340032 | tf_op jit(solution)/shard_map/all_to_all | solution.py:100
  151.9 0.0 slice-start.1
  151.9 0.0 copy-start.9
  151.9 0.0 slice-start.2
  151.9 7.4 %fusion.45 = f32[3584,512]{1,0:T(8,128)} fusion(bf16[512,512]{1,0:T(8,128)(2,1)} %copy-done.10, bf16[512,7168]{1,0:T(8,128)(2,1)} %bitcast.62), kind=kOutput, calls=%fused_computation.51 | convolution fusion | flops 1879048192 | bytes 11534336 | tf_op jit(solution)/shard_map/dot_general | solution.py:37
  159.3 0.0 slice-done.1
  159.3 0.0 copy-start.4
  159.3 0.0 copy-start.5
  159.3 0.0 slice-start.3
  159.3 5.1 %fusion.47 = f32[3584,512]{1,0:T(8,128)} fusion(bf16[512,512]{1,0:T(8,128)(2,1)S(1)} %copy-done.9, bf16[512,7168]{1,0:T(8,128)(2,1)S(1)} %bitcast.65), kind=kOutput, calls=%fused_computation.53 | convolution fusion | flops 1879048192 | bytes 11534336 | tf_op jit(solution)/shard_map/dot_general | solution.py:34
  164.4 0.0 copy-done.4
  164.5 2.2 %fusion.38 = f32[512,3584]{1,0:T(8,128)S(1)} fusion(bf16[512,7168]{1,0:T(8,128)(2,1)S(1)} %bitcast.66, f32[512,512]{1,0:T(8,128)S(1)} %copy-done.4, f32[512,512]{1,0:T(8,128)S(1)} %copy-done.5), kind=kOutput, calls=%fused_computation.44 | convolution fusion | flops 1880621056 | bytes 13107200 | tf_op jit(solution)/shard_map/dot_general | solution.py:40
  166.7 0.0 slice-done.2
  166.7 0.0 slice-done.3
  166.7 0.0 copy-done.7
  166.7 0.0 copy-start.12
  166.7 0.0 slice-start.5
  166.7 7.3 %fusion.3 = bf16[1,3584,512]{2,1,0:T(8,128)(2,1)} fusion(f32[3584,512]{1,0:T(8,128)} %fusion.45, bf16[512,512]{1,0:T(8,128)(2,1)S(1)} %copy-done.7, bf16[512,7168]{1,0:T(8,128)(2,1)S(1)} %bitcast.77), kind=kOutput, calls=%fused_computation.10 | convolution fusion | flops 1882718208 | bytes 15204352 | tf_op jit(solution)/shard_map/dot_general | solution.py:37
  174.0 0.0 slice-done.4
  174.1 4.2 %fusion.2 = bf16[1,3584,512]{2,1,0:T(8,128)(2,1)} fusion(f32[3584,512]{1,0:T(8,128)S(1)} %bitcast.81, bf16[512,512]{1,0:T(8,128)(2,1)S(1)} %copy-done.12, bf16[512,7168]{1,0:T(8,128)(2,1)S(1)} %bitcast.78), kind=kOutput, calls=%fused_computation.9 | convolution fusion | flops 1882718208 | bytes 15204352 | tf_op jit(solution)/shard_map/dot_general | solution.py:34
  178.3 4.3 %fusion.4 = bf16[1,512,3584]{2,1,0:T(8,128)(2,1)} fusion(f32[512,3584]{1,0:T(8,128)S(1)} %fusion.38, bf16[512,7168]{1,0:T(8,128)(2,1)S(1)} %bitcast.79, f32[512,512]{1,0:T(8,128)S(1)} %copy-done.18, f32[512,512]{1,0:T(8,128)S(1)} %copy-done.20), kind=kOutput, calls=%fused_computation.11 | convolution fusion | flops 1884291072 | bytes 16777216 | tf_op jit(solution)/shard_map/dot_general | solution.py:40
  182.5 17.0 %all-to-all-done.1 = bf16[64,8,3584]{2,1,0:T(8,128)(2,1)} async-done(((bf16[64,8,3584]{2,1,0:T(8,128)(2,1)}), bf16[64,8,3584]{2,1,0:T(8,128)(2,1)}, u32[]{:S(2)}, u32[]{:S(2)}) %all-to-all-start.1) | async-done | bytes 3670048 | tf_op jit(solution)/shard_map/all_to_all | solution.py:100
  199.5 4.4 %convolution_convert_fusion = bf16[256,3584]{1,0:T(8,128)(2,1)} fusion(bf16[256,512]{1,0:T(8,128)(2,1)S(1)} %fusion.55, bf16[64,8,3584]{2,1,0:T(8,128)(2,1)} %all-to-all-done.1), kind=kOutput, calls=%fused_computation.14 | convolution fusion | flops 940441600 | bytes 5767168 | tf_op jit(solution)/shard_map/dot_general | solution.py:111
  (29 shorter events, 0.1 us)
Async XLA Ops:
  7.6 100.5 %copy-start.13 = (s32[256,1]{0,1:T(1,128)S(1)}, s32[256,1]{0,1:T(1,128)}, u32[]{:S(2)}) copy-start(s32[256,1]{0,1:T(1,128)} %param.9) | copy-start | bytes 3076
  7.6 100.6 %copy-start = (bf16[1,3584,512]{2,1,0:T(8,128)(2,1)S(1)}, bf16[1,3584,512]{2,1,0:T(8,128)(2,1)}, u32[]{:S(2)}) copy-start(bf16[1,3584,512]{2,1,0:T(8,128)(2,1)} %param.12) | copy-start | bytes 11010052
  104.8 31.7 %copy-start.2 = (bf16[64,8,7168]{2,1,0:T(8,128)(2,1)}, bf16[64,8,7168]{2,1,0:T(8,128)(2,1)S(1)}, u32[]{:S(2)}) copy-start(bf16[64,8,7168]{2,1,0:T(8,128)(2,1)S(1)} %all_to_all.10) | copy-start | bytes 22020100
  104.8 14.5 %collective-permute-start = (bf16[64,8,7168]{2,1,0:T(8,128)(2,1)S(1)}, bf16[64,8,7168]{2,1,0:T(8,128)(2,1)S(1)}, u32[]{:S(2)}, u32[]{:S(2)}) collective-permute-start(bf16[64,8,7168]{2,1,0:T(8,128)(2,1)S(1)} %all_to_all.10), channel_id=1, source_target_pairs={{0,64},{64,0},{1,65},{65,1},{2,66},{66,2},{3,67},{67,3},{4,68},{68... | collective-permute-start | bytes 22020104 | tf_op jit(solution)/shard_map/ppermute | solution.py:76
  110.3 26.2 %copy-start.3 = (f32[512,512]{1,0:T(8,128)}, f32[512,512]{1,0:T(8,128)S(1)}, u32[]{:S(2)}) copy-start(f32[512,512]{1,0:T(8,128)S(1)} %fusion.30) | copy-start | bytes 3145732
  119.4 6.8 %copy-start.14 = (bf16[64,8,7168]{2,1,0:T(8,128)(2,1)}, bf16[64,8,7168]{2,1,0:T(8,128)(2,1)S(1)}, u32[]{:S(2)}) copy-start(bf16[64,8,7168]{2,1,0:T(8,128)(2,1)S(1)} %collective-permute-done) | copy-start | bytes 22020100
  119.4 4.7 %copy-start.1 = (bf16[1,3584,512]{2,1,0:T(8,128)(2,1)S(1)}, bf16[1,3584,512]{2,1,0:T(8,128)(2,1)}, u32[]{:S(2)}) copy-start(bf16[1,3584,512]{2,1,0:T(8,128)(2,1)} %param.11) | copy-start | bytes 11010052
  124.1 2.1 %copy-start.17 = (f32[512,512]{1,0:T(8,128)}, f32[512,512]{1,0:T(8,128)S(1)}, u32[]{:S(2)}) copy-start(f32[512,512]{1,0:T(8,128)S(1)} %fusion.26) | copy-start | bytes 3145732
  124.1 2.4 %copy-start.15 = (bf16[1,512,3584]{2,1,0:T(8,128)(2,1)S(1)}, bf16[1,512,3584]{2,1,0:T(8,128)(2,1)}, u32[]{:S(2)}) copy-start(bf16[1,512,3584]{2,1,0:T(8,128)(2,1)} %param.13) | copy-start | bytes 11010052
  126.5 2.4 %copy-start.19 = (f32[512,512]{1,0:T(8,128)}, f32[512,512]{1,0:T(8,128)S(1)}, u32[]{:S(2)}) copy-start(f32[512,512]{1,0:T(8,128)S(1)} %fusion.16) | copy-start | bytes 3145732
  128.9 1.2 copy-start.11
  128.9 4.1 %copy-start.6 = (bf16[512,512]{1,0:T(8,128)(2,1)}, bf16[512,512]{1,0:T(8,128)(2,1)S(1)}, u32[]{:S(2)}) copy-start(bf16[512,512]{1,0:T(8,128)(2,1)S(1)} %get-tuple-element.6) | copy-start | bytes 1572868
  132.4 2.0 %copy-start.16 = (bf16[1,512,3584]{2,1,0:T(8,128)(2,1)S(1)}, bf16[1,512,3584]{2,1,0:T(8,128)(2,1)}, u32[]{:S(2)}) copy-start(bf16[1,512,3584]{2,1,0:T(8,128)(2,1)} %param.13) | copy-start | bytes 11010052
  132.4 9.6 %collective-permute-start.1 = (bf16[256,3584]{1,0:T(8,128)(2,1)S(1)}, bf16[256,3584]{1,0:T(8,128)(2,1)S(1)}, u32[]{:S(2)}, u32[]{:S(2)}) collective-permute-start(bf16[256,3584]{1,0:T(8,128)(2,1)S(1)} %fusion.5), channel_id=1, source_target_pairs={{0,64},{64,0},{1,65},{65,1},{2,66},{66,2},{3,67},{67,3},{4,68},{68... | collective-permute-start | bytes 5505032 | tf_op jit(solution)/shard_map/ppermute | solution.py:89
  134.2 7.8 %collective-permute-start.2 = (bf16[256,3584]{1,0:T(8,128)(2,1)S(1)}, bf16[256,3584]{1,0:T(8,128)(2,1)S(1)}, u32[]{:S(2)}, u32[]{:S(2)}) collective-permute-start(bf16[256,3584]{1,0:T(8,128)(2,1)S(1)} %fusion.6), channel_id=1, source_target_pairs={{0,64},{64,0},{1,65},{65,1},{2,66},{66,2},{3,67},{67,3},{4,68},{68... | collective-permute-start | bytes 5505032 | tf_op jit(solution)/shard_map/ppermute | solution.py:91
  139.9 2.1 %copy-start.10 = (bf16[512,512]{1,0:T(8,128)(2,1)}, bf16[512,512]{1,0:T(8,128)(2,1)S(1)}, u32[]{:S(2)}) copy-start(bf16[512,512]{1,0:T(8,128)(2,1)S(1)} %get-tuple-element.5) | copy-start | bytes 1572868
  139.9 2.1 %copy-start.8 = (bf16[512,512]{1,0:T(8,128)(2,1)}, bf16[512,512]{1,0:T(8,128)(2,1)S(1)}, u32[]{:S(2)}) copy-start(bf16[512,512]{1,0:T(8,128)(2,1)S(1)} %get-tuple-element.4) | copy-start | bytes 1572868
  145.7 13.5 %slice-start = ((s8[7340032]{0:T(1024)(128)(4,1)}), s8[3145728]{0:T(1024)(128)(4,1)S(1)}, s32[]{:S(2)}) async-start(s8[7340032]{0:T(1024)(128)(4,1)} %bitcast.63), calls=%async_computation.2 | async-start | bytes 6291456
  145.7 53.7 %all-to-all-start.1 = ((bf16[64,8,3584]{2,1,0:T(8,128)(2,1)}), bf16[64,8,3584]{2,1,0:T(8,128)(2,1)}, u32[]{:S(2)}, u32[]{:S(2)}) async-start(bf16[64,8,3584]{2,1,0:T(8,128)(2,1)} %fusion.7), calls=%async_computation.1 | async-start | bytes 7340032 | tf_op jit(solution)/shard_map/all_to_all | solution.py:100
  151.9 7.4 %slice-start.1 = ((s8[7340032]{0:T(1024)(128)(4,1)}), s8[4194304]{0:T(1024)(128)(4,1)S(1)}, s32[]{:S(2)}) async-start(s8[7340032]{0:T(1024)(128)(4,1)} %bitcast.63), calls=%async_computation.3 | async-start | bytes 8388608
  151.9 7.4 %copy-start.9 = (bf16[512,512]{1,0:T(8,128)(2,1)S(1)}, bf16[512,512]{1,0:T(8,128)(2,1)}, u32[]{:S(2)}) copy-start(bf16[512,512]{1,0:T(8,128)(2,1)} %copy-done.8) | copy-start | bytes 1572868
  151.9 14.8 %slice-start.2 = ((s8[7340032]{0:T(1024)(128)(4,1)}), s8[4194304]{0:T(1024)(128)(4,1)S(1)}, s32[]{:S(2)}) async-start(s8[7340032]{0:T(1024)(128)(4,1)} %bitcast.75), calls=%async_computation.4 | async-start | bytes 8388608
  159.3 5.2 %copy-start.4 = (f32[512,512]{1,0:T(8,128)S(1)}, f32[512,512]{1,0:T(8,128)}, u32[]{:S(2)}) copy-start(f32[512,512]{1,0:T(8,128)} %copy-done.3) | copy-start | bytes 3145732
  159.3 5.2 %copy-start.5 = (f32[512,512]{1,0:T(8,128)S(1)}, f32[512,512]{1,0:T(8,128)}, u32[]{:S(2)}) copy-start(f32[512,512]{1,0:T(8,128)} %get-tuple-element.8) | copy-start | bytes 3145732
  159.3 7.4 %slice-start.3 = ((s8[7340032]{0:T(1024)(128)(4,1)}), s8[3145728]{0:T(1024)(128)(4,1)S(1)}, s32[]{:S(2)}) async-start(s8[7340032]{0:T(1024)(128)(4,1)} %bitcast.75), calls=%async_computation.5 | async-start | bytes 6291456
  164.4 2.2 %copy-start.7 = (bf16[512,512]{1,0:T(8,128)(2,1)S(1)}, bf16[512,512]{1,0:T(8,128)(2,1)}, u32[]{:S(2)}) copy-start(bf16[512,512]{1,0:T(8,128)(2,1)} %copy-done.6) | copy-start | bytes 1572868
  164.5 9.6 %slice-start.4 = ((s8[7340032]{0:T(1024)(128)(4,1)}), s8[4194304]{0:T(1024)(128)(4,1)S(1)}, s32[]{:S(2)}) async-start(s8[7340032]{0:T(1024)(128)(4,1)} %bitcast.80), calls=%async_computation.6 | async-start | bytes 8388608
  166.7 7.3 %copy-start.12 = (bf16[512,512]{1,0:T(8,128)(2,1)S(1)}, bf16[512,512]{1,0:T(8,128)(2,1)}, u32[]{:S(2)}) copy-start(bf16[512,512]{1,0:T(8,128)(2,1)} %copy-done.11) | copy-start | bytes 1572868
  166.7 7.3 %slice-start.5 = ((s8[7340032]{0:T(1024)(128)(4,1)}), s8[3145728]{0:T(1024)(128)(4,1)S(1)}, s32[]{:S(2)}) async-start(s8[7340032]{0:T(1024)(128)(4,1)} %bitcast.80), calls=%async_computation.7 | async-start | bytes 6291456
  174.1 4.2 %copy-start.18 = (f32[512,512]{1,0:T(8,128)S(1)}, f32[512,512]{1,0:T(8,128)}, u32[]{:S(2)}) copy-start(f32[512,512]{1,0:T(8,128)} %copy-done.17) | copy-start | bytes 3145732
  174.1 4.2 %copy-start.20 = (f32[512,512]{1,0:T(8,128)S(1)}, f32[512,512]{1,0:T(8,128)}, u32[]{:S(2)}) copy-start(f32[512,512]{1,0:T(8,128)} %copy-done.19) | copy-start | bytes 3145732

commit v9 on v7

--- a/solution.py
+++ b/solution.py
@@ -4,9 +4,11 @@
 from jax.sharding import PartitionSpec as P
 
 
-def front_rows(rows_x, rows_cot, gate_w, up_w, down_w):
-    gate_pre = jnp.dot(rows_x, gate_w, preferred_element_type=jnp.float32)
-    up_pre = jnp.dot(rows_x, up_w, preferred_element_type=jnp.float32)
+def front_rows(rows_x, rows_cot, gate_up_w, down_w):
+    hidden_width = down_w.shape[0]
+    both_pre = jnp.dot(rows_x, gate_up_w, preferred_element_type=jnp.float32)
+    gate_pre = both_pre[:, :hidden_width]
+    up_pre = both_pre[:, hidden_width:]
     sigmoid_gate = jax.nn.sigmoid(gate_pre)
     swish_gate = gate_pre * sigmoid_gate
     hidden = (swish_gate * up_pre).astype(jnp.bfloat16)
@@ -17,15 +19,13 @@
         jnp.bfloat16
     )
     d_up = (d_hidden * swish_gate).astype(jnp.bfloat16)
-    return (hidden, d_gate, d_up, input_grads(d_gate, d_up, gate_w, up_w))
+    return (hidden, d_gate, d_up)
 
 
-def input_grads(d_gate, d_up, gate_w, up_w):
+def input_grads(d_gate, d_up, gate_up_w):
+    both = jnp.concatenate([d_gate, d_up], axis=1)
     dx_part = lax.dot_general(
-        d_gate, gate_w, (((1,), (1,)), ((), ())), preferred_element_type=jnp.float32
-    )
-    dx_part = dx_part + lax.dot_general(
-        d_up, up_w, (((1,), (1,)), ((), ())), preferred_element_type=jnp.float32
+        both, gate_up_w, (((1,), (1,)), ((), ())), preferred_element_type=jnp.float32
     )
     return dx_part.astype(jnp.bfloat16)
 
@@ -73,26 +73,27 @@
     swap = [(0, 1), (1, 0)]
     other = lax.ppermute(came, "dp", swap)
     half_slots = owners * capacity
-    weights_own = (w_gate[0], w_up[0], w_down[0])
+    gate_up = jnp.concatenate([w_gate[0], w_up[0]], axis=1)
+    weights_own = (gate_up, w_down[0])
     came = came.reshape(half_slots, 2 * model_width)
     own_x = came[:, :model_width]
     own_cot = came[:, model_width:]
-    own_h, own_dg, own_du = front_rows(own_x, own_cot, *weights_own)[:3]
+    own_h, own_dg, own_du = front_rows(own_x, own_cot, *weights_own)
     other = other.reshape(half_slots, 2 * model_width)
     oth_x = other[:, :model_width]
     oth_cot = other[:, model_width:]
-    oth_h, oth_dg, oth_du = front_rows(oth_x, oth_cot, *weights_own)[:3]
+    oth_h, oth_dg, oth_du = front_rows(oth_x, oth_cot, *weights_own)
     split = half_slots // 2
-    dx_first = input_grads(oth_dg[:split], oth_du[:split], weights_own[0], weights_own[1])
+    dx_first = input_grads(oth_dg[:split], oth_du[:split], gate_up)
     back_first = lax.ppermute(dx_first, "dp", swap)
-    dx_second = input_grads(oth_dg[split:], oth_du[split:], weights_own[0], weights_own[1])
+    dx_second = input_grads(oth_dg[split:], oth_du[split:], gate_up)
     back_second = lax.ppermute(dx_second, "dp", swap)
     back = jnp.concatenate([back_first, back_second], axis=0)
     own_dx = lax.dot_general(
-        own_dg, weights_own[0], (((1,), (1,)), ((), ())), preferred_element_type=jnp.float32
-    )
-    own_dx = own_dx + lax.dot_general(
-        own_du, weights_own[1], (((1,), (1,)), ((), ())), preferred_element_type=jnp.float32
+        jnp.concatenate([own_dg, own_du], axis=1),
+        gate_up,
+        (((1,), (1,)), ((), ())),
+        preferred_element_type=jnp.float32,
     )
     summed = (own_dx + back.astype(jnp.float32)).astype(jnp.bfloat16)
     returned = lax.all_to_all(

time: 204 us -> 225 us (1.10)
  matrix products: 62.9 us -> 79.5 us
  waiting for transfers between devices: 26 us -> 32.2 us
    dot_general x10 -> x5, matrix products: 19.9 us -> 35.2 us  [the longest x2 17.3 us: front_rows(): both_pre = jnp.dot(rows_x, gate_up_w, preferred_element_type=jnp.float32)]
    dot_general x2, matrix products: 4.48 us -> 10.1 us  [front_rows(): lax.dot_general(rows_cot, down_w, (((1,), (1,)), ((), ())), preferred_ele...]
    all_to_all x1, waiting for transfers between devices: 16.9 us -> 20.9 us  [local(): lax.all_to_all(summed.reshape(owners, capacity, model_width), 'expert', s...]
    dot_general x2, matrix products: 14.7 us -> 10.8 us  [weight_sums(): lax.dot_general(rows_x, d_up, (((0,), (0,)), ((), ())), preferred_element...]
    dot_general x2, matrix products: 9.31 us -> 6.37 us  [weight_sums(): lax.dot_general(rows_x, d_gate, (((0,), (0,)), ((), ())), preferred_eleme...]
    dot_general x2, matrix products: 6.53 us -> 9.1 us  [weight_sums(): lax.dot_general(hidden, rows_cot, (((0,), (0,)), ((), ())), preferred_ele...]
where the time goes in v9:
time: 225 us; the launch traced here: 224 us
  blocking collectives  96.9 us (43%)
  matrix products  79.5 us (35%)
  waiting for transfers between devices  32.2 us (14%)
  starting transfers between devices  9.86 us (4%)
  other arithmetic  2.75 us (1%)
  local copies, waits for them, and re-layouts  2.27 us (1%)
    all_to_all x1, blocking collectives, local(): lax.all_to_all(sent, 'expert', split_axis=0, concat_axis=0, tiled=True)  96.9 us
    all_to_all x1, waiting for transfers between devices, local(): lax.all_to_all(summed.reshape(owners, capacity, model_width), 'expert', s...  20.9 us
    dot_general x2, matrix products, front_rows(): both_pre = jnp.dot(rows_x, gate_up_w, preferred_element_type=jnp.float32)  17.3 us
    ppermute x1, waiting for transfers between devices, local(): other = lax.ppermute(came, 'dp', swap)  11.3 us
    dot_general x2, matrix products, input_grads(): lax.dot_general(both, gate_up_w, (((1,), (1,)), ((), ())), preferred_elem...  10.9 us
    dot_general x2, matrix products, weight_sums(): lax.dot_general(rows_x, d_up, (((0,), (0,)), ((), ())), preferred_element...  10.8 us
    dot_general x2, matrix products, front_rows(): lax.dot_general(rows_cot, down_w, (((1,), (1,)), ((), ())), preferred_ele...  10.1 us
    dot_general x2, matrix products, weight_sums(): lax.dot_general(hidden, rows_cot, (((0,), (0,)), ((), ())), preferred_ele...  9.1 us
  transfers between devices with their start and end apart: 4, of which 2 were waited for; matrix products, arithmetic and copies ran while one was open for 20% of the time, Pallas kernels for 0%

profile of v9, /device:TPU:1, one launch (start us, length us, event | category | flops | bytes accessed | tf_op | source)
XLA Modules:
  0.0 224.4 jit_solution(7957955608085331913)
XLA Ops:
  0.6 0.0 copy-start.1
  0.6 1.0 fusion.28
  1.7 0.7 multiply_add_fusion
  2.4 1.9 multiply_convert_fusion
  4.3 0.0 copy-done.1
  4.3 2.5 %fusion = bf16[64,8,7168]{2,1,0:T(8,128)(2,1)S(1)} fusion(bf16[256,3584]{1,0:T(8,128)(2,1)S(1)} %multiply_convert_fusion, bf16[256,3584]{1,0:T(8,128)(2,1)S(1)} %copy-done.1, s32[256]{0:T(256)S(1)} %multiply_add_fusion), kind=kOutput, calls=%fused_computation.1 | convolution fusion | flops 1890189312 | bytes 11011072 | tf_op jit(solution)/shard_map/dot_general | solution.py:68
  6.8 0.0 copy-start.8
  6.9 96.9 %all_to_all.10 = bf16[64,8,7168]{2,1,0:T(8,128)(2,1)S(1)} all-to-all(bf16[64,8,7168]{2,1,0:T(8,128)(2,1)S(1)} %fusion), channel_id=1, replica_groups=mesh['dp'=2,'expert'=64] {'expert'}, dimensions={0} | all-to-all | bytes 14680064 | tf_op jit(solution)/shard_map/all_to_all | solution.py:72
  103.8 3.3 %collective-permute-start = (bf16[64,8,7168]{2,1,0:T(8,128)(2,1)S(1)}, bf16[64,8,7168]{2,1,0:T(8,128)(2,1)S(1)}, u32[]{:S(2)}, u32[]{:S(2)}) collective-permute-start(bf16[64,8,7168]{2,1,0:T(8,128)(2,1)S(1)} %all_to_all.10), channel_id=1, source_target_pairs={{0,64},{64,0},{1,65},{65,1},{2,66},{66,2},{3,67},{67,3},{4,68},{68... | collective-permute-start | bytes 22020104 | tf_op jit(solution)/shard_map/ppermute | solution.py:74
  107.1 0.0 copy-done.8
  107.1 11.3 %collective-permute-done = bf16[64,8,7168]{2,1,0:T(8,128)(2,1)S(1)} collective-permute-done((bf16[64,8,7168]{2,1,0:T(8,128)(2,1)S(1)}, bf16[64,8,7168]{2,1,0:T(8,128)(2,1)S(1)}, u32[]{:S(2)}, u32[]{:S(2)}) %collective-permute-start) | collective-permute-done | bytes 7340064 | tf_op jit(solution)/shard_map/ppermute | solution.py:74
  118.3 9.8 %fusion.20 = f32[512,1024]{0,1:T(8,128)S(1)} fusion(bf16[512,7168]{1,0:T(8,128)(2,1)S(1)} %bitcast.47, bf16[3584,512]{1,0:T(8,128)(2,1)} %bitcast.54, bf16[3584,512]{1,0:T(8,128)(2,1)} %bitcast.59), kind=kOutput, calls=%fused_computation.30 | convolution fusion | flops 3772776448 | bytes 13107200 | tf_op jit(solution)/shard_map/dot_general | solution.py:9
  128.2 0.0 copy-done.9
  128.2 0.0 copy-start.16
  128.2 0.0 copy-start.11
  128.2 5.2 %multiply_convert_fusion.4 = (bf16[512,512]{0,1:T(8,128)(2,1)S(1)}, bf16[512,512]{0,1:T(8,128)(2,1)S(1)}) fusion(f32[512,1024]{0,1:T(8,128)S(1)} %fusion.20, bf16[1,512,3584]{2,1,0:T(8,128)(2,1)} %param.13, bf16[512,7168]{1,0:T(8,128)(2,1)S(1)} %bitcast.48), kind=kOutput, calls=%fused_computation.47 | convolution fusion | flops 1882456064 | bytes 10485760 | tf_op jit(solution)/shard_map/dot_general | solution.py:15
  133.4 0.0 copy-done.16
  133.4 0.0 copy-start.2
  133.4 0.0 copy-start.4
  133.5 0.8 copy-done.2
  134.2 0.1 fusion.55
  134.3 0.2 copy-done.4
  134.5 0.0 copy-done.11
  134.5 5.4 %convolution_convert_fusion.2 = bf16[256,3584]{1,0:T(8,128)(2,1)} fusion(bf16[256,512]{0,1:T(8,128)(2,1)S(1)} %get-tuple-element.13, bf16[256,512]{0,1:T(8,128)(2,1)S(1)} %get-tuple-element.8, bf16[3584,512]{1,0:T(8,128)(2,1)S(1)} %bitcast.55, bf16[3584,512]{1,0:T(8,128)(2,1)} %bitcast.60), kind=kOutput, calls=%fused_computation.11 | convolution fusion | flops 1895694336 | bytes 9699328 | tf_op jit(solution)/shard_map/dot_general | solution.py:27
  139.9 0.4 collective-permute-start.1
  140.3 5.5 %convolution_convert_fusion.1 = bf16[256,3584]{1,0:T(8,128)(2,1)} fusion(bf16[256,512]{0,1:T(8,128)(2,1)S(1)} %get-tuple-element.12, bf16[256,512]{0,1:T(8,128)(2,1)S(1)} %get-tuple-element.9, bf16[3584,512]{1,0:T(8,128)(2,1)S(1)} %bitcast.56, bf16[3584,512]{1,0:T(8,128)(2,1)} %bitcast.61), kind=kOutput, calls=%fused_computation.10 | convolution fusion | flops 1895694336 | bytes 9699328 | tf_op jit(solution)/shard_map/dot_general | solution.py:27
  145.8 0.1 collective-permute-start.2
  146.0 0.1 fusion.43
  146.1 0.0 copy-done.12
  146.1 0.0 copy-start.10
  146.1 7.5 %fusion.26 = f32[512,1024]{0,1:T(8,128)} fusion(bf16[512,7168]{1,0:T(8,128)(2,1)S(1)} %bitcast.35, bf16[3584,512]{1,0:T(8,128)(2,1)S(1)} %bitcast.57, bf16[3584,512]{1,0:T(8,128)(2,1)} %bitcast.62), kind=kOutput, calls=%fused_computation.36 | convolution fusion | flops 3772776448 | bytes 13107200 | tf_op jit(solution)/shard_map/dot_general | solution.py:9
  153.6 0.0 copy-done
  153.6 0.0 copy-done.10
  153.6 4.9 %multiply_convert_fusion.6 = (bf16[512,512]{0,1:T(8,128)(2,1)S(1)}, bf16[512,512]{0,1:T(8,128)(2,1)}) fusion(f32[512,1024]{0,1:T(8,128)} %fusion.26, bf16[1,512,3584]{2,1,0:T(8,128)(2,1)S(1)} %copy-done.10, bf16[512,7168]{1,0:T(8,128)(2,1)S(1)} %bitcast.36), kind=kOutput, calls=%fused_computation.51 | convolution fusion | flops 1882456064 | bytes 10485760 | tf_op jit(solution)/shard_map/dot_general | solution.py:15
  158.5 0.0 collective-permute-done.1
  158.5 0.0 collective-permute-done.2
  158.5 0.9 copy-done.6
  159.4 0.0 copy-done.13
  159.4 6.9 %fusion.4 = bf16[64,8,3584]{2,1,0:T(8,128)(2,1)} fusion(bf16[256,3584]{1,0:T(8,128)(2,1)} %collective-permute-done.2, bf16[256,3584]{1,0:T(8,128)(2,1)S(1)} %collective-permute-done.1, bf16[512,512]{0,1:T(8,128)(2,1)} %get-tuple-element.5, bf16[512,512]{0,1:T(8,128)(2,1)S(1)} %get-tuple-element.4, bf16[3584,512]{1,0:T(8,128)(2,1)S(1)} %bitcast.58, ...), kind=kOutput, calls=%fused_computation.13 | convolution fusion | flops 3785883648 | bytes 15728640 | tf_op jit(solution)/shard_map/dot_general | solution.py:92
  166.3 6.1 %all-to-all-start.1 = ((bf16[64,8,3584]{2,1,0:T(8,128)(2,1)}), bf16[64,8,3584]{2,1,0:T(8,128)(2,1)}, u32[]{:S(2)}, u32[]{:S(2)}) async-start(bf16[64,8,3584]{2,1,0:T(8,128)(2,1)} %fusion.4), calls=%async_computation.1 | async-start | bytes 7340032 | tf_op jit(solution)/shard_map/all_to_all | solution.py:99
  172.4 0.0 slice-start.1
  172.4 0.0 copy-start.7
  172.4 4.5 %fusion.22 = f32[3584,512]{1,0:T(8,128)S(1)} fusion(bf16[512,512]{0,1:T(8,128)(2,1)} %get-tuple-element.5, bf16[512,7168]{1,0:T(8,128)(2,1)} %bitcast.37), kind=kOutput, calls=%fused_computation.32 | convolution fusion | flops 1879048192 | bytes 11534336 | tf_op jit(solution)/shard_map/dot_general | solution.py:37
  176.9 0.0 slice-done
  176.9 0.0 slice-done.1
  176.9 0.0 copy-done.7
  176.9 0.0 copy-start.15
  176.9 2.2 fusion.24
  179.1 0.0 copy-done.15
  179.1 0.0 copy-start.5
  179.1 0.0 slice-start.2
  179.1 5.1 %fusion.15 = f32[512,3584]{1,0:T(8,128)} fusion(bf16[512,7168]{1,0:T(8,128)(2,1)S(1)} %bitcast.41, f32[512,1024]{0,1:T(8,128)S(1)} %copy-done.15), kind=kOutput, calls=%fused_computation.25 | convolution fusion | flops 1880621056 | bytes 13107200 | tf_op jit(solution)/shard_map/dot_general | solution.py:40
  184.2 0.0 copy-done.5
  184.2 6.4 %fusion.2 = bf16[1,3584,512]{2,1,0:T(8,128)(2,1)} fusion(f32[3584,512]{1,0:T(8,128)S(1)} %fusion.22, bf16[512,512]{0,1:T(8,128)(2,1)S(1)} %copy-done.5, bf16[512,7168]{1,0:T(8,128)(2,1)} %bitcast.49), kind=kOutput, calls=%fused_computation.8 | convolution fusion | flops 1882718208 | bytes 15204352 | tf_op jit(solution)/shard_map/dot_general | solution.py:37
  190.6 0.0 slice-done.2
  190.6 0.0 copy-done.3
  190.6 0.0 slice-done.3
  190.6 0.0 copy-start.14
  190.6 0.0 copy-start.17
  190.7 4.2 %fusion.1 = bf16[1,3584,512]{2,1,0:T(8,128)(2,1)} fusion(f32[3584,512]{1,0:T(8,128)S(1)} %fusion.24, bf16[512,512]{0,1:T(8,128)(2,1)S(1)} %copy-done.3, bf16[512,7168]{1,0:T(8,128)(2,1)S(1)} %bitcast.52), kind=kOutput, calls=%fused_computation.7 | convolution fusion | flops 1882718208 | bytes 15204352 | tf_op jit(solution)/shard_map/dot_general | solution.py:34
  194.8 0.3 copy-done.17
  195.1 4.0 %fusion.3 = bf16[1,512,3584]{2,1,0:T(8,128)(2,1)} fusion(f32[512,3584]{1,0:T(8,128)S(1)} %copy-done.14, bf16[512,7168]{1,0:T(8,128)(2,1)S(1)} %bitcast.53, f32[512,1024]{0,1:T(8,128)S(1)} %copy-done.17), kind=kOutput, calls=%fused_computation.9 | convolution fusion | flops 1884291072 | bytes 16777216 | tf_op jit(solution)/shard_map/dot_general | solution.py:40
  199.1 20.9 %all-to-all-done.1 = bf16[64,8,3584]{2,1,0:T(8,128)(2,1)} async-done(((bf16[64,8,3584]{2,1,0:T(8,128)(2,1)}), bf16[64,8,3584]{2,1,0:T(8,128)(2,1)}, u32[]{:S(2)}, u32[]{:S(2)}) %all-to-all-start.1) | async-done | bytes 3670048 | tf_op jit(solution)/shard_map/all_to_all | solution.py:99
  220.0 4.4 %convolution_convert_fusion.3 = bf16[256,3584]{1,0:T(8,128)(2,1)} fusion(bf16[256,512]{1,0:T(8,128)(2,1)S(1)} %fusion.43, bf16[64,8,3584]{2,1,0:T(8,128)(2,1)} %all-to-all-done.1), kind=kOutput, calls=%fused_computation.12 | convolution fusion | flops 940441600 | bytes 5767168 | tf_op jit(solution)/shard_map/dot_general | solution.py:110
  (13 shorter events, 0.0 us)
Async XLA Ops:
  0.6 3.7 %copy-start.1 = (bf16[256,3584]{1,0:T(8,128)(2,1)S(1)}, bf16[256,3584]{1,0:T(8,128)(2,1)}, u32[]{:S(2)}) copy-start(bf16[256,3584]{1,0:T(8,128)(2,1)} %param.7) | copy-start | bytes 5505028
  6.8 100.2 %copy-start.8 = (s32[256,1]{0,1:T(1,128)S(1)}, s32[256,1]{0,1:T(1,128)}, u32[]{:S(2)}) copy-start(s32[256,1]{0,1:T(1,128)} %param.9) | copy-start | bytes 3076
  103.8 49.8 %copy-start = (bf16[64,8,7168]{2,1,0:T(8,128)(2,1)}, bf16[64,8,7168]{2,1,0:T(8,128)(2,1)S(1)}, u32[]{:S(2)}) copy-start(bf16[64,8,7168]{2,1,0:T(8,128)(2,1)S(1)} %all_to_all.10) | copy-start | bytes 22020100
  103.8 14.5 %collective-permute-start = (bf16[64,8,7168]{2,1,0:T(8,128)(2,1)S(1)}, bf16[64,8,7168]{2,1,0:T(8,128)(2,1)S(1)}, u32[]{:S(2)}, u32[]{:S(2)}) collective-permute-start(bf16[64,8,7168]{2,1,0:T(8,128)(2,1)S(1)} %all_to_all.10), channel_id=1, source_target_pairs={{0,64},{64,0},{1,65},{65,1},{2,66},{66,2},{3,67},{67,3},{4,68},{68... | collective-permute-start | bytes 22020104 | tf_op jit(solution)/shard_map/ppermute | solution.py:74
  118.3 9.8 %copy-start.9 = (bf16[64,8,7168]{2,1,0:T(8,128)(2,1)}, bf16[64,8,7168]{2,1,0:T(8,128)(2,1)S(1)}, u32[]{:S(2)}) copy-start(bf16[64,8,7168]{2,1,0:T(8,128)(2,1)S(1)} %collective-permute-done) | copy-start | bytes 22020100
  128.2 5.3 %copy-start.16 = (f32[512,1024]{0,1:T(8,128)}, f32[512,1024]{0,1:T(8,128)S(1)}, u32[]{:S(2)}) copy-start(f32[512,1024]{0,1:T(8,128)S(1)} %fusion.20) | copy-start | bytes 6291460
  128.2 6.3 %copy-start.11 = (bf16[1,3584,512]{2,1,0:T(8,128)(2,1)S(1)}, bf16[1,3584,512]{2,1,0:T(8,128)(2,1)}, u32[]{:S(2)}) copy-start(bf16[1,3584,512]{2,1,0:T(8,128)(2,1)} %param.12) | copy-start | bytes 11010052
  133.4 0.8 copy-start.2
  133.4 1.1 copy-start.4
  139.9 18.6 %collective-permute-start.1 = (bf16[256,3584]{1,0:T(8,128)(2,1)}, bf16[256,3584]{1,0:T(8,128)(2,1)S(1)}, u32[]{:S(2)}, u32[]{:S(2)}) collective-permute-start(bf16[256,3584]{1,0:T(8,128)(2,1)} %convolution_convert_fusion.2), channel_id=1, source_target_pairs={{0,64},{64,0},{1,65},{65,1},{2,66},{66,2},{3,67},{67,3},{4,68},{68... | collective-permute-start | bytes 5505032 | tf_op jit(solution)/shard_map/ppermute | solution.py:88
  140.3 5.8 %copy-start.12 = (bf16[1,3584,512]{2,1,0:T(8,128)(2,1)S(1)}, bf16[1,3584,512]{2,1,0:T(8,128)(2,1)}, u32[]{:S(2)}) copy-start(bf16[1,3584,512]{2,1,0:T(8,128)(2,1)} %param.12) | copy-start | bytes 11010052
  145.8 12.7 %collective-permute-start.2 = (bf16[256,3584]{1,0:T(8,128)(2,1)}, bf16[256,3584]{1,0:T(8,128)(2,1)}, u32[]{:S(2)}, u32[]{:S(2)}) collective-permute-start(bf16[256,3584]{1,0:T(8,128)(2,1)} %convolution_convert_fusion.1), channel_id=1, source_target_pairs={{0,64},{64,0},{1,65},{65,1},{2,66},{66,2},{3,67},{67,3},{4,68},{68... | collective-permute-start | bytes 5505032 | tf_op jit(solution)/shard_map/ppermute | solution.py:90
  146.1 7.5 %copy-start.10 = (bf16[1,512,3584]{2,1,0:T(8,128)(2,1)S(1)}, bf16[1,512,3584]{2,1,0:T(8,128)(2,1)}, u32[]{:S(2)}) copy-start(bf16[1,512,3584]{2,1,0:T(8,128)(2,1)} %param.13) | copy-start | bytes 11010052
  153.6 5.7 %copy-start.13 = (bf16[1,3584,512]{2,1,0:T(8,128)(2,1)S(1)}, bf16[1,3584,512]{2,1,0:T(8,128)(2,1)}, u32[]{:S(2)}) copy-start(bf16[1,3584,512]{2,1,0:T(8,128)(2,1)} %param.11) | copy-start | bytes 11010052
  158.5 0.9 copy-start.6
  166.3 10.6 %slice-start = ((s8[7340032]{0:T(1024)(128)(4,1)}), s8[3145728]{0:T(1024)(128)(4,1)S(1)}, s32[]{:S(2)}) async-start(s8[7340032]{0:T(1024)(128)(4,1)} %bitcast.38), calls=%async_computation.2 | async-start | bytes 6291456
  166.3 53.8 %all-to-all-start.1 = ((bf16[64,8,3584]{2,1,0:T(8,128)(2,1)}), bf16[64,8,3584]{2,1,0:T(8,128)(2,1)}, u32[]{:S(2)}, u32[]{:S(2)}) async-start(bf16[64,8,3584]{2,1,0:T(8,128)(2,1)} %fusion.4), calls=%async_computation.1 | async-start | bytes 7340032 | tf_op jit(solution)/shard_map/all_to_all | solution.py:99
  172.4 4.5 %slice-start.1 = ((s8[7340032]{0:T(1024)(128)(4,1)}), s8[4194304]{0:T(1024)(128)(4,1)S(1)}, s32[]{:S(2)}) async-start(s8[7340032]{0:T(1024)(128)(4,1)} %bitcast.38), calls=%async_computation.3 | async-start | bytes 8388608
  172.4 4.5 %copy-start.7 = (bf16[512,512]{0,1:T(8,128)(2,1)S(1)}, bf16[512,512]{0,1:T(8,128)(2,1)}, u32[]{:S(2)}) copy-start(bf16[512,512]{0,1:T(8,128)(2,1)} %copy-done.6) | copy-start | bytes 1572868
  176.9 2.2 copy-start.15
  179.1 5.1 %copy-start.5 = (bf16[512,512]{0,1:T(8,128)(2,1)S(1)}, bf16[512,512]{0,1:T(8,128)(2,1)}, u32[]{:S(2)}) copy-start(bf16[512,512]{0,1:T(8,128)(2,1)} %copy-done.4) | copy-start | bytes 1572868
  179.1 11.5 %slice-start.2 = ((s8[7340032]{0:T(1024)(128)(4,1)}), s8[4194304]{0:T(1024)(128)(4,1)S(1)}, s32[]{:S(2)}) async-start(s8[7340032]{0:T(1024)(128)(4,1)} %bitcast.50), calls=%async_computation.4 | async-start | bytes 8388608
  184.2 6.4 %copy-start.3 = (bf16[512,512]{0,1:T(8,128)(2,1)S(1)}, bf16[512,512]{0,1:T(8,128)(2,1)}, u32[]{:S(2)}) copy-start(bf16[512,512]{0,1:T(8,128)(2,1)} %copy-done.2) | copy-start | bytes 1572868
  184.2 6.4 %slice-start.3 = ((s8[7340032]{0:T(1024)(128)(4,1)}), s8[3145728]{0:T(1024)(128)(4,1)S(1)}, s32[]{:S(2)}) async-start(s8[7340032]{0:T(1024)(128)(4,1)} %bitcast.50), calls=%async_computation.5 | async-start | bytes 6291456
  190.6 4.2 %copy-start.14 = (f32[512,3584]{1,0:T(8,128)S(1)}, f32[512,3584]{1,0:T(8,128)}, u32[]{:S(2)}) copy-start(f32[512,3584]{1,0:T(8,128)} %fusion.15) | copy-start | bytes 22020100
  190.6 4.5 %copy-start.17 = (f32[512,1024]{0,1:T(8,128)S(1)}, f32[512,1024]{0,1:T(8,128)}, u32[]{:S(2)}) copy-start(f32[512,1024]{0,1:T(8,128)} %copy-done.16) | copy-start | bytes 6291460

commit v10 on v7

--- a/solution.py
+++ b/solution.py
@@ -82,12 +82,14 @@
     oth_x = other[:, :model_width]
     oth_cot = other[:, model_width:]
     oth_h, oth_dg, oth_du = front_rows(oth_x, oth_cot, *weights_own)[:3]
-    split = half_slots // 2
-    dx_first = input_grads(oth_dg[:split], oth_du[:split], weights_own[0], weights_own[1])
-    back_first = lax.ppermute(dx_first, "dp", swap)
-    dx_second = input_grads(oth_dg[split:], oth_du[split:], weights_own[0], weights_own[1])
-    back_second = lax.ppermute(dx_second, "dp", swap)
-    back = jnp.concatenate([back_first, back_second], axis=0)
+    pieces = 4
+    step = half_slots // pieces
+    backs = []
+    for piece in range(pieces):
+        rows = slice(piece * step, (piece + 1) * step)
+        dx_piece = input_grads(oth_dg[rows], oth_du[rows], weights_own[0], weights_own[1])
+        backs.append(lax.ppermute(dx_piece, "dp", swap))
+    back = jnp.concatenate(backs, axis=0)
     own_dx = lax.dot_general(
         own_dg, weights_own[0], (((1,), (1,)), ((), ())), preferred_element_type=jnp.float32
     )

time: 204 us -> 208 us (1.020)
  matrix products: 62.9 us -> 69.9 us
  waiting for transfers between devices: 26 us -> 23 us
    ppermute x1, waiting for transfers between devices: 9.08 us -> 6 us  [local(): other = lax.ppermute(came, 'dp', swap)]
    dot_general x2 -> x4, matrix products: 2.3 us -> 5.26 us  [input_grads(): lax.dot_general(d_up, up_w, (((1,), (1,)), ((), ())), preferred_element_t...]
    dot_general x2 -> x4, matrix products: 2.29 us -> 5.24 us  [input_grads(): lax.dot_general(d_gate, gate_w, (((1,), (1,)), ((), ())), preferred_eleme...]
  transfers between devices with their start and end apart: 4 -> 6, of which waited for: 2 -> 2; matrix products, arithmetic and copies ran while one was open for 20% -> 22% of each run, Pallas kernels for 0% -> 0%
where the time goes in v10:
time: 208 us
  blocking collectives  97.2 us (47%)
  matrix products  69.9 us (34%)
  waiting for transfers between devices  23 us (11%)
  starting transfers between devices  10.9 us (5%)
  local copies, waits for them, and re-layouts  2.76 us (1%)
  other arithmetic  2.76 us (1%)
    all_to_all x1, blocking collectives, local(): lax.all_to_all(sent, 'expert', split_axis=0, concat_axis=0, tiled=True)  97.2 us
    all_to_all x1, waiting for transfers between devices, local(): lax.all_to_all(summed.reshape(owners, capacity, model_width), 'expert', s...  17 us
    dot_general x2, matrix products, weight_sums(): lax.dot_general(rows_x, d_up, (((0,), (0,)), ((), ())), preferred_element...  14.7 us
    dot_general x2, matrix products, weight_sums(): lax.dot_general(rows_x, d_gate, (((0,), (0,)), ((), ())), preferred_eleme...  9.33 us
    dot_general x2, matrix products, weight_sums(): lax.dot_general(hidden, rows_cot, (((0,), (0,)), ((), ())), preferred_ele...  6.46 us
    all_to_all x1, starting transfers between devices, local(): lax.all_to_all(summed.reshape(owners, capacity, model_width), 'expert', s...  6.13 us
    ppermute x1, waiting for transfers between devices, local(): other = lax.ppermute(came, 'dp', swap)  6 us
    dot_general x2, matrix products, front_rows(): lax.dot_general(rows_cot, down_w, (((1,), (1,)), ((), ())), preferred_ele...  5.45 us
  transfers between devices with their start and end apart: 6, of which 2 were waited for; matrix products, arithmetic and copies ran while one was open for 22% of the time, Pallas kernels for 0%

profile of v10, /device:TPU:1, one launch (start us, length us, event | category | flops | bytes accessed | tf_op | source)
XLA Modules:
  0.0 207.6 jit_solution(2521179930317858588)
XLA Ops:
  0.6 0.0 copy-start.3
  0.6 1.0 fusion.58
  1.7 0.7 multiply_add_fusion
  2.4 1.9 multiply_convert_fusion
  4.3 2.5 %fusion = bf16[64,8,7168]{2,1,0:T(8,128)(2,1)S(1)} fusion(bf16[256,3584]{1,0:T(8,128)(2,1)S(1)} %multiply_convert_fusion, bf16[256,3584]{1,0:T(8,128)(2,1)S(1)} %copy-done.3, s32[256]{0:T(256)S(1)} %multiply_add_fusion), kind=kOutput, calls=%fused_computation.1 | convolution fusion | flops 1890189312 | bytes 11011072 | tf_op jit(solution)/shard_map/dot_general | solution.py:68
  6.8 0.0 copy-start.12
  6.9 0.0 copy-start
  6.9 97.2 %all_to_all.10 = bf16[64,8,7168]{2,1,0:T(8,128)(2,1)S(1)} all-to-all(bf16[64,8,7168]{2,1,0:T(8,128)(2,1)S(1)} %fusion), channel_id=1, replica_groups=mesh['dp'=2,'expert'=64] {'expert'}, dimensions={0} | all-to-all | bytes 14680064 | tf_op jit(solution)/shard_map/all_to_all | solution.py:72
  104.1 3.3 %collective-permute-start = (bf16[64,8,7168]{2,1,0:T(8,128)(2,1)S(1)}, bf16[64,8,7168]{2,1,0:T(8,128)(2,1)S(1)}, u32[]{:S(2)}, u32[]{:S(2)}) collective-permute-start(bf16[64,8,7168]{2,1,0:T(8,128)(2,1)S(1)} %all_to_all.10), channel_id=1, source_target_pairs={{0,64},{64,0},{1,65},{65,1},{2,66},{66,2},{3,67},{67,3},{4,68},{68... | collective-permute-start | bytes 22020104 | tf_op jit(solution)/shard_map/ppermute | solution.py:74
  107.3 0.1 fusion.61
  107.5 0.0 copy-start.14
  107.5 2.1 fusion.37
  109.6 0.0 copy-start.4
  109.6 3.1 %fusion.41 = f32[512,512]{1,0:T(8,128)} fusion(bf16[1,512,3584]{2,1,0:T(8,128)(2,1)S(1)} %copy-done.14, bf16[512,7168]{1,0:T(8,128)(2,1)S(1)} %bitcast.68), kind=kOutput, calls=%fused_computation.49 | convolution fusion | flops 1879048192 | bytes 8388608 | tf_op jit(solution)/shard_map/dot_general | solution.py:13
  112.6 6.0 %collective-permute-done = bf16[64,8,7168]{2,1,0:T(8,128)(2,1)S(1)} collective-permute-done((bf16[64,8,7168]{2,1,0:T(8,128)(2,1)S(1)}, bf16[64,8,7168]{2,1,0:T(8,128)(2,1)S(1)}, u32[]{:S(2)}, u32[]{:S(2)}) %collective-permute-start) | collective-permute-done | bytes 7340064 | tf_op jit(solution)/shard_map/ppermute | solution.py:74
  118.6 2.1 fusion.33
  120.7 2.6 %copy-done.1 = bf16[1,3584,512]{2,1,0:T(8,128)(2,1)S(1)} copy-done((bf16[1,3584,512]{2,1,0:T(8,128)(2,1)S(1)}, bf16[1,3584,512]{2,1,0:T(8,128)(2,1)}, u32[]{:S(2)}) %copy-start.1) | copy-done | bytes 3670040
  123.3 2.1 %fusion.21 = f32[512,512]{1,0:T(8,128)S(1)} fusion(bf16[1,3584,512]{2,1,0:T(8,128)(2,1)S(1)} %copy-done.1, bf16[512,7168]{1,0:T(8,128)(2,1)S(1)} %bitcast.81), kind=kOutput, calls=%fused_computation.31 | convolution fusion | flops 1879048192 | bytes 8388608 | tf_op jit(solution)/shard_map/dot_general | solution.py:8
  125.4 0.0 copy-done.13
  125.4 0.0 copy-done.17
  125.4 0.0 copy-start.19
  125.4 2.4 %multiply_convert_fusion.3 = (bf16[512,512]{1,0:T(8,128)(2,1)S(1)}, bf16[512,512]{1,0:T(8,128)(2,1)S(1)}) fusion(f32[512,512]{1,0:T(8,128)S(1)} %fusion.21, f32[512,512]{1,0:T(8,128)S(1)} %fusion.33, bf16[1,512,3584]{2,1,0:T(8,128)(2,1)S(1)} %copy-done.14, bf16[512,7168]{1,0:T(8,128)(2,1)S(1)} %bitcast.82), kind=kOutput, calls=%fused_computation.71 | convolution fusion | flops 1882456064 | bytes 10485760 | tf_op jit(solution)/shard_map/dot_general | solution.py:13
  127.8 0.0 copy-start.7
  127.9 1.3 fusion.19
  129.2 1.3 fusion.17
  130.5 1.3 fusion.15
  131.8 1.3 fusion.13
  133.1 1.3 fusion.4
  134.5 0.5 collective-permute-start.1
  134.9 1.3 fusion.5
  136.2 0.4 collective-permute-start.2
  136.7 1.3 fusion.6
  138.0 0.0 copy-start.21
  138.0 0.5 collective-permute-start.3
  138.5 1.3 fusion.7
  139.8 0.2 collective-permute-start.4
  140.0 0.0 copy-done.4
  140.0 3.4 %multiply_convert_fusion.6 = (bf16[512,512]{1,0:T(8,128)(2,1)S(1)}, bf16[512,512]{1,0:T(8,128)(2,1)S(1)}, f32[512,512]{1,0:T(8,128)}) fusion(f32[512,512]{1,0:T(8,128)S(1)} %copy-done.21, f32[512,512]{1,0:T(8,128)S(1)} %fusion.37, bf16[1,3584,512]{2,1,0:T(8,128)(2,1)S(1)} %copy-done.1, bf16[512,7168]{1,0:T(8,128)(2,1)S(1)} %bitcast.69), kind=kOutput, calls=%fused_computation.76 | convolution fusion | flops 1882456064 | bytes 11534336 | tf_op jit(solution)/shard_map/dot_general | solution.py:8
  143.4 2.1 %fusion.35 = f32[512,3584]{1,0:T(8,128)S(1)} fusion(bf16[512,512]{1,0:T(8,128)(2,1)S(1)} %get-tuple-element.5, bf16[1,3584,512]{2,1,0:T(8,128)(2,1)S(1)} %copy-done), kind=kOutput, calls=%fused_computation.43 | convolution fusion | flops 1879048192 | bytes 11534336 | tf_op jit(solution)/shard_map/dot_general | solution.py:96
  145.5 0.0 collective-permute-done.1
  145.5 0.0 collective-permute-done.2
  145.5 0.0 collective-permute-done.3
  145.5 0.0 collective-permute-done.4
  145.5 3.9 %fusion.8 = bf16[64,8,3584]{2,1,0:T(8,128)(2,1)} fusion(f32[512,3584]{1,0:T(8,128)S(1)} %fusion.35, bf16[128,3584]{1,0:T(8,128)(2,1)S(1)} %collective-permute-done.4, bf16[128,3584]{1,0:T(8,128)(2,1)S(1)} %collective-permute-done.3, bf16[128,3584]{1,0:T(8,128)(2,1)S(1)} %collective-permute-done.2, bf16[128,3584]{1,0:T(8,128)(2,1)S(1)} %collective-permute-done.1, ...), kind=kOutput, calls=%fused_computation.18 | convolution fusion | flops 1899233280 | bytes 18874368 | tf_op jit(solution)/shard_map/dot_general | solution.py:93
  149.5 6.1 %all-to-all-start.1 = ((bf16[64,8,3584]{2,1,0:T(8,128)(2,1)}), bf16[64,8,3584]{2,1,0:T(8,128)(2,1)}, u32[]{:S(2)}, u32[]{:S(2)}) async-start(bf16[64,8,3584]{2,1,0:T(8,128)(2,1)} %fusion.8), calls=%async_computation.1 | async-start | bytes 7340032 | tf_op jit(solution)/shard_map/all_to_all | solution.py:100
  155.6 0.0 slice-start.1
  155.6 0.0 copy-start.16
  155.6 0.0 slice-start.2
  155.6 7.3 %fusion.52 = f32[3584,512]{1,0:T(8,128)} fusion(bf16[512,512]{1,0:T(8,128)(2,1)} %copy-done.11, bf16[512,7168]{1,0:T(8,128)(2,1)} %bitcast.70), kind=kOutput, calls=%fused_computation.61 | convolution fusion | flops 1879048192 | bytes 11534336 | tf_op jit(solution)/shard_map/dot_general | solution.py:37
  163.0 0.0 slice-done
  163.0 0.0 copy-done.16
  163.0 0.0 copy-start.5
  163.0 0.0 copy-start.6
  163.0 0.0 slice-start.3
  163.0 5.2 %fusion.54 = f32[3584,512]{1,0:T(8,128)} fusion(bf16[512,512]{1,0:T(8,128)(2,1)S(1)} %copy-done.16, bf16[512,7168]{1,0:T(8,128)(2,1)S(1)} %bitcast.73), kind=kOutput, calls=%fused_computation.63 | convolution fusion | flops 1879048192 | bytes 11534336 | tf_op jit(solution)/shard_map/dot_general | solution.py:34
  168.2 2.2 %fusion.45 = f32[512,3584]{1,0:T(8,128)S(1)} fusion(bf16[512,7168]{1,0:T(8,128)(2,1)S(1)} %bitcast.74, f32[512,512]{1,0:T(8,128)S(1)} %copy-done.5, f32[512,512]{1,0:T(8,128)S(1)} %copy-done.6), kind=kOutput, calls=%fused_computation.54 | convolution fusion | flops 1880621056 | bytes 13107200 | tf_op jit(solution)/shard_map/dot_general | solution.py:40
  170.4 0.0 copy-start.8
  170.4 0.0 slice-start.5
  170.5 7.3 %fusion.2 = bf16[1,3584,512]{2,1,0:T(8,128)(2,1)} fusion(f32[3584,512]{1,0:T(8,128)} %fusion.52, bf16[512,512]{1,0:T(8,128)(2,1)S(1)} %copy-done.10, bf16[512,7168]{1,0:T(8,128)(2,1)S(1)} %bitcast.85), kind=kOutput, calls=%fused_computation.7 | convolution fusion | flops 1882718208 | bytes 15204352 | tf_op jit(solution)/shard_map/dot_general | solution.py:37
  177.8 0.0 slice-done.5
  177.8 4.2 %fusion.1 = bf16[1,3584,512]{2,1,0:T(8,128)(2,1)} fusion(f32[3584,512]{1,0:T(8,128)S(1)} %bitcast.89, bf16[512,512]{1,0:T(8,128)(2,1)S(1)} %copy-done.8, bf16[512,7168]{1,0:T(8,128)(2,1)S(1)} %bitcast.86), kind=kOutput, calls=%fused_computation.6 | convolution fusion | flops 1882718208 | bytes 15204352 | tf_op jit(solution)/shard_map/dot_general | solution.py:34
  182.0 4.3 %fusion.3 = bf16[1,512,3584]{2,1,0:T(8,128)(2,1)} fusion(f32[512,3584]{1,0:T(8,128)S(1)} %fusion.45, bf16[512,7168]{1,0:T(8,128)(2,1)S(1)} %bitcast.87, f32[512,512]{1,0:T(8,128)S(1)} %copy-done.18, f32[512,512]{1,0:T(8,128)S(1)} %copy-done.20), kind=kOutput, calls=%fused_computation.8 | convolution fusion | flops 1884291072 | bytes 16777216 | tf_op jit(solution)/shard_map/dot_general | solution.py:40
  186.3 17.0 %all-to-all-done.1 = bf16[64,8,3584]{2,1,0:T(8,128)(2,1)} async-done(((bf16[64,8,3584]{2,1,0:T(8,128)(2,1)}), bf16[64,8,3584]{2,1,0:T(8,128)(2,1)}, u32[]{:S(2)}, u32[]{:S(2)}) %all-to-all-start.1) | async-done | bytes 3670048 | tf_op jit(solution)/shard_map/all_to_all | solution.py:100
  203.2 4.4 %convolution_convert_fusion.1 = bf16[256,3584]{1,0:T(8,128)(2,1)} fusion(bf16[256,512]{1,0:T(8,128)(2,1)S(1)} %fusion.61, bf16[64,8,3584]{2,1,0:T(8,128)(2,1)} %all-to-all-done.1), kind=kOutput, calls=%fused_computation.9 | convolution fusion | flops 940441600 | bytes 5767168 | tf_op jit(solution)/shard_map/dot_general | solution.py:111
  (38 shorter events, 0.1 us)
Async XLA Ops:
  0.6 3.7 %copy-start.3 = (bf16[256,3584]{1,0:T(8,128)(2,1)S(1)}, bf16[256,3584]{1,0:T(8,128)(2,1)}, u32[]{:S(2)}) copy-start(bf16[256,3584]{1,0:T(8,128)(2,1)} %param.7) | copy-start | bytes 5505028
  6.8 100.5 %copy-start.12 = (s32[256,1]{0,1:T(1,128)S(1)}, s32[256,1]{0,1:T(1,128)}, u32[]{:S(2)}) copy-start(s32[256,1]{0,1:T(1,128)} %param.9) | copy-start | bytes 3076
  6.9 100.6 %copy-start = (bf16[1,3584,512]{2,1,0:T(8,128)(2,1)S(1)}, bf16[1,3584,512]{2,1,0:T(8,128)(2,1)}, u32[]{:S(2)}) copy-start(bf16[1,3584,512]{2,1,0:T(8,128)(2,1)} %param.12) | copy-start | bytes 11010052
  104.1 35.9 %copy-start.2 = (bf16[64,8,7168]{2,1,0:T(8,128)(2,1)}, bf16[64,8,7168]{2,1,0:T(8,128)(2,1)S(1)}, u32[]{:S(2)}) copy-start(bf16[64,8,7168]{2,1,0:T(8,128)(2,1)S(1)} %all_to_all.10) | copy-start | bytes 22020100
  104.1 14.5 %collective-permute-start = (bf16[64,8,7168]{2,1,0:T(8,128)(2,1)S(1)}, bf16[64,8,7168]{2,1,0:T(8,128)(2,1)S(1)}, u32[]{:S(2)}, u32[]{:S(2)}) collective-permute-start(bf16[64,8,7168]{2,1,0:T(8,128)(2,1)S(1)} %all_to_all.10), channel_id=1, source_target_pairs={{0,64},{64,0},{1,65},{65,1},{2,66},{66,2},{3,67},{67,3},{4,68},{68... | collective-permute-start | bytes 22020104 | tf_op jit(solution)/shard_map/ppermute | solution.py:74
  107.5 2.1 copy-start.14
  109.6 30.5 %copy-start.4 = (f32[512,512]{1,0:T(8,128)}, f32[512,512]{1,0:T(8,128)S(1)}, u32[]{:S(2)}) copy-start(f32[512,512]{1,0:T(8,128)S(1)} %fusion.37) | copy-start | bytes 3145732
  118.6 6.8 %copy-start.13 = (bf16[64,8,7168]{2,1,0:T(8,128)(2,1)}, bf16[64,8,7168]{2,1,0:T(8,128)(2,1)S(1)}, u32[]{:S(2)}) copy-start(bf16[64,8,7168]{2,1,0:T(8,128)(2,1)S(1)} %collective-permute-done) | copy-start | bytes 22020100
  118.6 4.7 %copy-start.1 = (bf16[1,3584,512]{2,1,0:T(8,128)(2,1)S(1)}, bf16[1,3584,512]{2,1,0:T(8,128)(2,1)}, u32[]{:S(2)}) copy-start(bf16[1,3584,512]{2,1,0:T(8,128)(2,1)} %param.11) | copy-start | bytes 11010052
  123.3 2.1 %copy-start.17 = (f32[512,512]{1,0:T(8,128)}, f32[512,512]{1,0:T(8,128)S(1)}, u32[]{:S(2)}) copy-start(f32[512,512]{1,0:T(8,128)S(1)} %fusion.33) | copy-start | bytes 3145732
  125.4 2.4 %copy-start.19 = (f32[512,512]{1,0:T(8,128)}, f32[512,512]{1,0:T(8,128)S(1)}, u32[]{:S(2)}) copy-start(f32[512,512]{1,0:T(8,128)S(1)} %fusion.21) | copy-start | bytes 3145732
  127.8 4.0 %copy-start.7 = (bf16[512,512]{1,0:T(8,128)(2,1)}, bf16[512,512]{1,0:T(8,128)(2,1)S(1)}, u32[]{:S(2)}) copy-start(bf16[512,512]{1,0:T(8,128)(2,1)S(1)} %get-tuple-element.7) | copy-start | bytes 1572868
  127.9 10.6 %copy-start.9 = (bf16[512,512]{1,0:T(8,128)(2,1)}, bf16[512,512]{1,0:T(8,128)(2,1)S(1)}, u32[]{:S(2)}) copy-start(bf16[512,512]{1,0:T(8,128)(2,1)S(1)} %get-tuple-element.6) | copy-start | bytes 1572868
  134.5 11.0 %collective-permute-start.1 = (bf16[128,3584]{1,0:T(8,128)(2,1)S(1)}, bf16[128,3584]{1,0:T(8,128)(2,1)S(1)}, u32[]{:S(2)}, u32[]{:S(2)}) collective-permute-start(bf16[128,3584]{1,0:T(8,128)(2,1)S(1)} %fusion.4), channel_id=1, source_target_pairs={{0,64},{64,0},{1,65},{65,1},{2,66},{66,2},{3,67},{67,3},{4,68},{68... | collective-permute-start | bytes 2752520 | tf_op jit(solution)/shard_map/ppermute | solution.py:91
  136.2 9.3 %collective-permute-start.2 = (bf16[128,3584]{1,0:T(8,128)(2,1)S(1)}, bf16[128,3584]{1,0:T(8,128)(2,1)S(1)}, u32[]{:S(2)}, u32[]{:S(2)}) collective-permute-start(bf16[128,3584]{1,0:T(8,128)(2,1)S(1)} %fusion.5), channel_id=1, source_target_pairs={{0,64},{64,0},{1,65},{65,1},{2,66},{66,2},{3,67},{67,3},{4,68},{68... | collective-permute-start | bytes 2752520 | tf_op jit(solution)/shard_map/ppermute | solution.py:91
  138.0 2.0 copy-start.21
  138.0 7.5 %collective-permute-start.3 = (bf16[128,3584]{1,0:T(8,128)(2,1)S(1)}, bf16[128,3584]{1,0:T(8,128)(2,1)S(1)}, u32[]{:S(2)}, u32[]{:S(2)}) collective-permute-start(bf16[128,3584]{1,0:T(8,128)(2,1)S(1)} %fusion.6), channel_id=1, source_target_pairs={{0,64},{64,0},{1,65},{65,1},{2,66},{66,2},{3,67},{67,3},{4,68},{68... | collective-permute-start | bytes 2752520 | tf_op jit(solution)/shard_map/ppermute | solution.py:91
  139.8 5.7 %collective-permute-start.4 = (bf16[128,3584]{1,0:T(8,128)(2,1)S(1)}, bf16[128,3584]{1,0:T(8,128)(2,1)S(1)}, u32[]{:S(2)}, u32[]{:S(2)}) collective-permute-start(bf16[128,3584]{1,0:T(8,128)(2,1)S(1)} %fusion.7), channel_id=1, source_target_pairs={{0,64},{64,0},{1,65},{65,1},{2,66},{66,2},{3,67},{67,3},{4,68},{68... | collective-permute-start | bytes 2752520 | tf_op jit(solution)/shard_map/ppermute | solution.py:91
  143.4 2.2 %copy-start.11 = (bf16[512,512]{1,0:T(8,128)(2,1)}, bf16[512,512]{1,0:T(8,128)(2,1)S(1)}, u32[]{:S(2)}) copy-start(bf16[512,512]{1,0:T(8,128)(2,1)S(1)} %get-tuple-element.5) | copy-start | bytes 1572868
  143.4 2.2 %copy-start.15 = (bf16[512,512]{1,0:T(8,128)(2,1)}, bf16[512,512]{1,0:T(8,128)(2,1)S(1)}, u32[]{:S(2)}) copy-start(bf16[512,512]{1,0:T(8,128)(2,1)S(1)} %get-tuple-element.4) | copy-start | bytes 1572868
  149.5 13.5 %slice-start = ((s8[7340032]{0:T(1024)(128)(4,1)}), s8[3145728]{0:T(1024)(128)(4,1)S(1)}, s32[]{:S(2)}) async-start(s8[7340032]{0:T(1024)(128)(4,1)} %bitcast.71), calls=%async_computation.2 | async-start | bytes 6291456
  149.5 53.8 %all-to-all-start.1 = ((bf16[64,8,3584]{2,1,0:T(8,128)(2,1)}), bf16[64,8,3584]{2,1,0:T(8,128)(2,1)}, u32[]{:S(2)}, u32[]{:S(2)}) async-start(bf16[64,8,3584]{2,1,0:T(8,128)(2,1)} %fusion.8), calls=%async_computation.1 | async-start | bytes 7340032 | tf_op jit(solution)/shard_map/all_to_all | solution.py:100
  155.6 7.4 %slice-start.1 = ((s8[7340032]{0:T(1024)(128)(4,1)}), s8[4194304]{0:T(1024)(128)(4,1)S(1)}, s32[]{:S(2)}) async-start(s8[7340032]{0:T(1024)(128)(4,1)} %bitcast.71), calls=%async_computation.3 | async-start | bytes 8388608
  155.6 7.4 %copy-start.16 = (bf16[512,512]{1,0:T(8,128)(2,1)S(1)}, bf16[512,512]{1,0:T(8,128)(2,1)}, u32[]{:S(2)}) copy-start(bf16[512,512]{1,0:T(8,128)(2,1)} %copy-done.15) | copy-start | bytes 1572868
  155.6 14.8 %slice-start.2 = ((s8[7340032]{0:T(1024)(128)(4,1)}), s8[4194304]{0:T(1024)(128)(4,1)S(1)}, s32[]{:S(2)}) async-start(s8[7340032]{0:T(1024)(128)(4,1)} %bitcast.83), calls=%async_computation.4 | async-start | bytes 8388608
  163.0 5.2 %copy-start.5 = (f32[512,512]{1,0:T(8,128)S(1)}, f32[512,512]{1,0:T(8,128)}, u32[]{:S(2)}) copy-start(f32[512,512]{1,0:T(8,128)} %copy-done.4) | copy-start | bytes 3145732
  163.0 5.2 %copy-start.6 = (f32[512,512]{1,0:T(8,128)S(1)}, f32[512,512]{1,0:T(8,128)}, u32[]{:S(2)}) copy-start(f32[512,512]{1,0:T(8,128)} %get-tuple-element.8) | copy-start | bytes 3145732
  163.0 7.4 %slice-start.3 = ((s8[7340032]{0:T(1024)(128)(4,1)}), s8[3145728]{0:T(1024)(128)(4,1)S(1)}, s32[]{:S(2)}) async-start(s8[7340032]{0:T(1024)(128)(4,1)} %bitcast.83), calls=%async_computation.5 | async-start | bytes 6291456
  168.2 2.2 %copy-start.10 = (bf16[512,512]{1,0:T(8,128)(2,1)S(1)}, bf16[512,512]{1,0:T(8,128)(2,1)}, u32[]{:S(2)}) copy-start(bf16[512,512]{1,0:T(8,128)(2,1)} %copy-done.9) | copy-start | bytes 1572868
  168.2 9.6 %slice-start.4 = ((s8[7340032]{0:T(1024)(128)(4,1)}), s8[4194304]{0:T(1024)(128)(4,1)S(1)}, s32[]{:S(2)}) async-start(s8[7340032]{0:T(1024)(128)(4,1)} %bitcast.88), calls=%async_computation.6 | async-start | bytes 8388608
  170.4 7.3 %copy-start.8 = (bf16[512,512]{1,0:T(8,128)(2,1)S(1)}, bf16[512,512]{1,0:T(8,128)(2,1)}, u32[]{:S(2)}) copy-start(bf16[512,512]{1,0:T(8,128)(2,1)} %copy-done.7) | copy-start | bytes 1572868
  170.4 7.3 %slice-start.5 = ((s8[7340032]{0:T(1024)(128)(4,1)}), s8[3145728]{0:T(1024)(128)(4,1)S(1)}, s32[]{:S(2)}) async-start(s8[7340032]{0:T(1024)(128)(4,1)} %bitcast.88), calls=%async_computation.7 | async-start | bytes 6291456
  177.8 4.2 %copy-start.18 = (f32[512,512]{1,0:T(8,128)S(1)}, f32[512,512]{1,0:T(8,128)}, u32[]{:S(2)}) copy-start(f32[512,512]{1,0:T(8,128)} %copy-done.17) | copy-start | bytes 3145732
  177.8 4.2 %copy-start.20 = (f32[512,512]{1,0:T(8,128)S(1)}, f32[512,512]{1,0:T(8,128)}, u32[]{:S(2)}) copy-start(f32[512,512]{1,0:T(8,128)} %copy-done.19) | copy-start | bytes 3145732
